TPU v7x, 512 devices: a whole 4x8x8 slice. The times are simulated.
512 devices in a mesh: row: 4 (over z_hi), col: 16 (over z_lo, x, core), chan: 8 (over y).
Axes of the slice: x: 4, y: 8, z: 8 (z_hi: 4, z_lo: 2; z = z_hi * 2 + z_lo), core: 2. Of those that a mesh axis runs over, the one named last changes fastest.
Arguments:
- snapshots: bfloat16 [8192, 2048], P('col', 'chan'), may hold values from -45 to 45
- offsets: int32 [4], replicated, may hold values from 0 to 15
- window_len: int32 [8192], replicated, may hold values from 64 to 256, as said below
- cone_exp: int32 [8192], replicated, may hold values from 0 to 3
Outputs:
- kernel: float32 [2048, 8192], P(('row', 'chan'), 'col')
Inputs may be any that keep to these rules, and one draw needn't show every extreme that they name: `window_len`: each value is a lag window length; at least one snapshot has a window of 256 lags.
All inputs are finite; a program needn't handle non-finite values.
Results may differ from a plain program's by a relative error of at most 0.0003.
Values may be sent and summed in bfloat16 or wider, within the bound.
No kernel may reach another device: no remote copies, remote signals or barrier semaphores. Data moves between devices by JAX's collectives and lax.ppermute only.
A program may use at most 64 MiB of HBM per device.

v0:
```python
import jax
import jax.numpy as jnp
from jax import lax
from jax.sharding import PartitionSpec as P

C = 2048
LAGS = 256


epsilon = 1e-05


def shifted(block, axis, distance):
    devices = range(lax.axis_size(axis))
    route = [((i - distance) % len(devices), i) for i in devices]
    return lax.ppermute(block, axis, route)


def spread(value, axis, source):
    kept = jnp.where(lax.axis_index(axis) == source, value, 0).astype(value.dtype)
    return lax.psum(kept, axis)


def power_int(frac, exps):
    square = frac * frac
    return jnp.where(
        exps == 0,
        jnp.ones_like(frac),
        jnp.where(exps == 1, frac, jnp.where(exps == 2, square, square * frac)),
    )


def cone_matrix(lengths, exps, lags):
    rows = lengths.shape[0]
    row_pos = lax.broadcasted_iota(jnp.int32, (rows, rows + lags - 1), 0)
    col_pos = lax.broadcasted_iota(jnp.int32, (rows, rows + lags - 1), 1)
    lag = row_pos + (lags - 1) - col_pos
    span = lengths[:, None]
    valid = (lag >= 0) & (lag < span)
    frac = (span.astype(jnp.float32) - lag.astype(jnp.float32)) / span.astype(jnp.float32)
    cone = jnp.where(valid, power_int(frac, exps[:, None]), jnp.zeros_like(frac))
    return cone / jnp.sum(cone, axis=1, keepdims=True)


def lag_sum(weights, dist, count):
    depth = dist.shape[0]
    width = dist.shape[1]
    columns = width - (depth - count)
    padded = jnp.pad(dist, ((0, 0), (count - 1, 0)))
    stride = width + count - 1
    flat = jnp.pad(padded.reshape(-1), (0, depth))
    skewed = flat.reshape(depth, stride + 1)[:, : columns + count - 1]
    diagonal = jnp.dot(
        weights, skewed, precision=lax.Precision.HIGHEST, preferred_element_type=jnp.float32
    )
    lined = diagonal.reshape(-1)[count - 1 : count - 1 + count * (columns + count - 2)]
    return lined.reshape(count, columns + count - 2)[:, :columns]


def shards(snapshots, offsets, window_len, cone_exp):
    block = snapshots.shape[0]
    lags = LAGS
    tail = snapshots[block - (lags - 1) :]
    history = shifted(tail, "col", 1)
    col_ext = jnp.concatenate([history, snapshots], axis=0)
    chosen = lax.dynamic_index_in_dim(offsets, lax.axis_index("row"), 0, keepdims=False)
    row_ext = spread(col_ext, "col", chosen)
    row_begin = chosen * block
    col_begin = lax.axis_index("col") * block
    row_weights = cone_matrix(
        lax.dynamic_slice_in_dim(window_len, row_begin, block),
        lax.dynamic_slice_in_dim(cone_exp, row_begin, block),
        lags,
    )
    col_weights = cone_matrix(
        lax.dynamic_slice_in_dim(window_len, col_begin, block),
        lax.dynamic_slice_in_dim(cone_exp, col_begin, block),
        lags,
    )
    share = block // lax.axis_size("chan")
    first = lax.axis_index("chan") * share
    mine = lax.dynamic_slice(row_weights, (first, first), (share, share + lags - 1))
    row_wide = row_ext.astype(jnp.float32)
    col_wide = col_ext.astype(jnp.float32)
    row_part = jnp.sum(row_wide * row_wide, axis=1)
    col_part = jnp.sum(col_wide * col_wide, axis=1)
    inner = jnp.dot(row_ext, col_ext.T, preferred_element_type=jnp.float32)
    dist = row_part[:, None] + col_part[None, :] - 2.0 * inner
    total = lax.psum_scatter(
        lag_sum(row_weights, dist, lax.axis_size("chan") * share),
        "chan",
        scatter_dimension=0,
        tiled=True,
    )
    row_full, col_norms = lax.psum((row_part, col_part), "chan")
    row_near = lax.dynamic_slice_in_dim(row_full, first, share + lags - 1)
    row_scale = jnp.sqrt(
        jnp.dot(mine, row_near, precision=lax.Precision.HIGHEST, preferred_element_type=jnp.float32)
        / C
        + epsilon
    )
    col_scale = jnp.sqrt(
        jnp.dot(
            col_weights,
            col_norms,
            precision=lax.Precision.HIGHEST,
            preferred_element_type=jnp.float32,
        )
        / C
        + epsilon
    )
    return jnp.exp(-total / (2.0 * C * row_scale[:, None] * col_scale[None, :]))


def solution(mesh):
    in_specs = (P("col", "chan"), P(), P(), P())
    out_specs = P(("row", "chan"), "col")
    return jax.shard_map(shards, mesh=mesh, in_specs=in_specs, out_specs=out_specs, check_vma=False)
```

profile of v0, /device:TPU:1, one launch (start us, length us, event | category | flops | bytes accessed | tf_op | source)
XLA Modules:
  0.0 237.5 jit_solution(13446755895322598838)
XLA Ops:
  6.5 0.0 copy-start
  6.5 0.0 all-reduce.5.cloned.1.call-start
  6.5 1.0 slice.12
  7.5 4.5 %collective-permute-start = (bf16[255,256]{1,0:T(8,128)(2,1)S(1)}, bf16[255,256]{1,0:T(8,128)(2,1)S(1)}, u32[]{:S(2)}, u32[]{:S(2)}) collective-permute-start(bf16[255,256]{1,0:T(8,128)(2,1)S(1)} %slice.12), channel_id=1, source_target_pairs={{120,0},{0,8},{8,16},{16,24},{24,32},{32,40},{40,48},{48,56},{56,6... | collective-permute-start | bytes 391688 | tf_op jit(solution)/shard_map/ppermute | solution.py:16
  12.1 1.2 dynamic_slice.22
  14.0 0.8 dynamic-slice_compare_fusion.5
  15.4 0.8 fusion.31
  16.2 1.0 collective-permute-done
  17.2 1.8 broadcast_select_fusion
  19.0 0.0 all-reduce.5.cloned.1.call-update
  19.0 0.0 reduce-scatter.2.cloned.1.call-start
  19.0 2.5 %fusion.21 = (f32[512]{0:T(512)S(1)}, f32[512]{0:T(512)S(1)}) fusion(pred[512]{0:T(512)(128)(4,1)S(1)} %get-tuple-element.17, f32[512]{0:T(512)S(1)} %get-tuple-element.19, pred[512]{0:T(512)(128)(4,1)S(1)} %get-tuple-element.16, pred[512]{0:T(512)(128)(4,1)S(1)} %get-tuple-element.18, s32[512]{0:T(512)S(1)} %get-tuple-element.20, ...), kind=kLoop, calls=%fused_computation.28 | loop fusion | flops 9816576 | bytes 17408 | tf_op jit(solution)/shard_map/reduce_sum | solution.py:42
  21.6 0.0 copy-done
  21.6 0.2 multiply_reduce_fusion
  21.7 127.7 %all-reduce.5.cloned.1.call-done = bf16[767,256]{1,0:T(8,128)(2,1)} async-done(((bf16[767,256]{1,0:T(8,128)(2,1)}), bf16[767,256]{1,0:T(8,128)(2,1)}) %all-reduce.5.cloned.1.call-update) | async-done | bytes 392720 | tf_op jit(solution)/shard_map/psum | solution.py:21
  149.5 1.2 multiply_reduce_fusion.1
  150.7 1.5 multiply_subtract_fusion
  152.2 2.7 %pad.8 = f32[767,1278]{1,0:T(8,128)} pad(f32[767,767]{1,0:T(8,128)S(1)} %multiply_subtract_fusion, f32[]{:T(128)} %constant.14.clone.1), padding=0_0x511_0 | pad | bytes 6274064 | tf_op jit(solution)/shard_map/jit(_pad)/pad | solution.py:49
  154.9 5.5 %reshape.37 = f32[980226]{0:T(1024)} reshape(f32[767,1278]{1,0:T(8,128)} %pad.8) | data formatting | bytes 7841808 | tf_op jit(solution)/shard_map/reshape | solution.py:51
  160.4 4.3 %pad.9 = f32[980993]{0:T(1024)} pad(f32[980226]{0:T(1024)} %reshape.37, f32[]{:T(128)} %constant.14.clone.1), padding=0_767 | pad | bytes 7844880 | tf_op jit(solution)/shard_map/jit(_pad)/pad | solution.py:51
  164.7 7.8 %reshape.38 = f32[767,1279]{1,0:T(8,128)} reshape(f32[980993]{0:T(1024)} %pad.9) | data formatting | bytes 7847944 | tf_op jit(solution)/shard_map/reshape | solution.py:52
  172.5 9.2 %fusion = f32[512,1023]{1,0:T(8,128)} fusion(f32[767,1279]{1,0:T(8,128)} %reshape.38, f32[512]{0:T(512)S(1)} %get-tuple-element.6, pred[512]{0:T(512)(128)(4,1)S(1)} %get-tuple-element.15, f32[512]{0:T(512)S(1)} %get-tuple-element.9, pred[512]{0:T(512)(128)(4,1)S(1)} %get-tuple-element.14, pred[512]{0:T(512)(128)(4,1)S(1)} %get-tuple-element.13, ...), kind=kOutput, calls=%fused_computation | convolution fusion | flops 4826332160 | bytes 5250560 | tf_op jit(solution)/shard_map/dot_general | solution.py:53
  181.7 2.9 %reshape.39 = f32[523776]{0:T(1024)S(1)} reshape(f32[512,1023]{1,0:T(8,128)} %fusion) | data formatting | bytes 4190208 | tf_op jit(solution)/shard_map/reshape | solution.py:56
  184.6 2.0 slice.17
  186.6 3.4 %reshape.40 = f32[512,1022]{1,0:T(8,128)S(1)} reshape(f32[523264]{0:T(1024)} %slice.17) | data formatting | bytes 4186112 | tf_op jit(solution)/shard_map/reshape | solution.py:57
  190.0 1.1 slice.18
  191.0 0.0 reduce-scatter.2.cloned.1.call-update
  191.1 0.9 broadcast_divide_fusion
  192.0 13.5 %all-reduce.2 = (f32[767]{0:T(1024)S(1)}, f32[767]{0:T(1024)S(1)}) all-reduce(f32[767]{0:T(1024)S(1)} %multiply_reduce_fusion, f32[767]{0:T(1024)S(1)} %multiply_reduce_fusion.1), channel_id=1, replica_groups=mesh['row'=4,'col'=16,'chan'=8] {'chan'}, use_global_device_ids=true, to_apply=%region_7.8 | all-reduce | flops 1534 | bytes 12272 | tf_op jit(solution)/shard_map/psum | solution.py:95
  205.5 0.1 dynamic_slice.26
  205.6 0.3 fusion.18
  205.8 2.5 %fusion.13 = f32[1,512]{1,0:T(1,128)S(1)} fusion(f32[767,1]{0,1:T(1,128)S(1)} %reshape.43, f32[512]{0:T(512)S(1)} %get-tuple-element.5, f32[512]{0:T(512)S(1)} %get-tuple-element.19, s32[512]{0:T(512)S(1)} %get-tuple-element.20, s32[512]{0:T(512)S(1)} %get-tuple-element.21, pred[512]{0:T(512)(128)(4,1)S(1)} %get-tuple-element.17, ...), kind=kOutput, calls=%fused_computation.17 | convolution fusion | flops 10210304 | bytes 14844 | tf_op jit(solution)/shard_map/dot_general | solution.py:103
  208.3 20.6 %reduce-scatter.2.cloned.1.call-done = f32[64,512]{1,0:T(8,128)} async-done(((f32[512,512]{1,0:T(8,128)}), f32[64,512]{1,0:T(8,128)}) %reduce-scatter.2.cloned.1.call-update) | async-done | bytes 131088 | tf_op jit(solution)/shard_map/reduce_scatter | solution.py:89
  229.0 1.7 divide_exponential_fusion
  (3 shorter events, 0.0 us)
Async XLA Ops:
  6.5 15.0 %copy-start = (bf16[512,256]{1,0:T(8,128)(2,1)S(1)}, bf16[512,256]{1,0:T(8,128)(2,1)}, u32[]{:S(2)}) copy-start(bf16[512,256]{1,0:T(8,128)(2,1)} %param.4) | copy-start | bytes 786436
  6.5 143.0 %all-reduce.5.cloned.1.call-start = ((), (), s32[]{:S(2)}) async-start(), calls=%async_computation.1 | async-start | bytes 786432 | tf_op jit(solution)/shard_map/psum | solution.py:21
  7.5 9.6 %collective-permute-start = (bf16[255,256]{1,0:T(8,128)(2,1)S(1)}, bf16[255,256]{1,0:T(8,128)(2,1)S(1)}, u32[]{:S(2)}, u32[]{:S(2)}) collective-permute-start(bf16[255,256]{1,0:T(8,128)(2,1)S(1)} %slice.12), channel_id=1, source_target_pairs={{120,0},{0,8},{8,16},{16,24},{24,32},{32,40},{40,48},{48,56},{56,6... | collective-permute-start | bytes 391688 | tf_op jit(solution)/shard_map/ppermute | solution.py:16
  19.0 210.0 %reduce-scatter.2.cloned.1.call-start = ((), (), s32[]{:S(2)}) async-start(), calls=%async_computation.2 | async-start | bytes 1179648 | tf_op jit(solution)/shard_map/reduce_scatter | solution.py:89
Sparse Core Ops, SparseCore 0:
  19.1 130.3 all-reduce.4
  191.2 37.7 reduce-scatter.1
where the time goes:
time: 241 us; the launch traced here: 237 us
  waiting for transfers between devices  149 us (62%)
  local copies, waits for them, and re-layouts  32 us (13%)
  between operations  14.8 us (6%)
  matrix products  13.5 us (6%)
  blocking collectives  13.5 us (6%)
  other arithmetic  9.83 us (4%)
  starting transfers between devices  4.55 us (2%)
    psum x1, waiting for transfers between devices, spread(): return lax.psum(kept, axis)  128 us
    reduce_scatter x1, waiting for transfers between devices, shards(): lax.psum_scatter(lag_sum(row_weights, dist, lax.axis_size('chan') * share...  20.6 us
    psum x1, blocking collectives, shards(): row_full, col_norms = lax.psum((row_part, col_part), 'chan')  13.5 us
    dot_general x1, matrix products, lag_sum(): jnp.dot(weights, skewed, precision=lax.Precision.HIGHEST, preferred_eleme...  9.22 us
    reshape x1, local copies, waits for them, and re-layouts, lag_sum(): skewed = flat.reshape(depth, stride + 1)[:, :columns + count - 1]  7.81 us
    reshape x1, local copies, waits for them, and re-layouts, lag_sum(): flat = jnp.pad(padded.reshape(-1), (0, depth))  5.49 us
  transfers between devices with their start and end apart: 3, of which 3 were waited for; matrix products, arithmetic and copies ran while one was open for 4% of the time, Pallas kernels for 0%

commit v1 on v0

--- a/solution.py
+++ b/solution.py
@@ -19,6 +19,42 @@
 def spread(value, axis, source):
     kept = jnp.where(lax.axis_index(axis) == source, value, 0).astype(value.dtype)
     return lax.psum(kept, axis)
+
+
+COL_PARTS = (2, 4, 2)
+
+
+def col_route(step):
+    outer, mid, inner = COL_PARTS
+    route = []
+    for c in range(outer * mid * inner):
+        z, x, k = c // (mid * inner), (c // inner) % mid, c % inner
+        z, x, k = step(z, x, k)
+        route.append((c, (z % outer * mid + x % mid) * inner + k % inner))
+    return route
+
+
+def broadcast_col(value, source):
+    outer, mid, inner = COL_PARTS
+    if lax.axis_size("col") != outer * mid * inner or mid != 4 or outer != 2 or inner != 2:
+        return spread(value, "col", source)
+    me = lax.axis_index("col")
+    dz = (me // (mid * inner) - source // (mid * inner)) % outer
+    dx = ((me // inner) % mid - (source // inner) % mid) % mid
+    dk = (me % inner - source % inner) % inner
+    got = lax.ppermute(value, "col", col_route(lambda z, x, k: (z, x, k + 1)))
+    value = jnp.where(dk == 1, got, value)
+    plus = col_route(lambda z, x, k: (z, x + 1, k))
+    minus = col_route(lambda z, x, k: (z, x - 1, k))
+    from_left = lax.ppermute(value, "col", plus)
+    from_right = lax.ppermute(value, "col", minus)
+    value = jnp.where(dx == 1, from_left, jnp.where(dx == 3, from_right, value))
+    half = value.shape[0] // 2
+    first = lax.ppermute(value[:half], "col", plus)
+    second = lax.ppermute(value[half:], "col", minus)
+    value = jnp.where(dx == 2, jnp.concatenate([first, second], axis=0), value)
+    got = lax.ppermute(value, "col", col_route(lambda z, x, k: (z + 1, x, k)))
+    return jnp.where(dz == 1, got, value)
 
 
 def power_int(frac, exps):
@@ -64,7 +100,7 @@
     history = shifted(tail, "col", 1)
     col_ext = jnp.concatenate([history, snapshots], axis=0)
     chosen = lax.dynamic_index_in_dim(offsets, lax.axis_index("row"), 0, keepdims=False)
-    row_ext = spread(col_ext, "col", chosen)
+    row_ext = broadcast_col(col_ext, chosen)
     row_begin = chosen * block
     col_begin = lax.axis_index("col") * block
     row_weights = cone_matrix(
@@ -92,7 +128,8 @@
         scatter_dimension=0,
         tiled=True,
     )
-    row_full, col_norms = lax.psum((row_part, col_part), "chan")
+    gathered = lax.all_gather(jnp.stack([row_part, col_part]), "chan")
+    row_full, col_norms = jnp.sum(gathered, axis=0)
     row_near = lax.dynamic_slice_in_dim(row_full, first, share + lags - 1)
     row_scale = jnp.sqrt(
         jnp.dot(mine, row_near, precision=lax.Precision.HIGHEST, preferred_element_type=jnp.float32)

time: 241 us -> 157 us (0.65)
  the two profiles are of different devices: /device:TPU:1 before, /device:TPU:2 now
where the time goes in v1:
time: 157 us; the launch traced here: 156 us
  waiting for transfers between devices  36.3 us (23%)
  local copies, waits for them, and re-layouts  31.9 us (20%)
  blocking collectives  24.7 us (16%)
  starting transfers between devices  24.5 us (16%)
  between operations  17 us (11%)
  matrix products  12.5 us (8%)
  other arithmetic  9.48 us (6%)
    all_gather x1, blocking collectives, shards(): gathered = lax.all_gather(jnp.stack([row_part, col_part]), 'chan')  24.7 us
    reduce_scatter x1, waiting for transfers between devices, shards(): lax.psum_scatter(lag_sum(row_weights, dist, lax.axis_size('chan') * share...  12.2 us
    dot_general x1, matrix products, lag_sum(): jnp.dot(weights, skewed, precision=lax.Precision.HIGHEST, preferred_eleme...  9.22 us
    ppermute x1, starting transfers between devices, broadcast_col(): from_right = lax.ppermute(value, 'col', minus)  8.45 us
    reshape x1, local copies, waits for them, and re-layouts, lag_sum(): skewed = flat.reshape(depth, stride + 1)[:, :columns + count - 1]  7.81 us
    ppermute x1, waiting for transfers between devices, broadcast_col(): got = lax.ppermute(value, 'col', col_route(lambda z, x, k: (z + 1, x, k)))  6.75 us
    ppermute x1, waiting for transfers between devices, broadcast_col(): from_left = lax.ppermute(value, 'col', plus)  6.4 us
    reshape x1, local copies, waits for them, and re-layouts, lag_sum(): flat = jnp.pad(padded.reshape(-1), (0, depth))  5.49 us
  transfers between devices with their start and end apart: 8, of which 7 were waited for; matrix products, arithmetic and copies ran while one was open for 6% of the time, Pallas kernels for 0%

profile of v1, /device:TPU:2, one launch (start us, length us, event | category | flops | bytes accessed | tf_op | source)
XLA Modules:
  0.0 156.4 jit_solution(18078675547755812848)
XLA Ops:
  6.5 0.0 reduce-scatter.2.cloned.1.call-start
  6.5 0.9 slice.18
  7.5 1.9 %collective-permute-start = (bf16[255,256]{1,0:T(8,128)(2,1)S(1)}, bf16[255,256]{1,0:T(8,128)(2,1)S(1)}, u32[]{:S(2)}, u32[]{:S(2)}) collective-permute-start(bf16[255,256]{1,0:T(8,128)(2,1)S(1)} %slice.18), channel_id=1, source_target_pairs={{120,0},{0,8},{8,16},{16,24},{24,32},{32,40},{40,48},{48,56},{56,6... | collective-permute-start | bytes 391688 | tf_op jit(solution)/shard_map/ppermute | solution.py:16
  9.4 4.4 %collective-permute-done = bf16[255,256]{1,0:T(8,128)(2,1)S(1)} collective-permute-done((bf16[255,256]{1,0:T(8,128)(2,1)S(1)}, bf16[255,256]{1,0:T(8,128)(2,1)S(1)}, u32[]{:S(2)}, u32[]{:S(2)}) %collective-permute-start) | collective-permute-done | bytes 130592 | tf_op jit(solution)/shard_map/ppermute | solution.py:16
  13.8 1.0 pad_maximum_fusion
  14.8 1.9 %collective-permute-start.1 = (bf16[767,256]{1,0:T(8,128)(2,1)S(1)}, bf16[767,256]{1,0:T(8,128)(2,1)S(1)}, u32[]{:S(2)}, u32[]{:S(2)}) collective-permute-start(bf16[767,256]{1,0:T(8,128)(2,1)S(1)} %pad_maximum_fusion), channel_id=1, source_target_pairs={{0,8},{8,0},{16,24},{24,16},{32,40},{40,32},{48,56},{56,48},{64,72... | collective-permute-start | bytes 1178120 | tf_op jit(solution)/shard_map/ppermute | solution.py:45
  16.7 1.2 dynamic_slice.24
  19.9 0.0 collective-permute-done.1
  20.0 1.1 broadcast_select_fusion
  21.0 3.4 %collective-permute-start.2 = (bf16[767,256]{1,0:T(8,128)(2,1)S(1)}, bf16[767,256]{1,0:T(8,128)(2,1)S(1)}, u32[]{:S(2)}, u32[]{:S(2)}) collective-permute-start(bf16[767,256]{1,0:T(8,128)(2,1)S(1)} %broadcast_select_fusion), channel_id=1, source_target_pairs={{0,16},{8,24},{16,32},{24,40},{32,48},{40,56},{48,0},{56,8},{64,80... | collective-permute-start | bytes 1178120 | tf_op jit(solution)/shard_map/ppermute | solution.py:49
  24.4 8.4 %collective-permute-start.3 = (bf16[767,256]{1,0:T(8,128)(2,1)S(1)}, bf16[767,256]{1,0:T(8,128)(2,1)S(1)}, u32[]{:S(2)}, u32[]{:S(2)}) collective-permute-start(bf16[767,256]{1,0:T(8,128)(2,1)S(1)} %broadcast_select_fusion), channel_id=1, source_target_pairs={{0,48},{8,56},{16,0},{24,8},{32,16},{40,24},{48,32},{56,40},{64,11... | collective-permute-start | bytes 1178120 | tf_op jit(solution)/shard_map/ppermute | solution.py:50
  34.3 0.0 copy-start
  34.3 6.4 %collective-permute-done.2 = bf16[767,256]{1,0:T(8,128)(2,1)S(1)} collective-permute-done((bf16[767,256]{1,0:T(8,128)(2,1)S(1)}, bf16[767,256]{1,0:T(8,128)(2,1)S(1)}, u32[]{:S(2)}, u32[]{:S(2)}) %collective-permute-start.2) | collective-permute-done | bytes 392736 | tf_op jit(solution)/shard_map/ppermute | solution.py:49
  40.7 1.2 collective-permute-done.3
  41.9 0.1 select_select_fusion
  42.1 5.0 %collective-permute-start.4 = (bf16[383,256]{1,0:T(8,128)(2,1)S(1)}, bf16[383,256]{1,0:T(8,128)(2,1)S(1)}, u32[]{:S(2)}, u32[]{:S(2)}) collective-permute-start(bf16[383,256]{1,0:T(8,128)(2,1)S(1)} %slice.24), channel_id=1, source_target_pairs={{0,16},{8,24},{16,32},{24,40},{32,48},{40,56},{48,0},{56,8},{64,80... | collective-permute-start | bytes 588296 | tf_op jit(solution)/shard_map/ppermute | solution.py:53
  47.1 1.9 %collective-permute-start.5 = (bf16[384,256]{1,0:T(8,128)(2,1)S(1)}, bf16[384,256]{1,0:T(8,128)(2,1)S(1)}, u32[]{:S(2)}, u32[]{:S(2)}) collective-permute-start(bf16[384,256]{1,0:T(8,128)(2,1)S(1)} %slice.25), channel_id=1, source_target_pairs={{0,48},{8,56},{16,0},{24,8},{32,16},{40,24},{48,32},{56,40},{64,11... | collective-permute-start | bytes 589832 | tf_op jit(solution)/shard_map/ppermute | solution.py:54
  49.0 0.8 dynamic-slice_compare_fusion.5
  49.8 0.8 fusion.33
  50.7 0.7 collective-permute-done.4
  51.4 4.7 %collective-permute-done.5 = bf16[384,256]{1,0:T(8,128)(2,1)S(1)} collective-permute-done((bf16[384,256]{1,0:T(8,128)(2,1)S(1)}, bf16[384,256]{1,0:T(8,128)(2,1)S(1)}, u32[]{:S(2)}, u32[]{:S(2)}) %collective-permute-start.5) | collective-permute-done | bytes 196640 | tf_op jit(solution)/shard_map/ppermute | solution.py:54
  56.1 0.1 maximum_select_fusion
  56.2 1.9 %collective-permute-start.6 = (bf16[767,256]{1,0:T(8,128)(2,1)S(1)}, bf16[767,256]{1,0:T(8,128)(2,1)S(1)}, u32[]{:S(2)}, u32[]{:S(2)}) collective-permute-start(bf16[767,256]{1,0:T(8,128)(2,1)S(1)} %maximum_select_fusion), channel_id=1, source_target_pairs={{0,64},{8,72},{16,80},{24,88},{32,96},{40,104},{48,112},{56,120},{... | collective-permute-start | bytes 1178120 | tf_op jit(solution)/shard_map/ppermute | solution.py:56
  58.1 2.5 %fusion.21 = (f32[512]{0:T(512)S(1)}, f32[512]{0:T(512)S(1)}) fusion(pred[512]{0:T(512)(128)(4,1)S(1)} %get-tuple-element.15, f32[512]{0:T(512)S(1)} %get-tuple-element.17, pred[512]{0:T(512)(128)(4,1)S(1)} %get-tuple-element.14, pred[512]{0:T(512)(128)(4,1)S(1)} %get-tuple-element.16, s32[512]{0:T(512)S(1)} %get-tuple-element.18, ...), kind=kLoop, calls=%fused_computation.28 | loop fusion | flops 9816576 | bytes 17408 | tf_op jit(solution)/shard_map/reduce_sum | solution.py:78
  60.6 0.0 copy-done
  60.7 0.2 multiply_reduce_fusion
  60.8 6.8 %collective-permute-done.6 = bf16[767,256]{1,0:T(8,128)(2,1)S(1)} collective-permute-done((bf16[767,256]{1,0:T(8,128)(2,1)S(1)}, bf16[767,256]{1,0:T(8,128)(2,1)S(1)}, u32[]{:S(2)}, u32[]{:S(2)}) %collective-permute-start.6) | collective-permute-done | bytes 392736 | tf_op jit(solution)/shard_map/ppermute | solution.py:56
  67.6 0.2 multiply_reduce_fusion.1
  67.8 0.5 multiply_subtract_fusion
  68.3 2.7 %pad.8 = f32[767,1278]{1,0:T(8,128)} pad(f32[767,767]{1,0:T(8,128)S(1)} %multiply_subtract_fusion, f32[]{:T(128)} %constant.120.clone.1), padding=0_0x511_0 | pad | bytes 6274064 | tf_op jit(solution)/shard_map/jit(_pad)/pad | solution.py:85
  71.1 5.5 %reshape.38 = f32[980226]{0:T(1024)} reshape(f32[767,1278]{1,0:T(8,128)} %pad.8) | data formatting | bytes 7841808 | tf_op jit(solution)/shard_map/reshape | solution.py:87
  76.6 4.3 %pad.9 = f32[980993]{0:T(1024)} pad(f32[980226]{0:T(1024)} %reshape.38, f32[]{:T(128)} %constant.120.clone.1), padding=0_767 | pad | bytes 7844880 | tf_op jit(solution)/shard_map/jit(_pad)/pad | solution.py:87
  80.8 7.8 %reshape.39 = f32[767,1279]{1,0:T(8,128)} reshape(f32[980993]{0:T(1024)} %pad.9) | data formatting | bytes 7847944 | tf_op jit(solution)/shard_map/reshape | solution.py:88
  88.6 9.2 %fusion = f32[512,1023]{1,0:T(8,128)} fusion(f32[767,1279]{1,0:T(8,128)} %reshape.39, f32[512]{0:T(512)S(1)} %get-tuple-element.6, pred[512]{0:T(512)(128)(4,1)S(1)} %get-tuple-element.13, f32[512]{0:T(512)S(1)} %get-tuple-element.7, pred[512]{0:T(512)(128)(4,1)S(1)} %get-tuple-element.12, pred[512]{0:T(512)(128)(4,1)S(1)} %get-tuple-element.11, ...), kind=kOutput, calls=%fused_computation | convolution fusion | flops 4826332160 | bytes 5250560 | tf_op jit(solution)/shard_map/dot_general | solution.py:89
  97.8 2.9 %reshape.40 = f32[523776]{0:T(1024)S(1)} reshape(f32[512,1023]{1,0:T(8,128)} %fusion) | data formatting | bytes 4190208 | tf_op jit(solution)/shard_map/reshape | solution.py:92
  100.8 2.0 %slice.27 = f32[523264]{0:T(1024)} slice(f32[523776]{0:T(1024)S(1)} %reshape.40), slice={[511:523775]} | slice | bytes 4186112 | tf_op jit(solution)/shard_map/slice | solution.py:92
  102.7 3.4 %reshape.41 = f32[512,1022]{1,0:T(8,128)S(1)} reshape(f32[523264]{0:T(1024)} %slice.27) | data formatting | bytes 4186112 | tf_op jit(solution)/shard_map/reshape | solution.py:93
  106.1 1.1 slice.28
  107.2 0.0 reduce-scatter.2.cloned.1.call-update
  107.2 0.9 broadcast_divide_fusion
  108.2 24.7 %all-gather.1 = f32[8,2,767]{2,1,0:T(2,128)S(1)} all-gather(f32[1,2,767]{2,1,0:T(2,128)S(1)} %maximum_bitcast_fusion), channel_id=2, replica_groups=mesh['row'=4,'col'=16,'chan'=8] {'chan'}, dimensions={0}, use_global_device_ids=true | all-gather | bytes 55224 | tf_op jit(solution)/shard_map/all_gather | solution.py:131
  132.9 0.3 fusion.18
  133.2 2.5 %fusion.13 = f32[1,512]{1,0:T(1,128)S(1)} fusion(f32[512]{0:T(512)S(1)} %get-tuple-element.5, f32[512]{0:T(512)S(1)} %get-tuple-element.17, s32[512]{0:T(512)S(1)} %get-tuple-element.18, s32[512]{0:T(512)S(1)} %get-tuple-element.19, pred[512]{0:T(512)(128)(4,1)S(1)} %get-tuple-element.15, pred[512]{0:T(512)(128)(4,1)S(1)} %get-tuple-element.14, ...), kind=kOutput, calls=%fused_computation.17 | convolution fusion | flops 10210304 | bytes 14848 | tf_op jit(solution)/shard_map/dot_general | solution.py:140
  135.7 12.2 %reduce-scatter.2.cloned.1.call-done = f32[64,512]{1,0:T(8,128)} async-done(((f32[512,512]{1,0:T(8,128)}), f32[64,512]{1,0:T(8,128)}) %reduce-scatter.2.cloned.1.call-update) | async-done | bytes 131088 | tf_op jit(solution)/shard_map/reduce_scatter | solution.py:125
  147.9 1.7 %divide_exponential_fusion = f32[64,512]{1,0:T(8,128)} fusion(f32[64,512]{1,0:T(8,128)} %reduce-scatter.2.cloned.1.call-done, f32[512]{0:T(512)S(1)} %add_sqrt_fusion, f32[64]{0:T(128)S(1)} %fusion.18), kind=kLoop, calls=%fused_computation.35 | loop fusion | flops 98304 | bytes 264448 | tf_op jit(solution)/shard_map/exp | solution.py:149
  (8 shorter events, 0.1 us)
Async XLA Ops:
  6.5 141.4 %reduce-scatter.2.cloned.1.call-start = ((), (), s32[]{:S(2)}) async-start(), calls=%async_computation.1 | async-start | bytes 1179648 | tf_op jit(solution)/shard_map/reduce_scatter | solution.py:125
  7.5 6.3 %collective-permute-start = (bf16[255,256]{1,0:T(8,128)(2,1)S(1)}, bf16[255,256]{1,0:T(8,128)(2,1)S(1)}, u32[]{:S(2)}, u32[]{:S(2)}) collective-permute-start(bf16[255,256]{1,0:T(8,128)(2,1)S(1)} %slice.18), channel_id=1, source_target_pairs={{120,0},{0,8},{8,16},{16,24},{24,32},{32,40},{40,48},{48,56},{56,6... | collective-permute-start | bytes 391688 | tf_op jit(solution)/shard_map/ppermute | solution.py:16
  14.8 5.2 %collective-permute-start.1 = (bf16[767,256]{1,0:T(8,128)(2,1)S(1)}, bf16[767,256]{1,0:T(8,128)(2,1)S(1)}, u32[]{:S(2)}, u32[]{:S(2)}) collective-permute-start(bf16[767,256]{1,0:T(8,128)(2,1)S(1)} %pad_maximum_fusion), channel_id=1, source_target_pairs={{0,8},{8,0},{16,24},{24,16},{32,40},{40,32},{48,56},{56,48},{64,72... | collective-permute-start | bytes 1178120 | tf_op jit(solution)/shard_map/ppermute | solution.py:45
  21.0 19.7 %collective-permute-start.2 = (bf16[767,256]{1,0:T(8,128)(2,1)S(1)}, bf16[767,256]{1,0:T(8,128)(2,1)S(1)}, u32[]{:S(2)}, u32[]{:S(2)}) collective-permute-start(bf16[767,256]{1,0:T(8,128)(2,1)S(1)} %broadcast_select_fusion), channel_id=1, source_target_pairs={{0,16},{8,24},{16,32},{24,40},{32,48},{40,56},{48,0},{56,8},{64,80... | collective-permute-start | bytes 1178120 | tf_op jit(solution)/shard_map/ppermute | solution.py:49
  24.4 17.5 %collective-permute-start.3 = (bf16[767,256]{1,0:T(8,128)(2,1)S(1)}, bf16[767,256]{1,0:T(8,128)(2,1)S(1)}, u32[]{:S(2)}, u32[]{:S(2)}) collective-permute-start(bf16[767,256]{1,0:T(8,128)(2,1)S(1)} %broadcast_select_fusion), channel_id=1, source_target_pairs={{0,48},{8,56},{16,0},{24,8},{32,16},{40,24},{48,32},{56,40},{64,11... | collective-permute-start | bytes 1178120 | tf_op jit(solution)/shard_map/ppermute | solution.py:50
  34.3 26.3 %copy-start = (bf16[512,256]{1,0:T(8,128)(2,1)S(1)}, bf16[512,256]{1,0:T(8,128)(2,1)}, u32[]{:S(2)}) copy-start(bf16[512,256]{1,0:T(8,128)(2,1)} %param.4) | copy-start | bytes 786436
  42.1 9.3 %collective-permute-start.4 = (bf16[383,256]{1,0:T(8,128)(2,1)S(1)}, bf16[383,256]{1,0:T(8,128)(2,1)S(1)}, u32[]{:S(2)}, u32[]{:S(2)}) collective-permute-start(bf16[383,256]{1,0:T(8,128)(2,1)S(1)} %slice.24), channel_id=1, source_target_pairs={{0,16},{8,24},{16,32},{24,40},{32,48},{40,56},{48,0},{56,8},{64,80... | collective-permute-start | bytes 588296 | tf_op jit(solution)/shard_map/ppermute | solution.py:53
  47.1 9.0 %collective-permute-start.5 = (bf16[384,256]{1,0:T(8,128)(2,1)S(1)}, bf16[384,256]{1,0:T(8,128)(2,1)S(1)}, u32[]{:S(2)}, u32[]{:S(2)}) collective-permute-start(bf16[384,256]{1,0:T(8,128)(2,1)S(1)} %slice.25), channel_id=1, source_target_pairs={{0,48},{8,56},{16,0},{24,8},{32,16},{40,24},{48,32},{56,40},{64,11... | collective-permute-start | bytes 589832 | tf_op jit(solution)/shard_map/ppermute | solution.py:54
  56.2 11.4 %collective-permute-start.6 = (bf16[767,256]{1,0:T(8,128)(2,1)S(1)}, bf16[767,256]{1,0:T(8,128)(2,1)S(1)}, u32[]{:S(2)}, u32[]{:S(2)}) collective-permute-start(bf16[767,256]{1,0:T(8,128)(2,1)S(1)} %maximum_select_fusion), channel_id=1, source_target_pairs={{0,64},{8,72},{16,80},{24,88},{32,96},{40,104},{48,112},{56,120},{... | collective-permute-start | bytes 1178120 | tf_op jit(solution)/shard_map/ppermute | solution.py:56
Sparse Core Ops, SparseCore 0:
  107.3 40.5 reduce-scatter.1

commit v2 on v1

--- a/solution.py
+++ b/solution.py
@@ -1,6 +1,10 @@
+import functools
+
 import jax
 import jax.numpy as jnp
 from jax import lax
+from jax.experimental import pallas as pl
+from jax.experimental.pallas import tpu as pltpu
 from jax.sharding import PartitionSpec as P
 
 C = 2048
@@ -78,19 +82,55 @@
     return cone / jnp.sum(cone, axis=1, keepdims=True)
 
 
-def lag_sum(weights, dist, count):
+def reversed_cone(lengths, exps, lags, depth):
+    rows = lengths.shape[0]
+    row_pos = lax.broadcasted_iota(jnp.int32, (rows, depth), 0)
+    col_pos = lax.broadcasted_iota(jnp.int32, (rows, depth), 1)
+    lag = row_pos + col_pos - (depth - lags)
+    span = lengths[:, None]
+    valid = (lag >= 0) & (lag < span)
+    frac = (span.astype(jnp.float32) - lag.astype(jnp.float32)) / span.astype(jnp.float32)
+    cone = jnp.where(valid, power_int(frac, exps[:, None]), jnp.zeros_like(frac))
+    return cone / jnp.sum(cone, axis=1, keepdims=True)
+
+
+def lag_kernel(lags, r_ref, q_ref, rp_ref, cp_ref, w_ref, o_ref):
+    inner = lax.dot_general(
+        r_ref[...], q_ref[...], (((1,), (1,)), ((), ())), preferred_element_type=jnp.float32
+    )
+    dist = rp_ref[...] + cp_ref[...] - 2.0 * inner
+    width = dist.shape[1]
     depth = dist.shape[0]
-    width = dist.shape[1]
-    columns = width - (depth - count)
-    padded = jnp.pad(dist, ((0, 0), (count - 1, 0)))
-    stride = width + count - 1
-    flat = jnp.pad(padded.reshape(-1), (0, depth))
-    skewed = flat.reshape(depth, stride + 1)[:, : columns + count - 1]
-    diagonal = jnp.dot(
-        weights, skewed, precision=lax.Precision.HIGHEST, preferred_element_type=jnp.float32
-    )
-    lined = diagonal.reshape(-1)[count - 1 : count - 1 + count * (columns + count - 2)]
-    return lined.reshape(count, columns + count - 2)[:, :columns]
+    skew = pltpu.roll(dist, width - lags, 1, stride=1, stride_axis=0)
+    block = o_ref.shape[1]
+    chunk = 128
+    band = chunk + lags
+    span = block + chunk
+    for m in range(o_ref.shape[0] // chunk):
+        low = depth - band - chunk * m
+        part = jnp.dot(
+            w_ref[chunk * m : chunk * (m + 1), low : low + band],
+            skew[low : low + band, low : low + span],
+            precision=lax.Precision.HIGHEST,
+            preferred_element_type=jnp.float32,
+        )
+        lined = pltpu.roll(part, span - (chunk - 1), 1, stride=1, stride_axis=0)
+        o_ref[chunk * m : chunk * (m + 1), :] = lined[:, :block]
+
+
+def lag_total(row_rev, col_pad, row_norm, col_norm, weights, block, lags):
+    depth = row_rev.shape[0]
+    width = col_pad.shape[0]
+    flops = 2 * depth * width * row_rev.shape[1] + 6 * 2 * block * (128 + lags) * (block + 128)
+    return pl.pallas_call(
+        functools.partial(lag_kernel, lags),
+        out_shape=jax.ShapeDtypeStruct((block, block), jnp.float32),
+        in_specs=[pl.BlockSpec(memory_space=pltpu.VMEM)] * 5,
+        out_specs=pl.BlockSpec(memory_space=pltpu.VMEM),
+        cost_estimate=pl.CostEstimate(
+            flops=flops, transcendentals=0, bytes_accessed=4 * (block * block + block * depth) + 2 * (depth + width) * 256
+        ),
+    )(row_rev, col_pad, row_norm, col_norm, weights)
 
 
 def shards(snapshots, offsets, window_len, cone_exp):
@@ -103,50 +143,37 @@
     row_ext = broadcast_col(col_ext, chosen)
     row_begin = chosen * block
     col_begin = lax.axis_index("col") * block
-    row_weights = cone_matrix(
-        lax.dynamic_slice_in_dim(window_len, row_begin, block),
-        lax.dynamic_slice_in_dim(cone_exp, row_begin, block),
-        lags,
-    )
+    extent = block + lags
+    row_lengths = lax.dynamic_slice_in_dim(window_len, row_begin, block)
+    row_exps = lax.dynamic_slice_in_dim(cone_exp, row_begin, block)
+    row_weights = reversed_cone(row_lengths, row_exps, lags, extent)
     col_weights = cone_matrix(
         lax.dynamic_slice_in_dim(window_len, col_begin, block),
         lax.dynamic_slice_in_dim(cone_exp, col_begin, block),
         lags,
     )
-    share = block // lax.axis_size("chan")
-    first = lax.axis_index("chan") * share
-    mine = lax.dynamic_slice(row_weights, (first, first), (share, share + lags - 1))
     row_wide = row_ext.astype(jnp.float32)
     col_wide = col_ext.astype(jnp.float32)
     row_part = jnp.sum(row_wide * row_wide, axis=1)
     col_part = jnp.sum(col_wide * col_wide, axis=1)
-    inner = jnp.dot(row_ext, col_ext.T, preferred_element_type=jnp.float32)
-    dist = row_part[:, None] + col_part[None, :] - 2.0 * inner
-    total = lax.psum_scatter(
-        lag_sum(row_weights, dist, lax.axis_size("chan") * share),
-        "chan",
-        scatter_dimension=0,
-        tiled=True,
-    )
-    gathered = lax.all_gather(jnp.stack([row_part, col_part]), "chan")
-    row_full, col_norms = jnp.sum(gathered, axis=0)
-    row_near = lax.dynamic_slice_in_dim(row_full, first, share + lags - 1)
-    row_scale = jnp.sqrt(
-        jnp.dot(mine, row_near, precision=lax.Precision.HIGHEST, preferred_element_type=jnp.float32)
-        / C
-        + epsilon
-    )
-    col_scale = jnp.sqrt(
-        jnp.dot(
-            col_weights,
-            col_norms,
-            precision=lax.Precision.HIGHEST,
-            preferred_element_type=jnp.float32,
-        )
-        / C
-        + epsilon
-    )
-    return jnp.exp(-total / (2.0 * C * row_scale[:, None] * col_scale[None, :]))
+    row_rev = jnp.pad(row_ext[::-1], ((extent - row_ext.shape[0], 0), (0, 0)))
+    row_part_rev = jnp.pad(row_part[::-1], (extent - row_ext.shape[0], 0))
+    width = 2 * block
+    col_pad = jnp.pad(col_ext, ((0, width - col_ext.shape[0]), (0, 0)))
+    col_part_pad = jnp.pad(col_part, (0, width - col_ext.shape[0]))
+    total = lag_total(row_rev, col_pad, row_part_rev[:, None], col_part_pad[None, :], row_weights, block, lags)
+    row_sum = jnp.dot(row_weights, row_part_rev, precision=lax.Precision.HIGHEST, preferred_element_type=jnp.float32)
+    col_sum = jnp.dot(col_weights, col_part, precision=lax.Precision.HIGHEST, preferred_element_type=jnp.float32)
+    n_chan = lax.axis_size("chan")
+    share = block // n_chan
+    tiles = total.reshape(n_chan, share, block)
+    col_rows = jnp.broadcast_to(col_sum[None, None, :], (n_chan, 1, block))
+    row_rows = jnp.pad(row_sum.reshape(n_chan, 1, share), ((0, 0), (0, 6), (0, block - share)))
+    payload = jnp.concatenate([tiles, col_rows, row_rows], axis=1).reshape(n_chan * (share + 8), block)
+    mine = lax.psum_scatter(payload, "chan", scatter_dimension=0, tiled=True)
+    row_scale = jnp.sqrt(mine[share + 1, :share] / C + epsilon)
+    col_scale = jnp.sqrt(mine[share] / C + epsilon)
+    return jnp.exp(-mine[:share] / (2.0 * C * row_scale[:, None] * col_scale[None, :]))
 
 
 def solution(mesh):

time: 157 us -> 134 us (0.85)
  the two profiles are of different devices: /device:TPU:2 before, /device:TPU:6 now
where the time goes in v2:
time: 134 us
  waiting for transfers between devices  57 us (43%)
  starting transfers between devices  27.1 us (20%)
  between operations  16.9 us (13%)
  other arithmetic  14.5 us (11%)
  local copies, waits for them, and re-layouts  6.82 us (5%)
  Pallas kernels  6.13 us (5%)
  matrix products  4.98 us (4%)
    reduce_scatter x1, waiting for transfers between devices, shards(): mine = lax.psum_scatter(payload, 'chan', scatter_dimension=0, tiled=True)  41.7 us
    pallas_call x1, Pallas kernels, lag_total(): pl.pallas_call(functools.partial(lag_kernel, lags), out_shape=jax.ShapeDt...  6.13 us
    ppermute x1, starting transfers between devices, broadcast_col(): from_left = lax.ppermute(value, 'col', plus)  5.92 us
    ppermute x1, starting transfers between devices, broadcast_col(): first = lax.ppermute(value[:half], 'col', plus)  5.6 us
    ppermute x1, starting transfers between devices, broadcast_col(): got = lax.ppermute(value, 'col', col_route(lambda z, x, k: (z + 1, x, k)))  5.54 us
    ppermute x1, waiting for transfers between devices, broadcast_col(): from_right = lax.ppermute(value, 'col', minus)  5.51 us
    ppermute x1, waiting for transfers between devices, broadcast_col(): got = lax.ppermute(value, 'col', col_route(lambda z, x, k: (z + 1, x, k)))  4.48 us
    ppermute x1, starting transfers between devices, broadcast_col(): got = lax.ppermute(value, 'col', col_route(lambda z, x, k: (z, x, k + 1)))  4.3 us
  transfers between devices with their start and end apart: 8, of which 5 were waited for; matrix products, arithmetic and copies ran while one was open for 9% of the time, Pallas kernels for 0%

profile of v2, /device:TPU:6, one launch (start us, length us, event | category | flops | bytes accessed | tf_op | source)
XLA Modules:
  0.0 133.5 jit_solution(15635636780925233290)
XLA Ops:
  6.5 0.0 reduce-scatter.2.cloned.1.call-start
  6.5 0.9 slice.18
  7.5 1.9 %collective-permute-start = (bf16[255,256]{1,0:T(8,128)(2,1)S(1)}, bf16[255,256]{1,0:T(8,128)(2,1)S(1)}, u32[]{:S(2)}, u32[]{:S(2)}) collective-permute-start(bf16[255,256]{1,0:T(8,128)(2,1)S(1)} %slice.18), channel_id=1, source_target_pairs={{120,0},{0,8},{8,16},{16,24},{24,32},{32,40},{40,48},{48,56},{56,6... | collective-permute-start | bytes 391688 | tf_op jit(solution)/shard_map/ppermute | solution.py:20
  9.4 1.2 dynamic_slice.16
  11.3 0.8 dynamic-slice_compare_fusion.2
  14.8 0.8 fusion.34
  15.6 0.0 collective-permute-done
  15.6 1.0 pad_maximum_fusion
  16.6 4.3 %collective-permute-start.1 = (bf16[767,256]{1,0:T(8,128)(2,1)S(1)}, bf16[767,256]{1,0:T(8,128)(2,1)S(1)}, u32[]{:S(2)}, u32[]{:S(2)}) collective-permute-start(bf16[767,256]{1,0:T(8,128)(2,1)S(1)} %pad_maximum_fusion), channel_id=1, source_target_pairs={{0,8},{8,0},{16,24},{24,16},{32,40},{40,32},{48,56},{56,48},{64,72... | collective-permute-start | bytes 1178120 | tf_op jit(solution)/shard_map/ppermute | solution.py:49
  20.9 1.4 %fusion.17 = f32[512]{0:T(512)S(1)} fusion(pred[512]{0:T(512)(128)(4,1)S(1)} %get-tuple-element.13, f32[512]{0:T(512)S(1)} %get-tuple-element.17, pred[512]{0:T(512)(128)(4,1)S(1)} %get-tuple-element.12, pred[512]{0:T(512)(128)(4,1)S(1)} %get-tuple-element.16, s32[512]{0:T(512)S(1)} %get-tuple-element.18), kind=kLoop, calls=%fused_computation.25 | loop fusion | flops 5897728 | bytes 7680 | tf_op jit(solution)/shard_map/reduce_sum | solution.py:94
  22.3 0.0 collective-permute-done.1
  22.3 1.1 broadcast_select_fusion
  23.4 1.9 %collective-permute-start.3 = (bf16[767,256]{1,0:T(8,128)(2,1)S(1)}, bf16[767,256]{1,0:T(8,128)(2,1)S(1)}, u32[]{:S(2)}, u32[]{:S(2)}) collective-permute-start(bf16[767,256]{1,0:T(8,128)(2,1)S(1)} %broadcast_select_fusion), channel_id=1, source_target_pairs={{0,48},{8,56},{16,0},{24,8},{32,16},{40,24},{48,32},{56,40},{64,11... | collective-permute-start | bytes 1178120 | tf_op jit(solution)/shard_map/ppermute | solution.py:54
  25.4 5.9 %collective-permute-start.2 = (bf16[767,256]{1,0:T(8,128)(2,1)S(1)}, bf16[767,256]{1,0:T(8,128)(2,1)S(1)}, u32[]{:S(2)}, u32[]{:S(2)}) collective-permute-start(bf16[767,256]{1,0:T(8,128)(2,1)S(1)} %broadcast_select_fusion), channel_id=1, source_target_pairs={{0,16},{8,24},{16,32},{24,40},{32,48},{40,56},{48,0},{56,8},{64,80... | collective-permute-start | bytes 1178120 | tf_op jit(solution)/shard_map/ppermute | solution.py:53
  31.3 2.1 %broadcast_divide_fusion.w_ref = f32[512,768]{1,0:T(8,128)} fusion(f32[512]{0:T(512)S(1)} %fusion.17, pred[512]{0:T(512)(128)(4,1)S(1)} %get-tuple-element.13, f32[512]{0:T(512)S(1)} %get-tuple-element.17, pred[512]{0:T(512)(128)(4,1)S(1)} %get-tuple-element.12, pred[512]{0:T(512)(128)(4,1)S(1)} %get-tuple-element.16, s32[512]{0:T(512)S(1)} %get-tuple-element.18), kind=kLoop, calls=%fused_computation.21 | loop fusion | flops 5898240 | bytes 1580544 | tf_op jit(solution)/shard_map/div | solution.py:94
  33.4 0.0 copy-start
  33.4 5.5 %collective-permute-done.3 = bf16[767,256]{1,0:T(8,128)(2,1)S(1)} collective-permute-done((bf16[767,256]{1,0:T(8,128)(2,1)S(1)}, bf16[767,256]{1,0:T(8,128)(2,1)S(1)}, u32[]{:S(2)}, u32[]{:S(2)}) %collective-permute-start.3) | collective-permute-done | bytes 392736 | tf_op jit(solution)/shard_map/ppermute | solution.py:54
  38.9 1.2 collective-permute-done.2
  40.1 0.1 select_select_fusion
  40.2 5.6 %collective-permute-start.4 = (bf16[383,256]{1,0:T(8,128)(2,1)S(1)}, bf16[383,256]{1,0:T(8,128)(2,1)S(1)}, u32[]{:S(2)}, u32[]{:S(2)}) collective-permute-start(bf16[383,256]{1,0:T(8,128)(2,1)S(1)} %slice.24), channel_id=1, source_target_pairs={{0,16},{8,24},{16,32},{24,40},{32,48},{40,56},{48,0},{56,8},{64,80... | collective-permute-start | bytes 588296 | tf_op jit(solution)/shard_map/ppermute | solution.py:57
  45.8 1.9 %collective-permute-start.5 = (bf16[384,256]{1,0:T(8,128)(2,1)S(1)}, bf16[384,256]{1,0:T(8,128)(2,1)S(1)}, u32[]{:S(2)}, u32[]{:S(2)}) collective-permute-start(bf16[384,256]{1,0:T(8,128)(2,1)S(1)} %slice.25), channel_id=1, source_target_pairs={{0,48},{8,56},{16,0},{24,8},{32,16},{40,24},{48,32},{56,40},{64,11... | collective-permute-start | bytes 589832 | tf_op jit(solution)/shard_map/ppermute | solution.py:58
  47.7 1.3 fusion.16
  49.1 0.0 copy-done
  49.1 0.2 multiply_reduce_fusion
  49.3 0.6 pad.23
  49.9 0.8 pad.21.q_ref
  50.7 0.0 collective-permute-done.4
  50.7 4.2 %collective-permute-done.5 = bf16[384,256]{1,0:T(8,128)(2,1)S(1)} collective-permute-done((bf16[384,256]{1,0:T(8,128)(2,1)S(1)}, bf16[384,256]{1,0:T(8,128)(2,1)S(1)}, u32[]{:S(2)}, u32[]{:S(2)}) %collective-permute-start.5) | collective-permute-done | bytes 196640 | tf_op jit(solution)/shard_map/ppermute | solution.py:58
  54.9 0.1 maximum_select_fusion
  55.0 5.5 %collective-permute-start.6 = (bf16[767,256]{1,0:T(8,128)(2,1)S(1)}, bf16[767,256]{1,0:T(8,128)(2,1)S(1)}, u32[]{:S(2)}, u32[]{:S(2)}) collective-permute-start(bf16[767,256]{1,0:T(8,128)(2,1)S(1)} %maximum_select_fusion), channel_id=1, source_target_pairs={{0,64},{8,72},{16,80},{24,88},{32,96},{40,104},{48,112},{56,120},{... | collective-permute-start | bytes 1178120 | tf_op jit(solution)/shard_map/ppermute | solution.py:60
  60.6 2.5 %fusion.10 = f32[1,512]{1,0:T(1,128)S(1)} fusion(f32[767,1]{0,1:T(1,128)S(1)} %reshape.51, f32[512]{0:T(512)S(1)} %fusion.16, f32[512]{0:T(512)S(1)} %get-tuple-element.5, s32[512]{0:T(512)S(1)} %get-tuple-element.6, s32[512]{0:T(512)S(1)} %get-tuple-element.19, pred[512]{0:T(512)(128)(4,1)S(1)} %get-tuple-element.15, ...), kind=kOutput, calls=%fused_computation.14 | convolution fusion | flops 10210304 | bytes 14844 | tf_op jit(solution)/shard_map/dot_general | solution.py:166
  63.0 4.5 %collective-permute-done.6 = bf16[767,256]{1,0:T(8,128)(2,1)S(1)} collective-permute-done((bf16[767,256]{1,0:T(8,128)(2,1)S(1)}, bf16[767,256]{1,0:T(8,128)(2,1)S(1)}, u32[]{:S(2)}, u32[]{:S(2)}) %collective-permute-start.6) | collective-permute-done | bytes 392736 | tf_op jit(solution)/shard_map/ppermute | solution.py:60
  67.5 0.2 multiply_reduce_fusion.1
  67.7 0.1 reverse
  67.8 0.1 slice.48
  67.9 0.1 pad.22
  68.0 0.9 broadcast_in_dim.81.rp_ref
  68.9 2.5 %fusion.20 = f32[1,512]{1,0:T(1,128)S(1)} fusion(f32[768,1]{0,1:T(1,128)S(1)} %reshape.53, f32[512]{0:T(512)S(1)} %fusion.17, pred[512]{0:T(512)(128)(4,1)S(1)} %get-tuple-element.13, f32[512]{0:T(512)S(1)} %get-tuple-element.17, pred[512]{0:T(512)(128)(4,1)S(1)} %get-tuple-element.12, pred[512]{0:T(512)(128)(4,1)S(1)} %get-tuple-element.16, ...), kind=kOutput, calls=%fused_computation.34 | convolution fusion | flops 10616832 | bytes 12800 | tf_op jit(solution)/shard_map/dot_general | solution.py:165
  71.4 0.1 reshape.49
  71.5 1.0 rev.6
  72.5 0.8 pad.20.r_ref
  73.4 6.1 %shard_map.46 = f32[512,512]{1,0:T(8,128)} custom-call(bf16[768,256]{1,0:T(8,128)(2,1)} %pad.20.r_ref, bf16[1024,256]{1,0:T(8,128)(2,1)} %pad.21.q_ref, f32[768,1]{1,0:T(8,128)} %broadcast_in_dim.81.rp_ref, f32[1,1024]{1,0:T(1,128)} %bitcast.16, f32[512,768]{1,0:T(8,128)} %broadcast_divide_fusion.w_ref), custom_call_target="tpu_custom_call" | custom-call | flops 1912602624 | bytes 3538944 | tf_op jit(solution)/shard_map/pallas_call | solution.py:125
  79.5 2.4 %select_maximum_fusion = f32[8,72,512]{2,1,0:T(8,128)} fusion(f32[8,1,64]{2,1,0:T(1,128)S(1)} %reshape.49, f32[8,1,512]{2,1,0:T(1,128)S(1)} %broadcast_in_dim.80, f32[8,64,512]{2,1,0:T(8,128)} %bitcast.13), kind=kLoop, calls=%fused_computation.18 | loop fusion | flops 1179648 | bytes 2246656 | tf_op jit(solution)/shard_map/concatenate | solution.py:172
  81.9 0.0 reduce-scatter.2.cloned.1.call-update
  81.9 41.7 %reduce-scatter.2.cloned.1.call-done = f32[72,512]{1,0:T(8,128)} async-done(((f32[576,512]{1,0:T(8,128)}), f32[72,512]{1,0:T(8,128)}) %reduce-scatter.2.cloned.1.call-update) | async-done | bytes 147472 | tf_op jit(solution)/shard_map/reduce_scatter | solution.py:173
  123.6 0.7 fusion.26
  124.3 0.7 fusion.22
  125.0 1.7 %fusion.19 = f32[64,512]{1,0:T(8,128)} fusion(f32[72,512]{1,0:T(8,128)} %reduce-scatter.2.cloned.1.call-done, f32[512]{0:T(512)S(1)} %bitcast.15, f32[64]{0:T(128)S(1)} %fusion.26), kind=kLoop, calls=%fused_computation.33 | loop fusion | flops 98304 | bytes 264448 | tf_op jit(solution)/shard_map/exp | solution.py:176
  (5 shorter events, 0.1 us)
Async XLA Ops:
  6.5 117.0 %reduce-scatter.2.cloned.1.call-start = ((), (), s32[]{:S(2)}) async-start(), calls=%async_computation.1 | async-start | bytes 1327104 | tf_op jit(solution)/shard_map/reduce_scatter | solution.py:173
  7.5 8.1 %collective-permute-start = (bf16[255,256]{1,0:T(8,128)(2,1)S(1)}, bf16[255,256]{1,0:T(8,128)(2,1)S(1)}, u32[]{:S(2)}, u32[]{:S(2)}) collective-permute-start(bf16[255,256]{1,0:T(8,128)(2,1)S(1)} %slice.18), channel_id=1, source_target_pairs={{120,0},{0,8},{8,16},{16,24},{24,32},{32,40},{40,48},{48,56},{56,6... | collective-permute-start | bytes 391688 | tf_op jit(solution)/shard_map/ppermute | solution.py:20
  16.6 5.8 %collective-permute-start.1 = (bf16[767,256]{1,0:T(8,128)(2,1)S(1)}, bf16[767,256]{1,0:T(8,128)(2,1)S(1)}, u32[]{:S(2)}, u32[]{:S(2)}) collective-permute-start(bf16[767,256]{1,0:T(8,128)(2,1)S(1)} %pad_maximum_fusion), channel_id=1, source_target_pairs={{0,8},{8,0},{16,24},{24,16},{32,40},{40,32},{48,56},{56,48},{64,72... | collective-permute-start | bytes 1178120 | tf_op jit(solution)/shard_map/ppermute | solution.py:49
  23.4 15.5 %collective-permute-start.3 = (bf16[767,256]{1,0:T(8,128)(2,1)S(1)}, bf16[767,256]{1,0:T(8,128)(2,1)S(1)}, u32[]{:S(2)}, u32[]{:S(2)}) collective-permute-start(bf16[767,256]{1,0:T(8,128)(2,1)S(1)} %broadcast_select_fusion), channel_id=1, source_target_pairs={{0,48},{8,56},{16,0},{24,8},{32,16},{40,24},{48,32},{56,40},{64,11... | collective-permute-start | bytes 1178120 | tf_op jit(solution)/shard_map/ppermute | solution.py:54
  25.4 14.7 %collective-permute-start.2 = (bf16[767,256]{1,0:T(8,128)(2,1)S(1)}, bf16[767,256]{1,0:T(8,128)(2,1)S(1)}, u32[]{:S(2)}, u32[]{:S(2)}) collective-permute-start(bf16[767,256]{1,0:T(8,128)(2,1)S(1)} %broadcast_select_fusion), channel_id=1, source_target_pairs={{0,16},{8,24},{16,32},{24,40},{32,48},{40,56},{48,0},{56,8},{64,80... | collective-permute-start | bytes 1178120 | tf_op jit(solution)/shard_map/ppermute | solution.py:53
  33.4 15.7 %copy-start = (bf16[512,256]{1,0:T(8,128)(2,1)S(1)}, bf16[512,256]{1,0:T(8,128)(2,1)}, u32[]{:S(2)}) copy-start(bf16[512,256]{1,0:T(8,128)(2,1)} %param.4) | copy-start | bytes 786436
  40.2 10.5 %collective-permute-start.4 = (bf16[383,256]{1,0:T(8,128)(2,1)S(1)}, bf16[383,256]{1,0:T(8,128)(2,1)S(1)}, u32[]{:S(2)}, u32[]{:S(2)}) collective-permute-start(bf16[383,256]{1,0:T(8,128)(2,1)S(1)} %slice.24), channel_id=1, source_target_pairs={{0,16},{8,24},{16,32},{24,40},{32,48},{40,56},{48,0},{56,8},{64,80... | collective-permute-start | bytes 588296 | tf_op jit(solution)/shard_map/ppermute | solution.py:57
  45.8 9.1 %collective-permute-start.5 = (bf16[384,256]{1,0:T(8,128)(2,1)S(1)}, bf16[384,256]{1,0:T(8,128)(2,1)S(1)}, u32[]{:S(2)}, u32[]{:S(2)}) collective-permute-start(bf16[384,256]{1,0:T(8,128)(2,1)S(1)} %slice.25), channel_id=1, source_target_pairs={{0,48},{8,56},{16,0},{24,8},{32,16},{40,24},{48,32},{56,40},{64,11... | collective-permute-start | bytes 589832 | tf_op jit(solution)/shard_map/ppermute | solution.py:58
  55.0 12.5 %collective-permute-start.6 = (bf16[767,256]{1,0:T(8,128)(2,1)S(1)}, bf16[767,256]{1,0:T(8,128)(2,1)S(1)}, u32[]{:S(2)}, u32[]{:S(2)}) collective-permute-start(bf16[767,256]{1,0:T(8,128)(2,1)S(1)} %maximum_select_fusion), channel_id=1, source_target_pairs={{0,64},{8,72},{16,80},{24,88},{32,96},{40,104},{48,112},{56,120},{... | collective-permute-start | bytes 1178120 | tf_op jit(solution)/shard_map/ppermute | solution.py:60
Sparse Core Ops, SparseCore 0:
  82.0 41.4 reduce-scatter.1

commit v3 on v2

--- a/solution.py
+++ b/solution.py
@@ -38,27 +38,50 @@
     return route
 
 
-def broadcast_col(value, source):
+def broadcast_band(tail, block, source):
     outer, mid, inner = COL_PARTS
-    if lax.axis_size("col") != outer * mid * inner or mid != 4 or outer != 2 or inner != 2:
-        return spread(value, "col", source)
+    count = outer * mid * inner
+    rows_total = tail.shape[0] + block.shape[0]
+    if lax.axis_size("col") != count or mid != 4 or outer != 2 or inner != 2 or rows_total % 4 != 0:
+        joined = jnp.concatenate([shifted(tail, "col", 1), block], axis=0)
+        return spread(joined, "col", source)
     me = lax.axis_index("col")
-    dz = (me // (mid * inner) - source // (mid * inner)) % outer
-    dx = ((me // inner) % mid - (source // inner) % mid) % mid
-    dk = (me % inner - source % inner) % inner
-    got = lax.ppermute(value, "col", col_route(lambda z, x, k: (z, x, k + 1)))
-    value = jnp.where(dk == 1, got, value)
+    value = jnp.concatenate([tail, block], axis=0)
+    split = tail.shape[0]
+    half = rows_total // 2
+    quarter = half // 2
+
+    def deltas(origin):
+        dz = (me // (mid * inner) - origin // (mid * inner)) % outer
+        dx = ((me // inner) % mid - (origin // inner) % mid) % mid
+        dk = (me % inner - origin % inner) % inner
+        return dz, dx, dk
+
+    tz, tx, tk = deltas((source + count - 1) % count)
+    bz, bx, bk = deltas(source)
+    core = me % inner
+    start = core * half
+    rows = start + lax.broadcasted_iota(jnp.int32, (half, 1), 0)
+
+    def pick(tail_test, block_test):
+        return jnp.where(rows < split, tail_test, block_test)
+
+    flip = col_route(lambda z, x, k: (z, x, k + 1))
+    wanted = lax.dynamic_slice_in_dim(value, (1 - core) * half, half)
+    got = lax.ppermute(wanted, "col", flip)
+    mine = jnp.where(pick(tk == 1, bk == 1), got, lax.dynamic_slice_in_dim(value, start, half))
     plus = col_route(lambda z, x, k: (z, x + 1, k))
     minus = col_route(lambda z, x, k: (z, x - 1, k))
-    from_left = lax.ppermute(value, "col", plus)
-    from_right = lax.ppermute(value, "col", minus)
-    value = jnp.where(dx == 1, from_left, jnp.where(dx == 3, from_right, value))
-    half = value.shape[0] // 2
-    first = lax.ppermute(value[:half], "col", plus)
-    second = lax.ppermute(value[half:], "col", minus)
-    value = jnp.where(dx == 2, jnp.concatenate([first, second], axis=0), value)
-    got = lax.ppermute(value, "col", col_route(lambda z, x, k: (z + 1, x, k)))
-    return jnp.where(dz == 1, got, value)
+    from_left = lax.ppermute(mine, "col", plus)
+    from_right = lax.ppermute(mine, "col", minus)
+    mine = jnp.where(pick(tx == 1, bx == 1), from_left, jnp.where(pick(tx == 3, bx == 3), from_right, mine))
+    first = lax.ppermute(mine[:quarter], "col", plus)
+    second = lax.ppermute(mine[quarter:], "col", minus)
+    mine = jnp.where(pick(tx == 2, bx == 2), jnp.concatenate([first, second], axis=0), mine)
+    got = lax.ppermute(mine, "col", col_route(lambda z, x, k: (z + 1, x, k)))
+    mine = jnp.where(pick(tz == 1, bz == 1), got, mine)
+    other = lax.ppermute(mine, "col", flip)
+    return jnp.where(core == 0, jnp.concatenate([mine, other], axis=0), jnp.concatenate([other, mine], axis=0))
 
 
 def power_int(frac, exps):
@@ -140,7 +163,7 @@
     history = shifted(tail, "col", 1)
     col_ext = jnp.concatenate([history, snapshots], axis=0)
     chosen = lax.dynamic_index_in_dim(offsets, lax.axis_index("row"), 0, keepdims=False)
-    row_ext = broadcast_col(col_ext, chosen)
+    row_ext = broadcast_band(snapshots[block - lags :], snapshots, chosen)[1:]
     row_begin = chosen * block
     col_begin = lax.axis_index("col") * block
     extent = block + lags

time: 134 us -> 133 us (level)
  the two profiles are of different devices: /device:TPU:6 before, /device:TPU:2 now
where the time goes in v3:
time: 133 us
  waiting for transfers between devices  54.8 us (41%)
  starting transfers between devices  26.2 us (20%)
  between operations  17.8 us (13%)
  other arithmetic  14.9 us (11%)
  local copies, waits for them, and re-layouts  7.71 us (6%)
  Pallas kernels  6.13 us (5%)
  matrix products  4.99 us (4%)
    reduce_scatter x1, waiting for transfers between devices, shards(): mine = lax.psum_scatter(payload, 'chan', scatter_dimension=0, tiled=True)  45.7 us
    ppermute x1, starting transfers between devices, broadcast_band(): from_right = lax.ppermute(mine, 'col', minus)  6.45 us
    pallas_call x1, Pallas kernels, lag_total(): pl.pallas_call(functools.partial(lag_kernel, lags), out_shape=jax.ShapeDt...  6.13 us
    ppermute x1, starting transfers between devices, broadcast_band(): got = lax.ppermute(mine, 'col', col_route(lambda z, x, k: (z + 1, x, k)))  4.77 us
    ppermute x1, waiting for transfers between devices, broadcast_band(): from_left = lax.ppermute(mine, 'col', plus)  4.12 us
    ppermute x1, starting transfers between devices, broadcast_band(): second = lax.ppermute(mine[quarter:], 'col', minus)  3.64 us
    ppermute x1, starting transfers between devices, broadcast_band(): got = lax.ppermute(wanted, 'col', flip)  3.42 us
  transfers between devices with their start and end apart: 9, of which 6 were waited for; matrix products, arithmetic and copies ran while one was open for 11% of the time, Pallas kernels for 0%

profile of v3, /device:TPU:2, one launch (start us, length us, event | category | flops | bytes accessed | tf_op | source)
XLA Modules:
  0.0 132.6 jit_solution(2829938026023314246)
XLA Ops:
  6.5 0.9 slice.28
  7.5 1.9 %collective-permute-start.7 = (bf16[255,256]{1,0:T(8,128)(2,1)S(1)}, bf16[255,256]{1,0:T(8,128)(2,1)S(1)}, u32[]{:S(2)}, u32[]{:S(2)}) collective-permute-start(bf16[255,256]{1,0:T(8,128)(2,1)S(1)} %slice.28), channel_id=1, source_target_pairs={{120,0},{0,8},{8,16},{16,24},{24,32},{32,40},{40,48},{48,56},{56,6... | collective-permute-start | bytes 391688 | tf_op jit(solution)/shard_map/ppermute | solution.py:20
  9.4 0.9 slice.24
  10.4 1.1 fusion.21
  11.4 3.4 %collective-permute-start = (bf16[384,256]{1,0:T(8,128)(2,1)S(1)}, bf16[384,256]{1,0:T(8,128)(2,1)S(1)}, u32[]{:S(2)}, u32[]{:S(2)}) collective-permute-start(bf16[384,256]{1,0:T(8,128)(2,1)S(1)} %fusion.21), channel_id=1, source_target_pairs={{0,8},{8,0},{16,24},{24,16},{32,40},{40,32},{48,56},{56,48},{64,72... | collective-permute-start | bytes 589832 | tf_op jit(solution)/shard_map/ppermute | solution.py:71
  14.9 1.2 dynamic_slice.22
  16.8 0.8 dynamic-slice_compare_fusion.2
  17.5 0.8 fusion.38
  18.3 1.4 %fusion.17 = f32[512]{0:T(512)S(1)} fusion(pred[512]{0:T(512)(128)(4,1)S(1)} %get-tuple-element.15, f32[512]{0:T(512)S(1)} %get-tuple-element.19, pred[512]{0:T(512)(128)(4,1)S(1)} %get-tuple-element.14, pred[512]{0:T(512)(128)(4,1)S(1)} %get-tuple-element.18, s32[512]{0:T(512)S(1)} %get-tuple-element.20), kind=kLoop, calls=%fused_computation.25 | loop fusion | flops 5897728 | bytes 7680 | tf_op jit(solution)/shard_map/reduce_sum | solution.py:117
  22.4 1.0 fusion.20
  23.5 0.0 copy-start
  23.5 6.5 %collective-permute-start.2 = (bf16[384,256]{1,0:T(8,128)(2,1)S(1)}, bf16[384,256]{1,0:T(8,128)(2,1)S(1)}, u32[]{:S(2)}, u32[]{:S(2)}) collective-permute-start(bf16[384,256]{1,0:T(8,128)(2,1)S(1)} %fusion.20), channel_id=1, source_target_pairs={{0,48},{8,56},{16,0},{24,8},{32,16},{40,24},{48,32},{56,40},{64,11... | collective-permute-start | bytes 589832 | tf_op jit(solution)/shard_map/ppermute | solution.py:76
  29.9 1.9 %collective-permute-start.1 = (bf16[384,256]{1,0:T(8,128)(2,1)S(1)}, bf16[384,256]{1,0:T(8,128)(2,1)S(1)}, u32[]{:S(2)}, u32[]{:S(2)}) collective-permute-start(bf16[384,256]{1,0:T(8,128)(2,1)S(1)} %fusion.20), channel_id=1, source_target_pairs={{0,16},{8,24},{16,32},{24,40},{32,48},{40,56},{48,0},{56,8},{64,80... | collective-permute-start | bytes 589832 | tf_op jit(solution)/shard_map/ppermute | solution.py:75
  31.9 2.1 %broadcast_divide_fusion.w_ref = f32[512,768]{1,0:T(8,128)} fusion(f32[512]{0:T(512)S(1)} %fusion.17, pred[512]{0:T(512)(128)(4,1)S(1)} %get-tuple-element.15, f32[512]{0:T(512)S(1)} %get-tuple-element.19, pred[512]{0:T(512)(128)(4,1)S(1)} %get-tuple-element.14, pred[512]{0:T(512)(128)(4,1)S(1)} %get-tuple-element.18, s32[512]{0:T(512)S(1)} %get-tuple-element.20), kind=kLoop, calls=%fused_computation.21 | loop fusion | flops 5898240 | bytes 1580544 | tf_op jit(solution)/shard_map/div | solution.py:117
  34.7 0.1 collective-permute-done.2
  34.8 4.1 %collective-permute-done.1 = bf16[384,256]{1,0:T(8,128)(2,1)S(1)} collective-permute-done((bf16[384,256]{1,0:T(8,128)(2,1)S(1)}, bf16[384,256]{1,0:T(8,128)(2,1)S(1)}, u32[]{:S(2)}, u32[]{:S(2)}) %collective-permute-start.1) | collective-permute-done | bytes 196640 | tf_op jit(solution)/shard_map/ppermute | solution.py:75
  38.9 0.2 select_select_fusion
  39.1 2.2 %collective-permute-start.3 = (bf16[192,256]{1,0:T(8,128)(2,1)S(1)}, bf16[192,256]{1,0:T(8,128)(2,1)S(1)}, u32[]{:S(2)}, u32[]{:S(2)}) collective-permute-start(bf16[192,256]{1,0:T(8,128)(2,1)S(1)} %get-tuple-element.11), channel_id=1, source_target_pairs={{0,16},{8,24},{16,32},{24,40},{32,48},{40,56},{48,0},{56,8},{64,80... | collective-permute-start | bytes 294920 | tf_op jit(solution)/shard_map/ppermute | solution.py:78
  41.3 3.6 %collective-permute-start.4 = (bf16[192,256]{1,0:T(8,128)(2,1)S(1)}, bf16[192,256]{1,0:T(8,128)(2,1)S(1)}, u32[]{:S(2)}, u32[]{:S(2)}) collective-permute-start(bf16[192,256]{1,0:T(8,128)(2,1)S(1)} %get-tuple-element.12), channel_id=1, source_target_pairs={{0,48},{8,56},{16,0},{24,8},{32,16},{40,24},{48,32},{56,40},{64,11... | collective-permute-start | bytes 294920 | tf_op jit(solution)/shard_map/ppermute | solution.py:79
  45.0 0.6 collective-permute-done.3
  45.6 2.2 %collective-permute-done.4 = bf16[192,256]{1,0:T(8,128)(2,1)S(1)} collective-permute-done((bf16[192,256]{1,0:T(8,128)(2,1)S(1)}, bf16[192,256]{1,0:T(8,128)(2,1)S(1)}, u32[]{:S(2)}, u32[]{:S(2)}) %collective-permute-start.4) | collective-permute-done | bytes 98336 | tf_op jit(solution)/shard_map/ppermute | solution.py:79
  47.9 0.1 maximum_select_fusion
  48.0 4.8 %collective-permute-start.5 = (bf16[384,256]{1,0:T(8,128)(2,1)S(1)}, bf16[384,256]{1,0:T(8,128)(2,1)S(1)}, u32[]{:S(2)}, u32[]{:S(2)}) collective-permute-start(bf16[384,256]{1,0:T(8,128)(2,1)S(1)} %maximum_select_fusion), channel_id=1, source_target_pairs={{0,64},{8,72},{16,80},{24,88},{32,96},{40,104},{48,112},{56,120},{... | collective-permute-start | bytes 589832 | tf_op jit(solution)/shard_map/ppermute | solution.py:81
  52.8 1.3 fusion.16
  54.1 0.2 multiply_reduce_fusion
  54.3 2.1 %collective-permute-done.5 = bf16[384,256]{1,0:T(8,128)(2,1)S(1)} collective-permute-done((bf16[384,256]{1,0:T(8,128)(2,1)S(1)}, bf16[384,256]{1,0:T(8,128)(2,1)S(1)}, u32[]{:S(2)}, u32[]{:S(2)}) %collective-permute-start.5) | collective-permute-done | bytes 196640 | tf_op jit(solution)/shard_map/ppermute | solution.py:81
  56.4 0.1 broadcast_select_fusion
  56.5 1.9 %collective-permute-start.6 = (bf16[384,256]{1,0:T(8,128)(2,1)S(1)}, bf16[384,256]{1,0:T(8,128)(2,1)S(1)}, u32[]{:S(2)}, u32[]{:S(2)}) collective-permute-start(bf16[384,256]{1,0:T(8,128)(2,1)S(1)} %broadcast_select_fusion), channel_id=1, source_target_pairs={{0,8},{8,0},{16,24},{24,16},{32,40},{40,32},{48,56},{56,48},{64,72... | collective-permute-start | bytes 589832 | tf_op jit(solution)/shard_map/ppermute | solution.py:83
  58.4 2.5 %fusion.10 = f32[1,512]{1,0:T(1,128)S(1)} fusion(f32[767,1]{0,1:T(1,128)S(1)} %reshape.72, f32[512]{0:T(512)S(1)} %fusion.16, f32[512]{0:T(512)S(1)} %get-tuple-element.5, s32[512]{0:T(512)S(1)} %get-tuple-element.6, s32[512]{0:T(512)S(1)} %get-tuple-element.23, pred[512]{0:T(512)(128)(4,1)S(1)} %get-tuple-element.17, ...), kind=kOutput, calls=%fused_computation.14 | convolution fusion | flops 10210304 | bytes 14844 | tf_op jit(solution)/shard_map/dot_general | solution.py:189
  60.9 0.6 pad.23
  61.5 0.1 pad_maximum_fusion.2
  61.6 0.8 pad.21.q_ref
  62.4 0.3 multiply_reduce_fusion.1
  62.7 0.1 reverse
  62.8 0.1 slice.56
  62.9 0.1 pad.22
  63.0 0.9 broadcast_in_dim.156.rp_ref
  63.9 2.5 %fusion.24 = f32[1,512]{1,0:T(1,128)S(1)} fusion(f32[768,1]{0,1:T(1,128)S(1)} %reshape.74, f32[512]{0:T(512)S(1)} %fusion.17, pred[512]{0:T(512)(128)(4,1)S(1)} %get-tuple-element.15, f32[512]{0:T(512)S(1)} %get-tuple-element.19, pred[512]{0:T(512)(128)(4,1)S(1)} %get-tuple-element.14, pred[512]{0:T(512)(128)(4,1)S(1)} %get-tuple-element.18, ...), kind=kOutput, calls=%fused_computation.43 | convolution fusion | flops 10616832 | bytes 12800 | tf_op jit(solution)/shard_map/dot_general | solution.py:188
  66.4 0.1 reshape.70
  66.5 1.0 rev.6
  67.6 0.8 pad.20.r_ref
  68.4 6.1 %shard_map.46 = f32[512,512]{1,0:T(8,128)} custom-call(bf16[768,256]{1,0:T(8,128)(2,1)} %pad.20.r_ref, bf16[1024,256]{1,0:T(8,128)(2,1)} %pad.21.q_ref, f32[768,1]{1,0:T(8,128)} %broadcast_in_dim.156.rp_ref, f32[1,1024]{1,0:T(1,128)} %bitcast.16, f32[512,768]{1,0:T(8,128)} %broadcast_divide_fusion.w_ref), custom_call_target="tpu_custom_call" | custom-call | flops 1912602624 | bytes 3538944 | tf_op jit(solution)/shard_map/pallas_call | solution.py:148
  74.6 2.4 %select_maximum_fusion = f32[8,72,512]{2,1,0:T(8,128)} fusion(f32[8,1,64]{2,1,0:T(1,128)S(1)} %reshape.70, f32[8,1,512]{2,1,0:T(1,128)S(1)} %broadcast_in_dim.155, f32[8,64,512]{2,1,0:T(8,128)} %bitcast.13), kind=kLoop, calls=%fused_computation.18 | loop fusion | flops 1179648 | bytes 2246656 | tf_op jit(solution)/shard_map/concatenate | solution.py:195
  76.9 0.0 reduce-scatter.2.cloned.1.call-update
  77.0 45.7 %reduce-scatter.2.cloned.1.call-done = f32[72,512]{1,0:T(8,128)} async-done(((f32[576,512]{1,0:T(8,128)}), f32[72,512]{1,0:T(8,128)}) %reduce-scatter.2.cloned.1.call-update) | async-done | bytes 147472 | tf_op jit(solution)/shard_map/reduce_scatter | solution.py:196
  122.6 0.7 fusion.32
  123.3 0.7 fusion.26
  124.0 1.7 %fusion.23 = f32[64,512]{1,0:T(8,128)} fusion(f32[72,512]{1,0:T(8,128)} %reduce-scatter.2.cloned.1.call-done, f32[512]{0:T(512)S(1)} %bitcast.15, f32[64]{0:T(128)S(1)} %fusion.32), kind=kLoop, calls=%fused_computation.42 | loop fusion | flops 98304 | bytes 264448 | tf_op jit(solution)/shard_map/exp | solution.py:199
  (13 shorter events, 0.1 us)
Async XLA Ops:
  6.5 116.1 %reduce-scatter.2.cloned.1.call-start = ((), (), s32[]{:S(2)}) async-start(), calls=%async_computation.1 | async-start | bytes 1327104 | tf_op jit(solution)/shard_map/reduce_scatter | solution.py:196
  7.5 46.6 %collective-permute-start.7 = (bf16[255,256]{1,0:T(8,128)(2,1)S(1)}, bf16[255,256]{1,0:T(8,128)(2,1)S(1)}, u32[]{:S(2)}, u32[]{:S(2)}) collective-permute-start(bf16[255,256]{1,0:T(8,128)(2,1)S(1)} %slice.28), channel_id=1, source_target_pairs={{120,0},{0,8},{8,16},{16,24},{24,32},{32,40},{40,48},{48,56},{56,6... | collective-permute-start | bytes 391688 | tf_op jit(solution)/shard_map/ppermute | solution.py:20
  11.4 11.0 %collective-permute-start = (bf16[384,256]{1,0:T(8,128)(2,1)S(1)}, bf16[384,256]{1,0:T(8,128)(2,1)S(1)}, u32[]{:S(2)}, u32[]{:S(2)}) collective-permute-start(bf16[384,256]{1,0:T(8,128)(2,1)S(1)} %fusion.21), channel_id=1, source_target_pairs={{0,8},{8,0},{16,24},{24,16},{32,40},{40,32},{48,56},{56,48},{64,72... | collective-permute-start | bytes 589832 | tf_op jit(solution)/shard_map/ppermute | solution.py:71
  23.5 30.7 %copy-start = (bf16[512,256]{1,0:T(8,128)(2,1)S(1)}, bf16[512,256]{1,0:T(8,128)(2,1)}, u32[]{:S(2)}) copy-start(bf16[512,256]{1,0:T(8,128)(2,1)} %param.4) | copy-start | bytes 786436
  23.5 11.3 %collective-permute-start.2 = (bf16[384,256]{1,0:T(8,128)(2,1)S(1)}, bf16[384,256]{1,0:T(8,128)(2,1)S(1)}, u32[]{:S(2)}, u32[]{:S(2)}) collective-permute-start(bf16[384,256]{1,0:T(8,128)(2,1)S(1)} %fusion.20), channel_id=1, source_target_pairs={{0,48},{8,56},{16,0},{24,8},{32,16},{40,24},{48,32},{56,40},{64,11... | collective-permute-start | bytes 589832 | tf_op jit(solution)/shard_map/ppermute | solution.py:76
  29.9 9.0 %collective-permute-start.1 = (bf16[384,256]{1,0:T(8,128)(2,1)S(1)}, bf16[384,256]{1,0:T(8,128)(2,1)S(1)}, u32[]{:S(2)}, u32[]{:S(2)}) collective-permute-start(bf16[384,256]{1,0:T(8,128)(2,1)S(1)} %fusion.20), channel_id=1, source_target_pairs={{0,16},{8,24},{16,32},{24,40},{32,48},{40,56},{48,0},{56,8},{64,80... | collective-permute-start | bytes 589832 | tf_op jit(solution)/shard_map/ppermute | solution.py:75
  39.1 6.5 %collective-permute-start.3 = (bf16[192,256]{1,0:T(8,128)(2,1)S(1)}, bf16[192,256]{1,0:T(8,128)(2,1)S(1)}, u32[]{:S(2)}, u32[]{:S(2)}) collective-permute-start(bf16[192,256]{1,0:T(8,128)(2,1)S(1)} %get-tuple-element.11), channel_id=1, source_target_pairs={{0,16},{8,24},{16,32},{24,40},{32,48},{40,56},{48,0},{56,8},{64,80... | collective-permute-start | bytes 294920 | tf_op jit(solution)/shard_map/ppermute | solution.py:78
  41.3 6.5 %collective-permute-start.4 = (bf16[192,256]{1,0:T(8,128)(2,1)S(1)}, bf16[192,256]{1,0:T(8,128)(2,1)S(1)}, u32[]{:S(2)}, u32[]{:S(2)}) collective-permute-start(bf16[192,256]{1,0:T(8,128)(2,1)S(1)} %get-tuple-element.12), channel_id=1, source_target_pairs={{0,48},{8,56},{16,0},{24,8},{32,16},{40,24},{48,32},{56,40},{64,11... | collective-permute-start | bytes 294920 | tf_op jit(solution)/shard_map/ppermute | solution.py:79
  48.0 8.4 %collective-permute-start.5 = (bf16[384,256]{1,0:T(8,128)(2,1)S(1)}, bf16[384,256]{1,0:T(8,128)(2,1)S(1)}, u32[]{:S(2)}, u32[]{:S(2)}) collective-permute-start(bf16[384,256]{1,0:T(8,128)(2,1)S(1)} %maximum_select_fusion), channel_id=1, source_target_pairs={{0,64},{8,72},{16,80},{24,88},{32,96},{40,104},{48,112},{56,120},{... | collective-permute-start | bytes 589832 | tf_op jit(solution)/shard_map/ppermute | solution.py:81
  56.5 5.9 %collective-permute-start.6 = (bf16[384,256]{1,0:T(8,128)(2,1)S(1)}, bf16[384,256]{1,0:T(8,128)(2,1)S(1)}, u32[]{:S(2)}, u32[]{:S(2)}) collective-permute-start(bf16[384,256]{1,0:T(8,128)(2,1)S(1)} %broadcast_select_fusion), channel_id=1, source_target_pairs={{0,8},{8,0},{16,24},{24,16},{32,40},{40,32},{48,56},{56,48},{64,72... | collective-permute-start | bytes 589832 | tf_op jit(solution)/shard_map/ppermute | solution.py:83
Sparse Core Ops, SparseCore 0:
  77.1 45.4 reduce-scatter.1

commit v4 on v3

--- a/solution.py
+++ b/solution.py
@@ -82,6 +82,27 @@
     mine = jnp.where(pick(tz == 1, bz == 1), got, mine)
     other = lax.ppermute(mine, "col", flip)
     return jnp.where(core == 0, jnp.concatenate([mine, other], axis=0), jnp.concatenate([other, mine], axis=0))
+
+
+def broadcast_pieces(tail, block, source):
+    count = lax.axis_size("col")
+    value = jnp.concatenate([tail, block], axis=0)
+    rows_total = value.shape[0]
+    if rows_total % count != 0:
+        joined = jnp.concatenate([shifted(tail, "col", 1), block], axis=0)
+        return spread(joined, "col", source)
+    piece = rows_total // count
+    split = tail.shape[0]
+    parts = value.reshape(count, piece, value.shape[1])
+    got = lax.all_to_all(parts, "col", 0, 0, tiled=False)
+    me = lax.axis_index("col")
+    rows = me * piece + lax.broadcasted_iota(jnp.int32, (piece, 1), 0)
+    early = lax.dynamic_index_in_dim(got, (source + count - 1) % count, 0, keepdims=False)
+    late = lax.dynamic_index_in_dim(got, source, 0, keepdims=False)
+    mine = jnp.where(rows < split, early, late)
+    spread_out = jnp.broadcast_to(mine[None], (count, piece, value.shape[1]))
+    full = lax.all_to_all(spread_out, "col", 0, 0, tiled=False)
+    return full.reshape(rows_total, value.shape[1])
 
 
 def power_int(frac, exps):
@@ -163,7 +184,7 @@
     history = shifted(tail, "col", 1)
     col_ext = jnp.concatenate([history, snapshots], axis=0)
     chosen = lax.dynamic_index_in_dim(offsets, lax.axis_index("row"), 0, keepdims=False)
-    row_ext = broadcast_band(snapshots[block - lags :], snapshots, chosen)[1:]
+    row_ext = broadcast_pieces(snapshots[block - lags :], snapshots, chosen)[1:]
     row_begin = chosen * block
     col_begin = lax.axis_index("col") * block
     extent = block + lags

time: 133 us -> 113 us (0.85)
  waiting for transfers between devices: 54.8 us -> 43.4 us
  starting transfers between devices: 26.2 us -> 18.7 us
    ppermute x7 -> x0, starting transfers between devices: 24.3 us -> none  [the longest x1 6.45 us: broadcast_band(): from_right = lax.ppermute(mine, 'col', minus)]
    all_to_all x0 -> x2, starting transfers between devices: none -> 16.8 us  [the longest x1 11 us: broadcast_pieces(): got = lax.all_to_all(parts, 'col', 0, 0, tiled=False)]
    ppermute x7 -> x0, waiting for transfers between devices: 9.11 us -> none  [the longest x1 4.12 us: broadcast_band(): from_left = lax.ppermute(mine, 'col', plus)]
    reduce_scatter x1, waiting for transfers between devices: 45.7 us -> 42.4 us  [shards(): mine = lax.psum_scatter(payload, 'chan', scatter_dimension=0, tiled=True)]
    select_n x8 -> x0, other arithmetic: 1.43 us -> none  [the longest x1 1 us: broadcast_band(): jnp.where(pick(tk == 1, bk == 1), got, lax.dynamic_slice_in_dim(value, st...]
  transfers between devices with their start and end apart: 9 -> 4, of which waited for: 6 -> 2; matrix products, arithmetic and copies ran while one was open for 11% -> 13% of each run, Pallas kernels for 0% -> 0%
where the time goes in v4:
time: 113 us; the launch traced here: 112 us
  waiting for transfers between devices  43.4 us (38%)
  starting transfers between devices  18.7 us (17%)
  between operations  16.8 us (15%)
  other arithmetic  14 us (12%)
  local copies, waits for them, and re-layouts  7.85 us (7%)
  Pallas kernels  6.15 us (5%)
  matrix products  4.95 us (4%)
    reduce_scatter x1, waiting for transfers between devices, shards(): mine = lax.psum_scatter(payload, 'chan', scatter_dimension=0, tiled=True)  42.4 us
    all_to_all x1, starting transfers between devices, broadcast_pieces(): got = lax.all_to_all(parts, 'col', 0, 0, tiled=False)  11 us
    pallas_call x1, Pallas kernels, lag_total(): pl.pallas_call(functools.partial(lag_kernel, lags), out_shape=jax.ShapeDt...  6.15 us
    all_to_all x1, starting transfers between devices, broadcast_pieces(): full = lax.all_to_all(spread_out, 'col', 0, 0, tiled=False)  5.72 us
    dot_general x1, matrix products, shards(): jnp.dot(row_weights, row_part_rev, precision=lax.Precision.HIGHEST, prefe...  2.52 us
    dot_general x1, matrix products, shards(): jnp.dot(col_weights, col_part, precision=lax.Precision.HIGHEST, preferred...  2.42 us
    concatenate x1, other arithmetic, shards(): jnp.concatenate([tiles, col_rows, row_rows], axis=1)  2.37 us
  transfers between devices with their start and end apart: 4, of which 2 were waited for; matrix products, arithmetic and copies ran while one was open for 13% of the time, Pallas kernels for 0%

profile of v4, /device:TPU:2, one launch (start us, length us, event | category | flops | bytes accessed | tf_op | source)
XLA Modules:
  0.0 111.9 jit_solution(13182063167574492308)
XLA Ops:
  6.5 0.0 copy-start.1
  6.5 0.9 slice.20
  7.5 1.9 %collective-permute-start = (bf16[255,256]{1,0:T(8,128)(2,1)S(1)}, bf16[255,256]{1,0:T(8,128)(2,1)S(1)}, u32[]{:S(2)}, u32[]{:S(2)}) collective-permute-start(bf16[255,256]{1,0:T(8,128)(2,1)S(1)} %slice.20), channel_id=1, source_target_pairs={{120,0},{0,8},{8,16},{16,24},{24,32},{32,40},{40,48},{48,56},{56,6... | collective-permute-start | bytes 391688 | tf_op jit(solution)/shard_map/ppermute | solution.py:20
  9.4 0.9 slice.18
  10.3 1.7 %pad_maximum_fusion = bf16[768,256]{1,0:T(8,128)(2,1)} fusion(bf16[512,256]{1,0:T(8,128)(2,1)} %param.4, bf16[256,256]{1,0:T(8,128)(2,1)S(1)} %slice.18), kind=kLoop, calls=%fused_computation.26 | loop fusion | flops 786432 | bytes 786432 | tf_op jit(solution)/shard_map/concatenate | solution.py:89
  12.1 11.0 %all-to-all-start = ((bf16[16,48,256]{2,1,0:T(8,128)(2,1)}), bf16[16,48,256]{2,1,0:T(8,128)(2,1)S(1)}, u32[]{:S(2)}, u32[]{:S(2)}) async-start(bf16[16,48,256]{2,1,0:T(8,128)(2,1)} %bitcast), calls=%async_computation | async-start | bytes 786432 | tf_op jit(solution)/shard_map/all_to_all | solution.py:97
  23.1 0.0 copy-start
  23.1 0.0 copy-done.1
  23.1 0.6 dynamic_slice.23
  24.4 0.8 dynamic-slice_compare_fusion.2
  25.2 0.8 fusion.34
  25.9 1.4 %fusion.17 = f32[512]{0:T(512)S(1)} fusion(pred[512]{0:T(512)(128)(4,1)S(1)} %get-tuple-element.11, f32[512]{0:T(512)S(1)} %get-tuple-element.15, pred[512]{0:T(512)(128)(4,1)S(1)} %get-tuple-element.10, pred[512]{0:T(512)(128)(4,1)S(1)} %get-tuple-element.14, s32[512]{0:T(512)S(1)} %get-tuple-element.16), kind=kLoop, calls=%fused_computation.25 | loop fusion | flops 5897728 | bytes 7680 | tf_op jit(solution)/shard_map/reduce_sum | solution.py:138
  30.0 2.1 %broadcast_divide_fusion.w_ref = f32[512,768]{1,0:T(8,128)} fusion(f32[512]{0:T(512)S(1)} %fusion.17, pred[512]{0:T(512)(128)(4,1)S(1)} %get-tuple-element.11, f32[512]{0:T(512)S(1)} %get-tuple-element.15, pred[512]{0:T(512)(128)(4,1)S(1)} %get-tuple-element.10, pred[512]{0:T(512)(128)(4,1)S(1)} %get-tuple-element.14, s32[512]{0:T(512)S(1)} %get-tuple-element.16), kind=kLoop, calls=%fused_computation.21 | loop fusion | flops 5898240 | bytes 1580544 | tf_op jit(solution)/shard_map/div | solution.py:138
  32.1 0.0 all-to-all-done
  32.1 0.1 select_bitcast_fusion
  32.2 0.8 broadcast_in_dim.86
  32.9 5.7 %all-to-all-start.1 = ((bf16[16,48,256]{2,1,0:T(8,128)(2,1)}), bf16[16,48,256]{2,1,0:T(8,128)(2,1)S(1)}, u32[]{:S(2)}, u32[]{:S(2)}) async-start(bf16[16,48,256]{2,1,0:T(8,128)(2,1)} %broadcast_in_dim.86), calls=%async_computation.1 | async-start | bytes 786432 | tf_op jit(solution)/shard_map/all_to_all | solution.py:104
  38.6 0.0 reduce-scatter.2.cloned.1.call-start
  38.7 1.3 %fusion.16 = f32[512]{0:T(512)S(1)} fusion(pred[512]{0:T(512)(128)(4,1)S(1)} %get-tuple-element.13, f32[512]{0:T(512)S(1)} %get-tuple-element.5, pred[512]{0:T(512)(128)(4,1)S(1)} %get-tuple-element.12, pred[512]{0:T(512)(128)(4,1)S(1)} %get-tuple-element.9, s32[512]{0:T(512)S(1)} %get-tuple-element.6, s32[512]{0:T(512)S(1)} %get-tuple-element.17), kind=kLoop, calls=%fused_computation.24 | loop fusion | flops 5497344 | bytes 9728 | tf_op jit(solution)/shard_map/reduce_sum | solution.py:126
  39.9 0.0 collective-permute-done
  40.0 0.0 copy-done
  40.0 0.2 multiply_reduce_fusion
  40.2 0.6 pad.23
  40.8 0.1 pad_maximum_fusion.1
  40.8 0.8 pad.21.q_ref
  41.7 2.4 %fusion.10 = f32[1,512]{1,0:T(1,128)S(1)} fusion(f32[767,1]{0,1:T(1,128)S(1)} %reshape.73, f32[512]{0:T(512)S(1)} %fusion.16, f32[512]{0:T(512)S(1)} %get-tuple-element.5, s32[512]{0:T(512)S(1)} %get-tuple-element.6, s32[512]{0:T(512)S(1)} %get-tuple-element.17, pred[512]{0:T(512)(128)(4,1)S(1)} %get-tuple-element.13, ...), kind=kOutput, calls=%fused_computation.14 | convolution fusion | flops 10210304 | bytes 14844 | tf_op jit(solution)/shard_map/dot_general | solution.py:210
  44.1 1.0 all-to-all-done.1
  45.1 0.2 multiply_reduce_fusion.1
  45.3 0.1 slice.24
  45.4 0.1 reverse
  45.5 0.1 slice.48
  45.6 0.1 pad.22
  45.7 0.9 broadcast_in_dim.100.rp_ref
  46.6 1.0 rev.6
  47.6 0.8 pad.20.r_ref
  48.4 2.5 %fusion.20 = f32[1,512]{1,0:T(1,128)S(1)} fusion(f32[768,1]{0,1:T(1,128)S(1)} %reshape.75, f32[512]{0:T(512)S(1)} %fusion.17, pred[512]{0:T(512)(128)(4,1)S(1)} %get-tuple-element.11, f32[512]{0:T(512)S(1)} %get-tuple-element.15, pred[512]{0:T(512)(128)(4,1)S(1)} %get-tuple-element.10, pred[512]{0:T(512)(128)(4,1)S(1)} %get-tuple-element.14, ...), kind=kOutput, calls=%fused_computation.31 | convolution fusion | flops 10616832 | bytes 12800 | tf_op jit(solution)/shard_map/dot_general | solution.py:209
  50.9 0.1 reshape.71
  51.0 6.1 %shard_map.46 = f32[512,512]{1,0:T(8,128)} custom-call(bf16[768,256]{1,0:T(8,128)(2,1)} %pad.20.r_ref, bf16[1024,256]{1,0:T(8,128)(2,1)} %pad.21.q_ref, f32[768,1]{1,0:T(8,128)} %broadcast_in_dim.100.rp_ref, f32[1,1024]{1,0:T(1,128)} %bitcast.22, f32[512,768]{1,0:T(8,128)} %broadcast_divide_fusion.w_ref), custom_call_target="tpu_custom_call" | custom-call | flops 1912602624 | bytes 3538944 | tf_op jit(solution)/shard_map/pallas_call | solution.py:169
  57.2 2.4 %select_maximum_fusion = f32[8,72,512]{2,1,0:T(8,128)} fusion(f32[8,1,64]{2,1,0:T(1,128)S(1)} %reshape.71, f32[8,1,512]{2,1,0:T(1,128)S(1)} %broadcast_in_dim.99, f32[8,64,512]{2,1,0:T(8,128)} %bitcast.19), kind=kLoop, calls=%fused_computation.18 | loop fusion | flops 1179648 | bytes 2246656 | tf_op jit(solution)/shard_map/concatenate | solution.py:216
  59.5 0.0 reduce-scatter.2.cloned.1.call-update
  59.6 42.4 %reduce-scatter.2.cloned.1.call-done = f32[72,512]{1,0:T(8,128)} async-done(((f32[576,512]{1,0:T(8,128)}), f32[72,512]{1,0:T(8,128)}) %reduce-scatter.2.cloned.1.call-update) | async-done | bytes 147472 | tf_op jit(solution)/shard_map/reduce_scatter | solution.py:217
  102.0 0.7 fusion.26
  102.7 0.7 fusion.22
  103.4 1.7 %fusion.19 = f32[64,512]{1,0:T(8,128)} fusion(f32[72,512]{1,0:T(8,128)} %reduce-scatter.2.cloned.1.call-done, f32[512]{0:T(512)S(1)} %bitcast.21, f32[64]{0:T(128)S(1)} %fusion.26), kind=kLoop, calls=%fused_computation.30 | loop fusion | flops 98304 | bytes 264448 | tf_op jit(solution)/shard_map/exp | solution.py:220
  (4 shorter events, 0.0 us)
Async XLA Ops:
  6.5 16.6 %copy-start.1 = (s32[4]{0:T(128)S(1)}, s32[4]{0:T(128)}, u32[]{:S(2)}) copy-start(s32[4]{0:T(128)} %param.5) | copy-start | bytes 52
  7.5 32.5 %collective-permute-start = (bf16[255,256]{1,0:T(8,128)(2,1)S(1)}, bf16[255,256]{1,0:T(8,128)(2,1)S(1)}, u32[]{:S(2)}, u32[]{:S(2)}) collective-permute-start(bf16[255,256]{1,0:T(8,128)(2,1)S(1)} %slice.20), channel_id=1, source_target_pairs={{120,0},{0,8},{8,16},{16,24},{24,32},{32,40},{40,48},{48,56},{56,6... | collective-permute-start | bytes 391688 | tf_op jit(solution)/shard_map/ppermute | solution.py:20
  12.1 20.0 %all-to-all-start = ((bf16[16,48,256]{2,1,0:T(8,128)(2,1)}), bf16[16,48,256]{2,1,0:T(8,128)(2,1)S(1)}, u32[]{:S(2)}, u32[]{:S(2)}) async-start(bf16[16,48,256]{2,1,0:T(8,128)(2,1)} %bitcast), calls=%async_computation | async-start | bytes 786432 | tf_op jit(solution)/shard_map/all_to_all | solution.py:97
  23.1 16.9 %copy-start = (bf16[512,256]{1,0:T(8,128)(2,1)S(1)}, bf16[512,256]{1,0:T(8,128)(2,1)}, u32[]{:S(2)}) copy-start(bf16[512,256]{1,0:T(8,128)(2,1)} %param.4) | copy-start | bytes 786436
  32.9 12.2 %all-to-all-start.1 = ((bf16[16,48,256]{2,1,0:T(8,128)(2,1)}), bf16[16,48,256]{2,1,0:T(8,128)(2,1)S(1)}, u32[]{:S(2)}, u32[]{:S(2)}) async-start(bf16[16,48,256]{2,1,0:T(8,128)(2,1)} %broadcast_in_dim.86), calls=%async_computation.1 | async-start | bytes 786432 | tf_op jit(solution)/shard_map/all_to_all | solution.py:104
  38.6 63.3 %reduce-scatter.2.cloned.1.call-start = ((), (), s32[]{:S(2)}) async-start(), calls=%async_computation.3 | async-start | bytes 1327104 | tf_op jit(solution)/shard_map/reduce_scatter | solution.py:217
Sparse Core Ops, SparseCore 0:
  59.7 42.2 reduce-scatter.1

commit v5 on v4

--- a/solution.py
+++ b/solution.py
@@ -213,8 +213,8 @@
     tiles = total.reshape(n_chan, share, block)
     col_rows = jnp.broadcast_to(col_sum[None, None, :], (n_chan, 1, block))
     row_rows = jnp.pad(row_sum.reshape(n_chan, 1, share), ((0, 0), (0, 6), (0, block - share)))
-    payload = jnp.concatenate([tiles, col_rows, row_rows], axis=1).reshape(n_chan * (share + 8), block)
-    mine = lax.psum_scatter(payload, "chan", scatter_dimension=0, tiled=True)
+    payload = jnp.concatenate([tiles, col_rows, row_rows], axis=1)
+    mine = jnp.sum(lax.all_to_all(payload, "chan", 0, 0, tiled=False), axis=0)
     row_scale = jnp.sqrt(mine[share + 1, :share] / C + epsilon)
     col_scale = jnp.sqrt(mine[share] / C + epsilon)
     return jnp.exp(-mine[:share] / (2.0 * C * row_scale[:, None] * col_scale[None, :]))

time: 113 us -> 90.5 us (0.80)
  the two profiles are of different devices: /device:TPU:2 before, /device:TPU:1 now
where the time goes in v5:
time: 90.5 us; the launch traced here: 89 us
  blocking collectives  33.3 us (37%)
  starting transfers between devices  19.7 us (22%)
  other arithmetic  10.8 us (12%)
  local copies, waits for them, and re-layouts  7.85 us (9%)
  Pallas kernels  6.15 us (7%)
  matrix products  4.95 us (5%)
  between operations  3.4 us (4%)
  waiting for transfers between devices  2.99 us (3%)
    all_to_all x1, blocking collectives, shards(): mine = jnp.sum(lax.all_to_all(payload, 'chan', 0, 0, tiled=False), axis=0)  33.3 us
    all_to_all x1, starting transfers between devices, broadcast_pieces(): got = lax.all_to_all(parts, 'col', 0, 0, tiled=False)  9.42 us
    pallas_call x1, Pallas kernels, lag_total(): pl.pallas_call(functools.partial(lag_kernel, lags), out_shape=jax.ShapeDt...  6.15 us
    all_to_all x1, starting transfers between devices, broadcast_pieces(): full = lax.all_to_all(spread_out, 'col', 0, 0, tiled=False)  5.72 us
    ppermute x1, starting transfers between devices, shifted(): return lax.ppermute(block, axis, route)  4.51 us
    all_to_all x1, waiting for transfers between devices, broadcast_pieces(): full = lax.all_to_all(spread_out, 'col', 0, 0, tiled=False)  2.99 us
    dot_general x1, matrix products, shards(): jnp.dot(row_weights, row_part_rev, precision=lax.Precision.HIGHEST, prefe...  2.52 us
    dot_general x1, matrix products, shards(): jnp.dot(col_weights, col_part, precision=lax.Precision.HIGHEST, preferred...  2.42 us
  transfers between devices with their start and end apart: 3, of which 1 were waited for; matrix products, arithmetic and copies ran while one was open for 16% of the time, Pallas kernels for 0%

profile of v5, /device:TPU:1, one launch (start us, length us, event | category | flops | bytes accessed | tf_op | source)
XLA Modules:
  0.0 89.0 jit_solution(16150789578406150863)
XLA Ops:
  0.0 0.0 copy-start.1
  0.0 0.9 %slice.20 = bf16[255,256]{1,0:T(8,128)(2,1)S(1)} slice(bf16[512,256]{1,0:T(8,128)(2,1)} %param.4), slice={[257:512], [0:256]} | slice | bytes 261120 | tf_op jit(solution)/shard_map/slice | solution.py:183
  1.0 4.5 %collective-permute-start = (bf16[255,256]{1,0:T(8,128)(2,1)S(1)}, bf16[255,256]{1,0:T(8,128)(2,1)S(1)}, u32[]{:S(2)}, u32[]{:S(2)}) collective-permute-start(bf16[255,256]{1,0:T(8,128)(2,1)S(1)} %slice.20), channel_id=1, source_target_pairs={{120,0},{0,8},{8,16},{16,24},{24,32},{32,40},{40,48},{48,56},{56,6... | collective-permute-start | bytes 391688 | tf_op jit(solution)/shard_map/ppermute | solution.py:20
  5.5 0.9 %slice.18 = bf16[256,256]{1,0:T(8,128)(2,1)S(1)} slice(bf16[512,256]{1,0:T(8,128)(2,1)} %param.4), slice={[256:512], [0:256]} | slice | bytes 262144 | tf_op jit(solution)/shard_map/slice | solution.py:187
  6.4 1.7 %pad_maximum_fusion = bf16[768,256]{1,0:T(8,128)(2,1)} fusion(bf16[512,256]{1,0:T(8,128)(2,1)} %param.4, bf16[256,256]{1,0:T(8,128)(2,1)S(1)} %slice.18), kind=kLoop, calls=%fused_computation.26 | loop fusion | flops 786432 | bytes 786432 | tf_op jit(solution)/shard_map/concatenate | solution.py:89
  8.1 9.4 %all-to-all-start = ((bf16[16,48,256]{2,1,0:T(8,128)(2,1)}), bf16[16,48,256]{2,1,0:T(8,128)(2,1)S(1)}, u32[]{:S(2)}, u32[]{:S(2)}) async-start(bf16[16,48,256]{2,1,0:T(8,128)(2,1)} %bitcast), calls=%async_computation | async-start | bytes 786432 | tf_op jit(solution)/shard_map/all_to_all | solution.py:97
  17.5 0.0 copy-start
  17.5 0.0 copy-done.1
  17.6 0.6 dynamic_slice.23
  18.8 0.8 dynamic-slice_compare_fusion.2
  19.6 0.8 fusion.34
  20.4 1.4 %fusion.17 = f32[512]{0:T(512)S(1)} fusion(pred[512]{0:T(512)(128)(4,1)S(1)} %get-tuple-element.11, f32[512]{0:T(512)S(1)} %get-tuple-element.15, pred[512]{0:T(512)(128)(4,1)S(1)} %get-tuple-element.10, pred[512]{0:T(512)(128)(4,1)S(1)} %get-tuple-element.14, s32[512]{0:T(512)S(1)} %get-tuple-element.16), kind=kLoop, calls=%fused_computation.25 | loop fusion | flops 5897728 | bytes 7680 | tf_op jit(solution)/shard_map/reduce_sum | solution.py:138
  24.4 2.1 %broadcast_divide_fusion.w_ref = f32[512,768]{1,0:T(8,128)} fusion(f32[512]{0:T(512)S(1)} %fusion.17, pred[512]{0:T(512)(128)(4,1)S(1)} %get-tuple-element.11, f32[512]{0:T(512)S(1)} %get-tuple-element.15, pred[512]{0:T(512)(128)(4,1)S(1)} %get-tuple-element.10, pred[512]{0:T(512)(128)(4,1)S(1)} %get-tuple-element.14, s32[512]{0:T(512)S(1)} %get-tuple-element.16), kind=kLoop, calls=%fused_computation.21 | loop fusion | flops 5898240 | bytes 1580544 | tf_op jit(solution)/shard_map/div | solution.py:138
  26.5 0.0 all-to-all-done
  26.5 0.1 select_bitcast_fusion
  26.6 0.8 broadcast_in_dim.86
  27.4 5.7 %all-to-all-start.1 = ((bf16[16,48,256]{2,1,0:T(8,128)(2,1)}), bf16[16,48,256]{2,1,0:T(8,128)(2,1)S(1)}, u32[]{:S(2)}, u32[]{:S(2)}) async-start(bf16[16,48,256]{2,1,0:T(8,128)(2,1)} %broadcast_in_dim.86), calls=%async_computation.1 | async-start | bytes 786432 | tf_op jit(solution)/shard_map/all_to_all | solution.py:104
  33.1 1.2 %fusion.16 = f32[512]{0:T(512)S(1)} fusion(pred[512]{0:T(512)(128)(4,1)S(1)} %get-tuple-element.13, f32[512]{0:T(512)S(1)} %get-tuple-element.5, pred[512]{0:T(512)(128)(4,1)S(1)} %get-tuple-element.12, pred[512]{0:T(512)(128)(4,1)S(1)} %get-tuple-element.9, s32[512]{0:T(512)S(1)} %get-tuple-element.6, s32[512]{0:T(512)S(1)} %get-tuple-element.17), kind=kLoop, calls=%fused_computation.24 | loop fusion | flops 5497344 | bytes 9728 | tf_op jit(solution)/shard_map/reduce_sum | solution.py:126
  34.3 0.0 collective-permute-done
  34.3 0.0 copy-done
  34.3 0.2 multiply_reduce_fusion
  34.5 0.6 pad.23
  35.1 0.1 pad_maximum_fusion.1
  35.2 0.8 pad.21.q_ref
  36.1 2.4 %fusion.10 = f32[1,512]{1,0:T(1,128)S(1)} fusion(f32[767,1]{0,1:T(1,128)S(1)} %reshape.69, f32[512]{0:T(512)S(1)} %fusion.16, f32[512]{0:T(512)S(1)} %get-tuple-element.5, s32[512]{0:T(512)S(1)} %get-tuple-element.6, s32[512]{0:T(512)S(1)} %get-tuple-element.17, pred[512]{0:T(512)(128)(4,1)S(1)} %get-tuple-element.13, ...), kind=kOutput, calls=%fused_computation.14 | convolution fusion | flops 10210304 | bytes 14844 | tf_op jit(solution)/shard_map/dot_general | solution.py:210
  38.5 3.0 %all-to-all-done.1 = bf16[16,48,256]{2,1,0:T(8,128)(2,1)S(1)} async-done(((bf16[16,48,256]{2,1,0:T(8,128)(2,1)}), bf16[16,48,256]{2,1,0:T(8,128)(2,1)S(1)}, u32[]{:S(2)}, u32[]{:S(2)}) %all-to-all-start.1) | async-done | bytes 393248 | tf_op jit(solution)/shard_map/all_to_all | solution.py:104
  41.5 0.2 multiply_reduce_fusion.1
  41.7 0.1 slice.24
  41.8 0.1 reverse
  41.9 0.1 slice.48
  41.9 0.1 pad.22
  42.0 0.9 %broadcast_in_dim.100.rp_ref = f32[768,1]{1,0:T(8,128)} reshape(f32[768]{0:T(1024)S(1)} %pad.22) | data formatting | bytes 6144 | tf_op jit(solution)/shard_map/broadcast_in_dim | solution.py:208
  42.9 1.0 %rev.6 = bf16[767,256]{1,0:T(8,128)(2,1)S(1)} reverse(bf16[767,256]{1,0:T(8,128)(2,1)S(1)} %slice.24), dimensions={0} | reverse | bytes 785408 | tf_op jit(solution)/shard_map/rev | solution.py:203
  43.9 0.8 pad.20.r_ref
  44.8 2.5 %fusion.20 = f32[1,512]{1,0:T(1,128)S(1)} fusion(f32[768,1]{0,1:T(1,128)S(1)} %reshape.71, f32[512]{0:T(512)S(1)} %fusion.17, pred[512]{0:T(512)(128)(4,1)S(1)} %get-tuple-element.11, f32[512]{0:T(512)S(1)} %get-tuple-element.15, pred[512]{0:T(512)(128)(4,1)S(1)} %get-tuple-element.10, pred[512]{0:T(512)(128)(4,1)S(1)} %get-tuple-element.14, ...), kind=kOutput, calls=%fused_computation.31 | convolution fusion | flops 10616832 | bytes 12800 | tf_op jit(solution)/shard_map/dot_general | solution.py:209
  47.3 0.1 reshape.68
  47.4 6.1 %shard_map.46 = f32[512,512]{1,0:T(8,128)} custom-call(bf16[768,256]{1,0:T(8,128)(2,1)} %pad.20.r_ref, bf16[1024,256]{1,0:T(8,128)(2,1)} %pad.21.q_ref, f32[768,1]{1,0:T(8,128)} %broadcast_in_dim.100.rp_ref, f32[1,1024]{1,0:T(1,128)} %bitcast.20, f32[512,768]{1,0:T(8,128)} %broadcast_divide_fusion.w_ref), custom_call_target="tpu_custom_call" | custom-call | flops 1912602624 | bytes 3538944 | tf_op jit(solution)/shard_map/pallas_call | solution.py:169
  53.5 1.4 %select_maximum_fusion = f32[8,72,512]{2,1,0:T(8,128)S(1)} fusion(f32[8,1,64]{2,1,0:T(1,128)S(1)} %reshape.68, f32[8,1,512]{2,1,0:T(1,128)S(1)} %broadcast_in_dim.99, f32[8,64,512]{2,1,0:T(8,128)} %bitcast.17), kind=kLoop, calls=%fused_computation.18 | loop fusion | flops 1179648 | bytes 2246656 | tf_op jit(solution)/shard_map/concatenate | solution.py:216
  54.9 33.3 %all_to_all.15 = f32[8,72,512]{2,1,0:T(8,128)S(1)} all-to-all(f32[8,72,512]{2,1,0:T(8,128)S(1)} %select_maximum_fusion), channel_id=1, replica_groups=mesh['row'=4,'col'=16,'chan'=8] {'chan'}, dimensions={0} | all-to-all | bytes 2359296 | tf_op jit(solution)/shard_map/all_to_all | solution.py:217
  88.1 0.1 reduce_sum.49
  88.3 0.8 fusion.19
  (6 shorter events, 0.0 us)
Async XLA Ops:
  0.0 17.5 %copy-start.1 = (s32[4]{0:T(128)S(1)}, s32[4]{0:T(128)}, u32[]{:S(2)}) copy-start(s32[4]{0:T(128)} %param.5) | copy-start | bytes 52
  1.0 33.4 %collective-permute-start = (bf16[255,256]{1,0:T(8,128)(2,1)S(1)}, bf16[255,256]{1,0:T(8,128)(2,1)S(1)}, u32[]{:S(2)}, u32[]{:S(2)}) collective-permute-start(bf16[255,256]{1,0:T(8,128)(2,1)S(1)} %slice.20), channel_id=1, source_target_pairs={{120,0},{0,8},{8,16},{16,24},{24,32},{32,40},{40,48},{48,56},{56,6... | collective-permute-start | bytes 391688 | tf_op jit(solution)/shard_map/ppermute | solution.py:20
  8.1 18.4 %all-to-all-start = ((bf16[16,48,256]{2,1,0:T(8,128)(2,1)}), bf16[16,48,256]{2,1,0:T(8,128)(2,1)S(1)}, u32[]{:S(2)}, u32[]{:S(2)}) async-start(bf16[16,48,256]{2,1,0:T(8,128)(2,1)} %bitcast), calls=%async_computation | async-start | bytes 786432 | tf_op jit(solution)/shard_map/all_to_all | solution.py:97
  17.5 16.8 %copy-start = (bf16[512,256]{1,0:T(8,128)(2,1)S(1)}, bf16[512,256]{1,0:T(8,128)(2,1)}, u32[]{:S(2)}) copy-start(bf16[512,256]{1,0:T(8,128)(2,1)} %param.4) | copy-start | bytes 786436
  27.4 14.1 %all-to-all-start.1 = ((bf16[16,48,256]{2,1,0:T(8,128)(2,1)}), bf16[16,48,256]{2,1,0:T(8,128)(2,1)S(1)}, u32[]{:S(2)}, u32[]{:S(2)}) async-start(bf16[16,48,256]{2,1,0:T(8,128)(2,1)} %broadcast_in_dim.86), calls=%async_computation.1 | async-start | bytes 786432 | tf_op jit(solution)/shard_map/all_to_all | solution.py:104

commit v6 on v3

--- a/solution.py
+++ b/solution.py
@@ -84,6 +84,18 @@
     return jnp.where(core == 0, jnp.concatenate([mine, other], axis=0), jnp.concatenate([other, mine], axis=0))
 
 
+def broadcast_block(block, source):
+    count = lax.axis_size("col")
+    piece = block.shape[0] // count
+    parts = block.reshape(count, piece, block.shape[1])
+    got = lax.all_to_all(parts, "col", 0, 0, tiled=False)
+    early = lax.dynamic_index_in_dim(got, (source + count - 1) % count, 0, keepdims=False)
+    late = lax.dynamic_index_in_dim(got, source, 0, keepdims=False)
+    pair = jnp.stack([early, late])
+    spread_out = jnp.broadcast_to(pair[None], (count,) + pair.shape)
+    return lax.all_to_all(spread_out, "col", 0, 0, tiled=False)
+
+
 def power_int(frac, exps):
     square = frac * frac
     return jnp.where(
@@ -109,7 +121,7 @@
     rows = lengths.shape[0]
     row_pos = lax.broadcasted_iota(jnp.int32, (rows, depth), 0)
     col_pos = lax.broadcasted_iota(jnp.int32, (rows, depth), 1)
-    lag = row_pos + col_pos - (depth - lags)
+    lag = row_pos + col_pos - (depth - lags) + 1
     span = lengths[:, None]
     valid = (lag >= 0) & (lag < span)
     frac = (span.astype(jnp.float32) - lag.astype(jnp.float32)) / span.astype(jnp.float32)
@@ -117,19 +129,33 @@
     return cone / jnp.sum(cone, axis=1, keepdims=True)
 
 
-def lag_kernel(lags, r_ref, q_ref, rp_ref, cp_ref, w_ref, o_ref):
+def lag_kernel(lags, r_ref, q_ref, cp_ref, csum_ref, w_ref, o_ref):
+    rows = r_ref[...]
+    wide = rows.astype(jnp.float32)
+    square = wide * wide
+    row_norm = jnp.sum(square, axis=1, keepdims=True)
     inner = lax.dot_general(
-        r_ref[...], q_ref[...], (((1,), (1,)), ((), ())), preferred_element_type=jnp.float32
-    )
-    dist = rp_ref[...] + cp_ref[...] - 2.0 * inner
+        rows, q_ref[...], (((1,), (1,)), ((), ())), preferred_element_type=jnp.float32
+    )
+    dist = row_norm + cp_ref[...] - 2.0 * inner
     width = dist.shape[1]
     depth = dist.shape[0]
-    skew = pltpu.roll(dist, width - lags, 1, stride=1, stride_axis=0)
-    block = o_ref.shape[1]
+    skew = pltpu.roll(dist, width - lags + 1, 1, stride=1, stride_axis=0)
+    ones = jnp.ones((8, square.shape[1]), jnp.float32)
+    norm_rows = lax.dot_general(
+        ones, square, (((1,), (1,)), ((), ())), precision=lax.Precision.HIGHEST,
+        preferred_element_type=jnp.float32,
+    )
+    row_sum = lax.dot_general(
+        norm_rows, w_ref[...], (((1,), (1,)), ((), ())), precision=lax.Precision.HIGHEST,
+        preferred_element_type=jnp.float32,
+    )
+    count, share, block = o_ref.shape[0], 64, o_ref.shape[2]
+    share = block // count
     chunk = 128
     band = chunk + lags
     span = block + chunk
-    for m in range(o_ref.shape[0] // chunk):
+    for m in range(block // chunk):
         low = depth - band - chunk * m
         part = jnp.dot(
             w_ref[chunk * m : chunk * (m + 1), low : low + band],
@@ -138,32 +164,46 @@
             preferred_element_type=jnp.float32,
         )
         lined = pltpu.roll(part, span - (chunk - 1), 1, stride=1, stride_axis=0)
-        o_ref[chunk * m : chunk * (m + 1), :] = lined[:, :block]
-
-
-def lag_total(row_rev, col_pad, row_norm, col_norm, weights, block, lags):
+        for h in range(chunk // share):
+            o_ref[(chunk * m) // share + h, 0:share, :] = lined[share * h : share * (h + 1), :block]
+    extra = o_ref.shape[1] - share
+    tail_rows = jnp.concatenate(
+        [csum_ref[...], row_sum[0:1, :], jnp.zeros((extra - 2, block), jnp.float32)], axis=0
+    )
+    for k in range(count):
+        o_ref[k, share:, :] = tail_rows
+
+
+def lag_total(row_rev, col_pad, col_norm, col_sum, weights, count, lags):
     depth = row_rev.shape[0]
     width = col_pad.shape[0]
+    block = weights.shape[0]
+    share = block // count
     flops = 2 * depth * width * row_rev.shape[1] + 6 * 2 * block * (128 + lags) * (block + 128)
     return pl.pallas_call(
         functools.partial(lag_kernel, lags),
-        out_shape=jax.ShapeDtypeStruct((block, block), jnp.float32),
+        out_shape=jax.ShapeDtypeStruct((count, share + 8, block), jnp.float32),
         in_specs=[pl.BlockSpec(memory_space=pltpu.VMEM)] * 5,
         out_specs=pl.BlockSpec(memory_space=pltpu.VMEM),
         cost_estimate=pl.CostEstimate(
             flops=flops, transcendentals=0, bytes_accessed=4 * (block * block + block * depth) + 2 * (depth + width) * 256
         ),
-    )(row_rev, col_pad, row_norm, col_norm, weights)
+    )(row_rev, col_pad, col_norm, col_sum, weights)
 
 
 def shards(snapshots, offsets, window_len, cone_exp):
     block = snapshots.shape[0]
     lags = LAGS
+    count = lax.axis_size("col")
     tail = snapshots[block - (lags - 1) :]
     history = shifted(tail, "col", 1)
     col_ext = jnp.concatenate([history, snapshots], axis=0)
     chosen = lax.dynamic_index_in_dim(offsets, lax.axis_index("row"), 0, keepdims=False)
-    row_ext = broadcast_band(snapshots[block - lags :], snapshots, chosen)[1:]
+    pieces = broadcast_block(snapshots, chosen)
+    piece = block // count
+    band_rows = pieces[:, 1].reshape(block, snapshots.shape[1])
+    tail_rows = pieces[count - lags // piece :, 0].reshape(lags, snapshots.shape[1])
+    row_rev = jnp.concatenate([tail_rows, band_rows], axis=0)[::-1]
     row_begin = chosen * block
     col_begin = lax.axis_index("col") * block
     extent = block + lags
@@ -175,26 +215,18 @@
         lax.dynamic_slice_in_dim(cone_exp, col_begin, block),
         lags,
     )
-    row_wide = row_ext.astype(jnp.float32)
     col_wide = col_ext.astype(jnp.float32)
-    row_part = jnp.sum(row_wide * row_wide, axis=1)
     col_part = jnp.sum(col_wide * col_wide, axis=1)
-    row_rev = jnp.pad(row_ext[::-1], ((extent - row_ext.shape[0], 0), (0, 0)))
-    row_part_rev = jnp.pad(row_part[::-1], (extent - row_ext.shape[0], 0))
     width = 2 * block
     col_pad = jnp.pad(col_ext, ((0, width - col_ext.shape[0]), (0, 0)))
     col_part_pad = jnp.pad(col_part, (0, width - col_ext.shape[0]))
-    total = lag_total(row_rev, col_pad, row_part_rev[:, None], col_part_pad[None, :], row_weights, block, lags)
-    row_sum = jnp.dot(row_weights, row_part_rev, precision=lax.Precision.HIGHEST, preferred_element_type=jnp.float32)
     col_sum = jnp.dot(col_weights, col_part, precision=lax.Precision.HIGHEST, preferred_element_type=jnp.float32)
     n_chan = lax.axis_size("chan")
     share = block // n_chan
-    tiles = total.reshape(n_chan, share, block)
-    col_rows = jnp.broadcast_to(col_sum[None, None, :], (n_chan, 1, block))
-    row_rows = jnp.pad(row_sum.reshape(n_chan, 1, share), ((0, 0), (0, 6), (0, block - share)))
-    payload = jnp.concatenate([tiles, col_rows, row_rows], axis=1).reshape(n_chan * (share + 8), block)
-    mine = lax.psum_scatter(payload, "chan", scatter_dimension=0, tiled=True)
-    row_scale = jnp.sqrt(mine[share + 1, :share] / C + epsilon)
+    payload = lag_total(row_rev, col_pad, col_part_pad[None, :], col_sum[None, :], row_weights, n_chan, lags)
+    mine = jnp.sum(lax.all_to_all(payload, "chan", 0, 0, tiled=False), axis=0)
+    row_sum = lax.dynamic_slice_in_dim(mine[share + 1], lax.axis_index("chan") * share, share)
+    row_scale = jnp.sqrt(row_sum / C + epsilon)
     col_scale = jnp.sqrt(mine[share] / C + epsilon)
     return jnp.exp(-mine[:share] / (2.0 * C * row_scale[:, None] * col_scale[None, :]))
 

time: 133 us -> 89.5 us (0.67)
  the two profiles are of different devices: /device:TPU:2 before, /device:TPU:1 now
where the time goes in v6:
time: 89.5 us; the launch traced here: 88.9 us
  waiting for transfers between devices  35.9 us (40%)
  starting transfers between devices  22.9 us (26%)
  local copies, waits for them, and re-layouts  8.42 us (9%)
  Pallas kernels  7.72 us (9%)
  other arithmetic  7.71 us (9%)
  between operations  3.37 us (4%)
  matrix products  2.97 us (3%)
    all_to_all x1, waiting for transfers between devices, shards(): mine = jnp.sum(lax.all_to_all(payload, 'chan', 0, 0, tiled=False), axis=0)  32 us
    all_to_all x1, starting transfers between devices, broadcast_block(): got = lax.all_to_all(parts, 'col', 0, 0, tiled=False)  10.2 us
    pallas_call x1, Pallas kernels, lag_total(): pl.pallas_call(functools.partial(lag_kernel, lags), out_shape=jax.ShapeDt...  7.72 us
    all_to_all x1, starting transfers between devices, broadcast_block(): return lax.all_to_all(spread_out, 'col', 0, 0, tiled=False)  4.94 us
    all_to_all x1, starting transfers between devices, shards(): mine = jnp.sum(lax.all_to_all(payload, 'chan', 0, 0, tiled=False), axis=0)  4.16 us
    rev x1, local copies, waits for them, and re-layouts, shards(): row_rev = jnp.concatenate([tail_rows, band_rows], axis=0)[::-1]  3.87 us
    all_to_all x1, waiting for transfers between devices, broadcast_block(): return lax.all_to_all(spread_out, 'col', 0, 0, tiled=False)  3.86 us
    ppermute x1, starting transfers between devices, shifted(): return lax.ppermute(block, axis, route)  3.55 us
  transfers between devices with their start and end apart: 4, of which 2 were waited for; matrix products, arithmetic and copies ran while one was open for 16% of the time, Pallas kernels for 0%

profile of v6, /device:TPU:1, one launch (start us, length us, event | category | flops | bytes accessed | tf_op | source)
XLA Modules:
  0.0 88.9 jit_solution(7023498414376768889)
XLA Ops:
  0.0 10.2 %all-to-all-start = ((bf16[16,32,256]{2,1,0:T(8,128)(2,1)}), bf16[16,32,256]{2,1,0:T(8,128)(2,1)S(1)}, u32[]{:S(2)}, u32[]{:S(2)}) async-start(bf16[16,32,256]{2,1,0:T(8,128)(2,1)} %bitcast.10), calls=%async_computation | async-start | bytes 524288 | tf_op jit(solution)/shard_map/all_to_all | solution.py:91
  10.2 1.0 %slice.20 = bf16[255,256]{1,0:T(8,128)(2,1)S(1)} slice(bf16[512,256]{1,0:T(8,128)(2,1)} %param.4), slice={[257:512], [0:256]} | slice | bytes 261120 | tf_op jit(solution)/shard_map/slice | solution.py:198
  11.2 3.5 %collective-permute-start = (bf16[255,256]{1,0:T(8,128)(2,1)S(1)}, bf16[255,256]{1,0:T(8,128)(2,1)S(1)}, u32[]{:S(2)}, u32[]{:S(2)}) collective-permute-start(bf16[255,256]{1,0:T(8,128)(2,1)S(1)} %slice.20), channel_id=1, source_target_pairs={{120,0},{0,8},{8,16},{16,24},{24,32},{32,40},{40,48},{48,56},{56,6... | collective-permute-start | bytes 391688 | tf_op jit(solution)/shard_map/ppermute | solution.py:20
  14.7 1.2 %dynamic_slice.26 = s32[1]{0:T(128)} dynamic-slice(s32[4]{0:T(128)} %param.5, s32[]{:T(128)S(6)} %select_n.57), dynamic_slice_sizes={1} | dynamic-slice | bytes 12 | tf_op jit(solution)/shard_map/jit(dynamic_index_in_dim)/dynamic_slice | solution.py:201
  18.6 0.8 dynamic-slice_compare_fusion.2
  19.4 0.8 fusion.27
  20.9 1.4 %fusion.15 = f32[512]{0:T(512)S(1)} fusion(pred[512]{0:T(512)(128)(4,1)S(1)} %get-tuple-element.17, f32[512]{0:T(512)S(1)} %get-tuple-element.5, pred[512]{0:T(512)(128)(4,1)S(1)} %get-tuple-element.16, pred[512]{0:T(512)(128)(4,1)S(1)} %get-tuple-element.13, s32[512]{0:T(512)S(1)} %get-tuple-element.6), kind=kLoop, calls=%fused_computation.21 | loop fusion | flops 5897728 | bytes 7680 | tf_op jit(solution)/shard_map/reduce_sum | solution.py:129
  22.4 0.0 copy-start
  22.4 2.1 %broadcast_divide_fusion.w_ref = f32[512,768]{1,0:T(8,128)} fusion(f32[512]{0:T(512)S(1)} %fusion.15, pred[512]{0:T(512)(128)(4,1)S(1)} %get-tuple-element.17, f32[512]{0:T(512)S(1)} %get-tuple-element.5, pred[512]{0:T(512)(128)(4,1)S(1)} %get-tuple-element.16, pred[512]{0:T(512)(128)(4,1)S(1)} %get-tuple-element.13, s32[512]{0:T(512)S(1)} %get-tuple-element.6), kind=kLoop, calls=%fused_computation.18 | loop fusion | flops 5898240 | bytes 1580544 | tf_op jit(solution)/shard_map/div | solution.py:129
  24.5 0.0 all-to-all-done
  24.5 0.9 broadcast_in_dim.68
  25.4 4.9 %all-to-all-start.1 = ((bf16[16,2,32,256]{3,2,1,0:T(8,128)(2,1)}), bf16[16,2,32,256]{3,2,1,0:T(8,128)(2,1)S(1)}, u32[]{:S(2)}, u32[]{:S(2)}) async-start(bf16[16,2,32,256]{3,2,1,0:T(8,128)(2,1)} %broadcast_in_dim.68), calls=%async_computation.1 | async-start | bytes 1048576 | tf_op jit(solution)/shard_map/all_to_all | solution.py:96
  30.3 1.2 %fusion.17 = f32[512]{0:T(512)S(1)} fusion(pred[512]{0:T(512)(128)(4,1)S(1)} %get-tuple-element.15, f32[512]{0:T(512)S(1)} %get-tuple-element.19, pred[512]{0:T(512)(128)(4,1)S(1)} %get-tuple-element.14, pred[512]{0:T(512)(128)(4,1)S(1)} %get-tuple-element.18, s32[512]{0:T(512)S(1)} %get-tuple-element.20, s32[512]{0:T(512)S(1)} %get-tuple-element.21), kind=kLoop, calls=%fused_computation.22 | loop fusion | flops 5497344 | bytes 9728 | tf_op jit(solution)/shard_map/reduce_sum | solution.py:117
  31.6 0.0 collective-permute-done
  31.6 0.0 copy-done
  31.6 0.2 multiply_reduce_fusion
  31.8 0.6 pad.9
  32.4 0.1 pad_maximum_fusion.1
  32.4 0.8 pad.8.q_ref
  33.3 3.0 %fusion.10.csum_ref = f32[1,512]{1,0:T(1,128)} fusion(f32[767,1]{0,1:T(1,128)S(1)} %reshape.42, f32[512]{0:T(512)S(1)} %fusion.17, f32[512]{0:T(512)S(1)} %get-tuple-element.19, s32[512]{0:T(512)S(1)} %get-tuple-element.20, s32[512]{0:T(512)S(1)} %get-tuple-element.21, pred[512]{0:T(512)(128)(4,1)S(1)} %get-tuple-element.15, ...), kind=kOutput, calls=%fused_computation.14 | convolution fusion | flops 10210304 | bytes 14844 | tf_op jit(solution)/shard_map/dot_general | solution.py:223
  36.2 3.9 %all-to-all-done.1 = bf16[16,2,32,256]{3,2,1,0:T(8,128)(2,1)S(1)} async-done(((bf16[16,2,32,256]{3,2,1,0:T(8,128)(2,1)}), bf16[16,2,32,256]{3,2,1,0:T(8,128)(2,1)S(1)}, u32[]{:S(2)}, u32[]{:S(2)}) %all-to-all-start.1) | async-done | bytes 524320 | tf_op jit(solution)/shard_map/all_to_all | solution.py:96
  40.2 3.9 %rev.3.r_ref = bf16[768,256]{1,0:T(8,128)(2,1)} reverse(bf16[768,256]{1,0:T(8,128)(2,1)S(1)} %pad_maximum_fusion), dimensions={0} | reverse | bytes 786432 | tf_op jit(solution)/shard_map/rev | solution.py:206
  44.0 7.7 %shard_map.46 = f32[8,72,512]{2,1,0:T(8,128)} custom-call(bf16[768,256]{1,0:T(8,128)(2,1)} %rev.3.r_ref, bf16[1024,256]{1,0:T(8,128)(2,1)} %pad.8.q_ref, f32[1,1024]{1,0:T(1,128)} %bitcast.14, f32[1,512]{1,0:T(1,128)} %fusion.10.csum_ref, f32[512,768]{1,0:T(8,128)} %broadcast_divide_fusion.w_ref), custom_call_target="tpu_custom_call" | custom-call | flops 1912602624 | bytes 3538944 | tf_op jit(solution)/shard_map/pallas_call | solution.py:183
  51.8 4.2 %all-to-all-start.2 = ((f32[8,72,512]{2,1,0:T(8,128)}), f32[8,72,512]{2,1,0:T(8,128)S(1)}, u32[]{:S(2)}, u32[]{:S(2)}) async-start(f32[8,72,512]{2,1,0:T(8,128)} %shard_map.46), calls=%async_computation.2 | async-start | bytes 2359296 | tf_op jit(solution)/shard_map/all_to_all | solution.py:227
  55.9 32.0 %all-to-all-done.2 = f32[8,72,512]{2,1,0:T(8,128)S(1)} async-done(((f32[8,72,512]{2,1,0:T(8,128)}), f32[8,72,512]{2,1,0:T(8,128)S(1)}, u32[]{:S(2)}, u32[]{:S(2)}) %all-to-all-start.2) | async-done | bytes 1179680 | tf_op jit(solution)/shard_map/all_to_all | solution.py:227
  87.9 0.1 reduce_sum.39
  88.0 0.1 multiply_bitcast_fusion
  88.1 0.8 fusion.19
  (7 shorter events, 0.1 us)
Async XLA Ops:
  0.0 24.5 %all-to-all-start = ((bf16[16,32,256]{2,1,0:T(8,128)(2,1)}), bf16[16,32,256]{2,1,0:T(8,128)(2,1)S(1)}, u32[]{:S(2)}, u32[]{:S(2)}) async-start(bf16[16,32,256]{2,1,0:T(8,128)(2,1)} %bitcast.10), calls=%async_computation | async-start | bytes 524288 | tf_op jit(solution)/shard_map/all_to_all | solution.py:91
  11.2 20.4 %collective-permute-start = (bf16[255,256]{1,0:T(8,128)(2,1)S(1)}, bf16[255,256]{1,0:T(8,128)(2,1)S(1)}, u32[]{:S(2)}, u32[]{:S(2)}) collective-permute-start(bf16[255,256]{1,0:T(8,128)(2,1)S(1)} %slice.20), channel_id=1, source_target_pairs={{120,0},{0,8},{8,16},{16,24},{24,32},{32,40},{40,48},{48,56},{56,6... | collective-permute-start | bytes 391688 | tf_op jit(solution)/shard_map/ppermute | solution.py:20
  22.4 9.2 %copy-start = (bf16[512,256]{1,0:T(8,128)(2,1)S(1)}, bf16[512,256]{1,0:T(8,128)(2,1)}, u32[]{:S(2)}) copy-start(bf16[512,256]{1,0:T(8,128)(2,1)} %param.4) | copy-start | bytes 786436
  25.4 14.7 %all-to-all-start.1 = ((bf16[16,2,32,256]{3,2,1,0:T(8,128)(2,1)}), bf16[16,2,32,256]{3,2,1,0:T(8,128)(2,1)S(1)}, u32[]{:S(2)}, u32[]{:S(2)}) async-start(bf16[16,2,32,256]{3,2,1,0:T(8,128)(2,1)} %broadcast_in_dim.68), calls=%async_computation.1 | async-start | bytes 1048576 | tf_op jit(solution)/shard_map/all_to_all | solution.py:96
  51.8 36.2 %all-to-all-start.2 = ((f32[8,72,512]{2,1,0:T(8,128)}), f32[8,72,512]{2,1,0:T(8,128)S(1)}, u32[]{:S(2)}, u32[]{:S(2)}) async-start(f32[8,72,512]{2,1,0:T(8,128)} %shard_map.46), calls=%async_computation.2 | async-start | bytes 2359296 | tf_op jit(solution)/shard_map/all_to_all | solution.py:227

commit v7 on v6

--- a/solution.py
+++ b/solution.py
@@ -91,7 +91,7 @@
     got = lax.all_to_all(parts, "col", 0, 0, tiled=False)
     early = lax.dynamic_index_in_dim(got, (source + count - 1) % count, 0, keepdims=False)
     late = lax.dynamic_index_in_dim(got, source, 0, keepdims=False)
-    pair = jnp.stack([early, late])
+    pair = jnp.stack([early, late])[:, ::-1]
     spread_out = jnp.broadcast_to(pair[None], (count,) + pair.shape)
     return lax.all_to_all(spread_out, "col", 0, 0, tiled=False)
 
@@ -130,7 +130,12 @@
 
 
 def lag_kernel(lags, r_ref, q_ref, cp_ref, csum_ref, w_ref, o_ref):
-    rows = r_ref[...]
+    count = r_ref.shape[0]
+    tail_count = lags // r_ref.shape[2]
+    rows = jnp.concatenate(
+        [r_ref[count - 1 - s, 1] for s in range(count)] + [r_ref[count - 1 - s, 0] for s in range(tail_count)],
+        axis=0,
+    )
     wide = rows.astype(jnp.float32)
     square = wide * wide
     row_norm = jnp.sum(square, axis=1, keepdims=True)
@@ -175,11 +180,11 @@
 
 
 def lag_total(row_rev, col_pad, col_norm, col_sum, weights, count, lags):
-    depth = row_rev.shape[0]
+    depth = weights.shape[1]
     width = col_pad.shape[0]
     block = weights.shape[0]
     share = block // count
-    flops = 2 * depth * width * row_rev.shape[1] + 6 * 2 * block * (128 + lags) * (block + 128)
+    flops = 2 * depth * width * col_pad.shape[1] + 6 * 2 * block * (128 + lags) * (block + 128)
     return pl.pallas_call(
         functools.partial(lag_kernel, lags),
         out_shape=jax.ShapeDtypeStruct((count, share + 8, block), jnp.float32),
@@ -200,10 +205,6 @@
     col_ext = jnp.concatenate([history, snapshots], axis=0)
     chosen = lax.dynamic_index_in_dim(offsets, lax.axis_index("row"), 0, keepdims=False)
     pieces = broadcast_block(snapshots, chosen)
-    piece = block // count
-    band_rows = pieces[:, 1].reshape(block, snapshots.shape[1])
-    tail_rows = pieces[count - lags // piece :, 0].reshape(lags, snapshots.shape[1])
-    row_rev = jnp.concatenate([tail_rows, band_rows], axis=0)[::-1]
     row_begin = chosen * block
     col_begin = lax.axis_index("col") * block
     extent = block + lags
@@ -223,7 +224,7 @@
     col_sum = jnp.dot(col_weights, col_part, precision=lax.Precision.HIGHEST, preferred_element_type=jnp.float32)
     n_chan = lax.axis_size("chan")
     share = block // n_chan
-    payload = lag_total(row_rev, col_pad, col_part_pad[None, :], col_sum[None, :], row_weights, n_chan, lags)
+    payload = lag_total(pieces, col_pad, col_part_pad[None, :], col_sum[None, :], row_weights, n_chan, lags)
     mine = jnp.sum(lax.all_to_all(payload, "chan", 0, 0, tiled=False), axis=0)
     row_sum = lax.dynamic_slice_in_dim(mine[share + 1], lax.axis_index("chan") * share, share)
     row_scale = jnp.sqrt(row_sum / C + epsilon)

time: 89.5 us -> 86.4 us (0.965)
  local copies, waits for them, and re-layouts: 8.42 us -> 5.4 us
    rev x1, local copies, waits for them, and re-layouts: 3.87 us -> 0.09 us  [broadcast_block(): pair = jnp.stack([early, late])[:, ::-1]]
  transfers between devices with their start and end apart: 4 -> 4, of which waited for: 2 -> 2; matrix products, arithmetic and copies ran while one was open for 16% -> 17% of each run, Pallas kernels for 0% -> 0%
where the time goes in v7:
time: 86.4 us; the launch traced here: 85.9 us
  waiting for transfers between devices  35.9 us (42%)
  starting transfers between devices  22.9 us (27%)
  Pallas kernels  7.76 us (9%)
  other arithmetic  7.68 us (9%)
  local copies, waits for them, and re-layouts  5.4 us (6%)
  between operations  3.37 us (4%)
  matrix products  2.98 us (3%)
    all_to_all x1, waiting for transfers between devices, shards(): mine = jnp.sum(lax.all_to_all(payload, 'chan', 0, 0, tiled=False), axis=0)  32 us
    all_to_all x1, starting transfers between devices, broadcast_block(): got = lax.all_to_all(parts, 'col', 0, 0, tiled=False)  10.2 us
    pallas_call x1, Pallas kernels, lag_total(): pl.pallas_call(functools.partial(lag_kernel, lags), out_shape=jax.ShapeDt...  7.76 us
    all_to_all x1, starting transfers between devices, broadcast_block(): return lax.all_to_all(spread_out, 'col', 0, 0, tiled=False)  4.94 us
    all_to_all x1, starting transfers between devices, shards(): mine = jnp.sum(lax.all_to_all(payload, 'chan', 0, 0, tiled=False), axis=0)  4.17 us
    all_to_all x1, waiting for transfers between devices, broadcast_block(): return lax.all_to_all(spread_out, 'col', 0, 0, tiled=False)  3.85 us
    ppermute x1, starting transfers between devices, shifted(): return lax.ppermute(block, axis, route)  3.55 us
    dot_general x1, matrix products, shards(): jnp.dot(col_weights, col_part, precision=lax.Precision.HIGHEST, preferred...  2.98 us
  transfers between devices with their start and end apart: 4, of which 2 were waited for; matrix products, arithmetic and copies ran while one was open for 17% of the time, Pallas kernels for 0%

profile of v7, /device:TPU:1, one launch (start us, length us, event | category | flops | bytes accessed | tf_op | source)
XLA Modules:
  0.0 85.9 jit_solution(2023386647122411560)
XLA Ops:
  0.0 10.2 %all-to-all-start = ((bf16[16,32,256]{2,1,0:T(8,128)(2,1)}), bf16[16,32,256]{2,1,0:T(8,128)(2,1)S(1)}, u32[]{:S(2)}, u32[]{:S(2)}) async-start(bf16[16,32,256]{2,1,0:T(8,128)(2,1)} %bitcast.8), calls=%async_computation | async-start | bytes 524288 | tf_op jit(solution)/shard_map/all_to_all | solution.py:91
  10.2 1.0 %slice.12 = bf16[255,256]{1,0:T(8,128)(2,1)S(1)} slice(bf16[512,256]{1,0:T(8,128)(2,1)} %param.4), slice={[257:512], [0:256]} | slice | bytes 261120 | tf_op jit(solution)/shard_map/slice | solution.py:203
  11.2 3.5 %collective-permute-start = (bf16[255,256]{1,0:T(8,128)(2,1)S(1)}, bf16[255,256]{1,0:T(8,128)(2,1)S(1)}, u32[]{:S(2)}, u32[]{:S(2)}) collective-permute-start(bf16[255,256]{1,0:T(8,128)(2,1)S(1)} %slice.12), channel_id=1, source_target_pairs={{120,0},{0,8},{8,16},{16,24},{24,32},{32,40},{40,48},{48,56},{56,6... | collective-permute-start | bytes 391688 | tf_op jit(solution)/shard_map/ppermute | solution.py:20
  14.7 1.2 %dynamic_slice.26 = s32[1]{0:T(128)} dynamic-slice(s32[4]{0:T(128)} %param.5, s32[]{:T(128)S(6)} %select_n.57), dynamic_slice_sizes={1} | dynamic-slice | bytes 12 | tf_op jit(solution)/shard_map/jit(dynamic_index_in_dim)/dynamic_slice | solution.py:206
  18.6 0.8 dynamic-slice_compare_fusion.2
  19.5 0.8 fusion.27
  21.0 1.4 %fusion.15 = f32[512]{0:T(512)S(1)} fusion(pred[512]{0:T(512)(128)(4,1)S(1)} %get-tuple-element.17, f32[512]{0:T(512)S(1)} %get-tuple-element.5, pred[512]{0:T(512)(128)(4,1)S(1)} %get-tuple-element.16, pred[512]{0:T(512)(128)(4,1)S(1)} %get-tuple-element.13, s32[512]{0:T(512)S(1)} %get-tuple-element.6), kind=kLoop, calls=%fused_computation.21 | loop fusion | flops 5897728 | bytes 7680 | tf_op jit(solution)/shard_map/reduce_sum | solution.py:129
  22.4 0.0 copy-start
  22.4 2.1 %broadcast_divide_fusion.w_ref = f32[512,768]{1,0:T(8,128)} fusion(f32[512]{0:T(512)S(1)} %fusion.15, pred[512]{0:T(512)(128)(4,1)S(1)} %get-tuple-element.17, f32[512]{0:T(512)S(1)} %get-tuple-element.5, pred[512]{0:T(512)(128)(4,1)S(1)} %get-tuple-element.16, pred[512]{0:T(512)(128)(4,1)S(1)} %get-tuple-element.13, s32[512]{0:T(512)S(1)} %get-tuple-element.6), kind=kLoop, calls=%fused_computation.18 | loop fusion | flops 5898240 | bytes 1580544 | tf_op jit(solution)/shard_map/div | solution.py:129
  24.5 0.0 all-to-all-done
  24.5 0.1 rev.3
  24.6 0.9 %broadcast_in_dim.68 = bf16[16,2,32,256]{3,2,1,0:T(8,128)(2,1)} broadcast(bf16[2,32,256]{2,1,0:T(8,128)(2,1)S(1)} %rev.3), dimensions={1,2,3} | broadcast | bytes 557056 | tf_op jit(solution)/shard_map/broadcast_in_dim | solution.py:95
  25.5 4.9 %all-to-all-start.1 = ((bf16[16,2,32,256]{3,2,1,0:T(8,128)(2,1)}), bf16[16,2,32,256]{3,2,1,0:T(8,128)(2,1)S(1)}, u32[]{:S(2)}, u32[]{:S(2)}) async-start(bf16[16,2,32,256]{3,2,1,0:T(8,128)(2,1)} %broadcast_in_dim.68), calls=%async_computation.1 | async-start | bytes 1048576 | tf_op jit(solution)/shard_map/all_to_all | solution.py:96
  30.4 1.2 %fusion.17 = f32[512]{0:T(512)S(1)} fusion(pred[512]{0:T(512)(128)(4,1)S(1)} %get-tuple-element.15, f32[512]{0:T(512)S(1)} %get-tuple-element.19, pred[512]{0:T(512)(128)(4,1)S(1)} %get-tuple-element.14, pred[512]{0:T(512)(128)(4,1)S(1)} %get-tuple-element.18, s32[512]{0:T(512)S(1)} %get-tuple-element.20, s32[512]{0:T(512)S(1)} %iota_add_fusion), kind=kLoop, calls=%fused_computation.22 | loop fusion | flops 5497344 | bytes 9728 | tf_op jit(solution)/shard_map/reduce_sum | solution.py:117
  31.6 0.0 collective-permute-done
  31.7 0.0 copy-done
  31.7 0.2 multiply_reduce_fusion
  31.9 0.6 pad.9
  32.5 0.1 pad_maximum_fusion
  32.5 0.8 pad.8.q_ref
  33.4 3.0 %fusion.10.csum_ref = f32[1,512]{1,0:T(1,128)} fusion(f32[767,1]{0,1:T(1,128)S(1)} %reshape.42, f32[512]{0:T(512)S(1)} %fusion.17, f32[512]{0:T(512)S(1)} %get-tuple-element.19, s32[512]{0:T(512)S(1)} %get-tuple-element.20, s32[512]{0:T(512)S(1)} %iota_add_fusion, pred[512]{0:T(512)(128)(4,1)S(1)} %get-tuple-element.15, ...), kind=kOutput, calls=%fused_computation.14 | convolution fusion | flops 10210304 | bytes 14844 | tf_op jit(solution)/shard_map/dot_general | solution.py:224
  36.3 3.9 %all-to-all-done.1.r_ref = bf16[16,2,32,256]{3,2,1,0:T(8,128)(2,1)S(1)} async-done(((bf16[16,2,32,256]{3,2,1,0:T(8,128)(2,1)}), bf16[16,2,32,256]{3,2,1,0:T(8,128)(2,1)S(1)}, u32[]{:S(2)}, u32[]{:S(2)}) %all-to-all-start.1) | async-done | bytes 524320 | tf_op jit(solution)/shard_map/all_to_all | solution.py:96
  40.2 0.0 copy-start.1
  40.2 0.8 copy-done.1
  41.0 7.8 %shard_map.46 = f32[8,72,512]{2,1,0:T(8,128)} custom-call(bf16[16,2,32,256]{3,2,1,0:T(8,128)(2,1)} %copy-done.1, bf16[1024,256]{1,0:T(8,128)(2,1)} %pad.8.q_ref, f32[1,1024]{1,0:T(1,128)} %bitcast.10, f32[1,512]{1,0:T(1,128)} %fusion.10.csum_ref, f32[512,768]{1,0:T(8,128)} %broadcast_divide_fusion.w_ref), custom_call_target="tpu_custom_call" | custom-call | flops 1912602624 | bytes 3538944 | tf_op jit(solution)/shard_map/pallas_call | solution.py:188
  48.8 4.2 %all-to-all-start.2 = ((f32[8,72,512]{2,1,0:T(8,128)}), f32[8,72,512]{2,1,0:T(8,128)S(1)}, u32[]{:S(2)}, u32[]{:S(2)}) async-start(f32[8,72,512]{2,1,0:T(8,128)} %shard_map.46), calls=%async_computation.2 | async-start | bytes 2359296 | tf_op jit(solution)/shard_map/all_to_all | solution.py:228
  52.9 32.0 %all-to-all-done.2 = f32[8,72,512]{2,1,0:T(8,128)S(1)} async-done(((f32[8,72,512]{2,1,0:T(8,128)}), f32[8,72,512]{2,1,0:T(8,128)S(1)}, u32[]{:S(2)}, u32[]{:S(2)}) %all-to-all-start.2) | async-done | bytes 1179680 | tf_op jit(solution)/shard_map/all_to_all | solution.py:228
  84.9 0.1 reduce_sum.39
  85.0 0.1 multiply_bitcast_fusion
  85.1 0.8 fusion.19
  (5 shorter events, 0.0 us)
Async XLA Ops:
  0.0 24.5 %all-to-all-start = ((bf16[16,32,256]{2,1,0:T(8,128)(2,1)}), bf16[16,32,256]{2,1,0:T(8,128)(2,1)S(1)}, u32[]{:S(2)}, u32[]{:S(2)}) async-start(bf16[16,32,256]{2,1,0:T(8,128)(2,1)} %bitcast.8), calls=%async_computation | async-start | bytes 524288 | tf_op jit(solution)/shard_map/all_to_all | solution.py:91
  11.2 20.5 %collective-permute-start = (bf16[255,256]{1,0:T(8,128)(2,1)S(1)}, bf16[255,256]{1,0:T(8,128)(2,1)S(1)}, u32[]{:S(2)}, u32[]{:S(2)}) collective-permute-start(bf16[255,256]{1,0:T(8,128)(2,1)S(1)} %slice.12), channel_id=1, source_target_pairs={{120,0},{0,8},{8,16},{16,24},{24,32},{32,40},{40,48},{48,56},{56,6... | collective-permute-start | bytes 391688 | tf_op jit(solution)/shard_map/ppermute | solution.py:20
  22.4 9.3 %copy-start = (bf16[512,256]{1,0:T(8,128)(2,1)S(1)}, bf16[512,256]{1,0:T(8,128)(2,1)}, u32[]{:S(2)}) copy-start(bf16[512,256]{1,0:T(8,128)(2,1)} %param.4) | copy-start | bytes 786436
  25.5 14.7 %all-to-all-start.1 = ((bf16[16,2,32,256]{3,2,1,0:T(8,128)(2,1)}), bf16[16,2,32,256]{3,2,1,0:T(8,128)(2,1)S(1)}, u32[]{:S(2)}, u32[]{:S(2)}) async-start(bf16[16,2,32,256]{3,2,1,0:T(8,128)(2,1)} %broadcast_in_dim.68), calls=%async_computation.1 | async-start | bytes 1048576 | tf_op jit(solution)/shard_map/all_to_all | solution.py:96
  40.2 0.8 copy-start.1
  48.8 36.2 %all-to-all-start.2 = ((f32[8,72,512]{2,1,0:T(8,128)}), f32[8,72,512]{2,1,0:T(8,128)S(1)}, u32[]{:S(2)}, u32[]{:S(2)}) async-start(f32[8,72,512]{2,1,0:T(8,128)} %shard_map.46), calls=%async_computation.2 | async-start | bytes 2359296 | tf_op jit(solution)/shard_map/all_to_all | solution.py:228

commit v8 on v7

--- a/solution.py
+++ b/solution.py
@@ -165,7 +165,7 @@
         part = jnp.dot(
             w_ref[chunk * m : chunk * (m + 1), low : low + band],
             skew[low : low + band, low : low + span],
-            precision=lax.Precision.HIGHEST,
+            precision=lax.Precision.HIGH,
             preferred_element_type=jnp.float32,
         )
         lined = pltpu.roll(part, span - (chunk - 1), 1, stride=1, stride_axis=0)

time: 86.4 us -> 85.3 us (0.987)
  Pallas kernels: 7.76 us -> 6.6 us
    pallas_call x1, Pallas kernels: 7.76 us -> 6.6 us  [lag_total(): pl.pallas_call(functools.partial(lag_kernel, lags), out_shape=jax.ShapeDt...]
where the time goes in v8:
time: 85.3 us; the launch traced here: 84.7 us
  waiting for transfers between devices  35.9 us (42%)
  starting transfers between devices  22.9 us (27%)
  other arithmetic  7.68 us (9%)
  Pallas kernels  6.6 us (8%)
  local copies, waits for them, and re-layouts  5.4 us (6%)
  between operations  3.37 us (4%)
  matrix products  2.98 us (3%)
    all_to_all x1, waiting for transfers between devices, shards(): mine = jnp.sum(lax.all_to_all(payload, 'chan', 0, 0, tiled=False), axis=0)  32 us
    all_to_all x1, starting transfers between devices, broadcast_block(): got = lax.all_to_all(parts, 'col', 0, 0, tiled=False)  10.2 us
    pallas_call x1, Pallas kernels, lag_total(): pl.pallas_call(functools.partial(lag_kernel, lags), out_shape=jax.ShapeDt...  6.6 us
    all_to_all x1, starting transfers between devices, broadcast_block(): return lax.all_to_all(spread_out, 'col', 0, 0, tiled=False)  4.94 us
    all_to_all x1, starting transfers between devices, shards(): mine = jnp.sum(lax.all_to_all(payload, 'chan', 0, 0, tiled=False), axis=0)  4.17 us
    all_to_all x1, waiting for transfers between devices, broadcast_block(): return lax.all_to_all(spread_out, 'col', 0, 0, tiled=False)  3.85 us
    ppermute x1, starting transfers between devices, shifted(): return lax.ppermute(block, axis, route)  3.55 us
    dot_general x1, matrix products, shards(): jnp.dot(col_weights, col_part, precision=lax.Precision.HIGHEST, preferred...  2.98 us
  transfers between devices with their start and end apart: 4, of which 2 were waited for; matrix products, arithmetic and copies ran while one was open for 17% of the time, Pallas kernels for 0%

profile of v8, /device:TPU:1, one launch (start us, length us, event | category | flops | bytes accessed | tf_op | source)
XLA Modules:
  0.0 84.7 jit_solution(12254231661680820452)
XLA Ops:
  0.0 10.2 %all-to-all-start = ((bf16[16,32,256]{2,1,0:T(8,128)(2,1)}), bf16[16,32,256]{2,1,0:T(8,128)(2,1)S(1)}, u32[]{:S(2)}, u32[]{:S(2)}) async-start(bf16[16,32,256]{2,1,0:T(8,128)(2,1)} %bitcast.8), calls=%async_computation | async-start | bytes 524288 | tf_op jit(solution)/shard_map/all_to_all | solution.py:91
  10.2 1.0 %slice.12 = bf16[255,256]{1,0:T(8,128)(2,1)S(1)} slice(bf16[512,256]{1,0:T(8,128)(2,1)} %param.4), slice={[257:512], [0:256]} | slice | bytes 261120 | tf_op jit(solution)/shard_map/slice | solution.py:203
  11.2 3.5 %collective-permute-start = (bf16[255,256]{1,0:T(8,128)(2,1)S(1)}, bf16[255,256]{1,0:T(8,128)(2,1)S(1)}, u32[]{:S(2)}, u32[]{:S(2)}) collective-permute-start(bf16[255,256]{1,0:T(8,128)(2,1)S(1)} %slice.12), channel_id=1, source_target_pairs={{120,0},{0,8},{8,16},{16,24},{24,32},{32,40},{40,48},{48,56},{56,6... | collective-permute-start | bytes 391688 | tf_op jit(solution)/shard_map/ppermute | solution.py:20
  14.7 1.2 %dynamic_slice.26 = s32[1]{0:T(128)} dynamic-slice(s32[4]{0:T(128)} %param.5, s32[]{:T(128)S(6)} %select_n.57), dynamic_slice_sizes={1} | dynamic-slice | bytes 12 | tf_op jit(solution)/shard_map/jit(dynamic_index_in_dim)/dynamic_slice | solution.py:206
  18.6 0.8 %dynamic-slice_compare_fusion.2 = (pred[512]{0:T(512)(128)(4,1)S(1)}, pred[512]{0:T(512)(128)(4,1)S(1)}, pred[512]{0:T(512)(128)(4,1)S(1)}, pred[512]{0:T(512)(1...) fusion(s32[8192]{0:T(1024)} %param.7, s32[]{:T(128)S(6)} %select_n.66, s32[]{:T(128)S(6)} %select_n.61), kind=kLoop, calls=%fused_computation.34 | loop fusion | flops 3072 | bytes 7176 | tf_op jit(solution)/shard_map/eq | solution.py:102
  19.5 0.8 fusion.27
  21.0 1.4 %fusion.15 = f32[512]{0:T(512)S(1)} fusion(pred[512]{0:T(512)(128)(4,1)S(1)} %get-tuple-element.17, f32[512]{0:T(512)S(1)} %get-tuple-element.5, pred[512]{0:T(512)(128)(4,1)S(1)} %get-tuple-element.16, pred[512]{0:T(512)(128)(4,1)S(1)} %get-tuple-element.13, s32[512]{0:T(512)S(1)} %get-tuple-element.6), kind=kLoop, calls=%fused_computation.21 | loop fusion | flops 5897728 | bytes 7680 | tf_op jit(solution)/shard_map/reduce_sum | solution.py:129
  22.4 0.0 copy-start
  22.4 2.1 %broadcast_divide_fusion.w_ref = f32[512,768]{1,0:T(8,128)} fusion(f32[512]{0:T(512)S(1)} %fusion.15, pred[512]{0:T(512)(128)(4,1)S(1)} %get-tuple-element.17, f32[512]{0:T(512)S(1)} %get-tuple-element.5, pred[512]{0:T(512)(128)(4,1)S(1)} %get-tuple-element.16, pred[512]{0:T(512)(128)(4,1)S(1)} %get-tuple-element.13, s32[512]{0:T(512)S(1)} %get-tuple-element.6), kind=kLoop, calls=%fused_computation.18 | loop fusion | flops 5898240 | bytes 1580544 | tf_op jit(solution)/shard_map/div | solution.py:129
  24.5 0.0 all-to-all-done
  24.5 0.1 rev.3
  24.6 0.9 %broadcast_in_dim.68 = bf16[16,2,32,256]{3,2,1,0:T(8,128)(2,1)} broadcast(bf16[2,32,256]{2,1,0:T(8,128)(2,1)S(1)} %rev.3), dimensions={1,2,3} | broadcast | bytes 557056 | tf_op jit(solution)/shard_map/broadcast_in_dim | solution.py:95
  25.5 4.9 %all-to-all-start.1 = ((bf16[16,2,32,256]{3,2,1,0:T(8,128)(2,1)}), bf16[16,2,32,256]{3,2,1,0:T(8,128)(2,1)S(1)}, u32[]{:S(2)}, u32[]{:S(2)}) async-start(bf16[16,2,32,256]{3,2,1,0:T(8,128)(2,1)} %broadcast_in_dim.68), calls=%async_computation.1 | async-start | bytes 1048576 | tf_op jit(solution)/shard_map/all_to_all | solution.py:96
  30.4 1.2 %fusion.17 = f32[512]{0:T(512)S(1)} fusion(pred[512]{0:T(512)(128)(4,1)S(1)} %get-tuple-element.15, f32[512]{0:T(512)S(1)} %get-tuple-element.19, pred[512]{0:T(512)(128)(4,1)S(1)} %get-tuple-element.14, pred[512]{0:T(512)(128)(4,1)S(1)} %get-tuple-element.18, s32[512]{0:T(512)S(1)} %get-tuple-element.20, s32[512]{0:T(512)S(1)} %iota_add_fusion), kind=kLoop, calls=%fused_computation.22 | loop fusion | flops 5497344 | bytes 9728 | tf_op jit(solution)/shard_map/reduce_sum | solution.py:117
  31.6 0.0 collective-permute-done
  31.7 0.0 copy-done
  31.7 0.2 multiply_reduce_fusion
  31.9 0.6 pad.9
  32.5 0.1 pad_maximum_fusion
  32.5 0.8 pad.8.q_ref
  33.4 3.0 %fusion.10.csum_ref = f32[1,512]{1,0:T(1,128)} fusion(f32[767,1]{0,1:T(1,128)S(1)} %reshape.42, f32[512]{0:T(512)S(1)} %fusion.17, f32[512]{0:T(512)S(1)} %get-tuple-element.19, s32[512]{0:T(512)S(1)} %get-tuple-element.20, s32[512]{0:T(512)S(1)} %iota_add_fusion, pred[512]{0:T(512)(128)(4,1)S(1)} %get-tuple-element.15, ...), kind=kOutput, calls=%fused_computation.14 | convolution fusion | flops 10210304 | bytes 14844 | tf_op jit(solution)/shard_map/dot_general | solution.py:224
  36.3 3.9 %all-to-all-done.1.r_ref = bf16[16,2,32,256]{3,2,1,0:T(8,128)(2,1)S(1)} async-done(((bf16[16,2,32,256]{3,2,1,0:T(8,128)(2,1)}), bf16[16,2,32,256]{3,2,1,0:T(8,128)(2,1)S(1)}, u32[]{:S(2)}, u32[]{:S(2)}) %all-to-all-start.1) | async-done | bytes 524320 | tf_op jit(solution)/shard_map/all_to_all | solution.py:96
  40.2 0.0 copy-start.1
  40.2 0.8 copy-done.1
  41.0 6.6 %shard_map.46 = f32[8,72,512]{2,1,0:T(8,128)} custom-call(bf16[16,2,32,256]{3,2,1,0:T(8,128)(2,1)} %copy-done.1, bf16[1024,256]{1,0:T(8,128)(2,1)} %pad.8.q_ref, f32[1,1024]{1,0:T(1,128)} %bitcast.10, f32[1,512]{1,0:T(1,128)} %fusion.10.csum_ref, f32[512,768]{1,0:T(8,128)} %broadcast_divide_fusion.w_ref), custom_call_target="tpu_custom_call" | custom-call | flops 1912602624 | bytes 3538944 | tf_op jit(solution)/shard_map/pallas_call | solution.py:188
  47.6 4.2 %all-to-all-start.2 = ((f32[8,72,512]{2,1,0:T(8,128)}), f32[8,72,512]{2,1,0:T(8,128)S(1)}, u32[]{:S(2)}, u32[]{:S(2)}) async-start(f32[8,72,512]{2,1,0:T(8,128)} %shard_map.46), calls=%async_computation.2 | async-start | bytes 2359296 | tf_op jit(solution)/shard_map/all_to_all | solution.py:228
  51.8 32.0 %all-to-all-done.2 = f32[8,72,512]{2,1,0:T(8,128)S(1)} async-done(((f32[8,72,512]{2,1,0:T(8,128)}), f32[8,72,512]{2,1,0:T(8,128)S(1)}, u32[]{:S(2)}, u32[]{:S(2)}) %all-to-all-start.2) | async-done | bytes 1179680 | tf_op jit(solution)/shard_map/all_to_all | solution.py:228
  83.8 0.1 reduce_sum.39
  83.9 0.1 multiply_bitcast_fusion
  84.0 0.8 fusion.19
  (5 shorter events, 0.0 us)
Async XLA Ops:
  0.0 24.5 %all-to-all-start = ((bf16[16,32,256]{2,1,0:T(8,128)(2,1)}), bf16[16,32,256]{2,1,0:T(8,128)(2,1)S(1)}, u32[]{:S(2)}, u32[]{:S(2)}) async-start(bf16[16,32,256]{2,1,0:T(8,128)(2,1)} %bitcast.8), calls=%async_computation | async-start | bytes 524288 | tf_op jit(solution)/shard_map/all_to_all | solution.py:91
  11.2 20.5 %collective-permute-start = (bf16[255,256]{1,0:T(8,128)(2,1)S(1)}, bf16[255,256]{1,0:T(8,128)(2,1)S(1)}, u32[]{:S(2)}, u32[]{:S(2)}) collective-permute-start(bf16[255,256]{1,0:T(8,128)(2,1)S(1)} %slice.12), channel_id=1, source_target_pairs={{120,0},{0,8},{8,16},{16,24},{24,32},{32,40},{40,48},{48,56},{56,6... | collective-permute-start | bytes 391688 | tf_op jit(solution)/shard_map/ppermute | solution.py:20
  22.4 9.3 %copy-start = (bf16[512,256]{1,0:T(8,128)(2,1)S(1)}, bf16[512,256]{1,0:T(8,128)(2,1)}, u32[]{:S(2)}) copy-start(bf16[512,256]{1,0:T(8,128)(2,1)} %param.4) | copy-start | bytes 786436
  25.5 14.7 %all-to-all-start.1 = ((bf16[16,2,32,256]{3,2,1,0:T(8,128)(2,1)}), bf16[16,2,32,256]{3,2,1,0:T(8,128)(2,1)S(1)}, u32[]{:S(2)}, u32[]{:S(2)}) async-start(bf16[16,2,32,256]{3,2,1,0:T(8,128)(2,1)} %broadcast_in_dim.68), calls=%async_computation.1 | async-start | bytes 1048576 | tf_op jit(solution)/shard_map/all_to_all | solution.py:96
  40.2 0.8 copy-start.1
  47.6 36.2 %all-to-all-start.2 = ((f32[8,72,512]{2,1,0:T(8,128)}), f32[8,72,512]{2,1,0:T(8,128)S(1)}, u32[]{:S(2)}, u32[]{:S(2)}) async-start(f32[8,72,512]{2,1,0:T(8,128)} %shard_map.46), calls=%async_computation.2 | async-start | bytes 2359296 | tf_op jit(solution)/shard_map/all_to_all | solution.py:228

commit v9 on v8

--- a/solution.py
+++ b/solution.py
@@ -142,10 +142,16 @@
     inner = lax.dot_general(
         rows, q_ref[...], (((1,), (1,)), ((), ())), preferred_element_type=jnp.float32
     )
-    dist = row_norm + cp_ref[...] - 2.0 * inner
-    width = dist.shape[1]
-    depth = dist.shape[0]
+    depth = inner.shape[0]
+    near = row_norm + cp_ref[...] - 2.0 * inner
+    width = 2 * o_ref.shape[2]
+    dist = jnp.concatenate([near, jnp.zeros((depth, width - near.shape[1]), jnp.float32)], axis=1)
     skew = pltpu.roll(dist, width - lags + 1, 1, stride=1, stride_axis=0)
+    skew_hi = skew.astype(jnp.bfloat16)
+    skew_lo = (skew - skew_hi.astype(jnp.float32)).astype(jnp.bfloat16)
+    weights = w_ref[...]
+    w_hi = weights.astype(jnp.bfloat16)
+    w_lo = (weights - w_hi.astype(jnp.float32)).astype(jnp.bfloat16)
     ones = jnp.ones((8, square.shape[1]), jnp.float32)
     norm_rows = lax.dot_general(
         ones, square, (((1,), (1,)), ((), ())), precision=lax.Precision.HIGHEST,
@@ -162,11 +168,13 @@
     span = block + chunk
     for m in range(block // chunk):
         low = depth - band - chunk * m
-        part = jnp.dot(
-            w_ref[chunk * m : chunk * (m + 1), low : low + band],
-            skew[low : low + band, low : low + span],
-            precision=lax.Precision.HIGH,
-            preferred_element_type=jnp.float32,
+        rows_at = slice(chunk * m, chunk * (m + 1))
+        cols_at = slice(low, low + band)
+        out_at = slice(low, low + span)
+        part = (
+            jnp.dot(w_hi[rows_at, cols_at], skew_hi[cols_at, out_at], preferred_element_type=jnp.float32)
+            + jnp.dot(w_hi[rows_at, cols_at], skew_lo[cols_at, out_at], preferred_element_type=jnp.float32)
+            + jnp.dot(w_lo[rows_at, cols_at], skew_hi[cols_at, out_at], preferred_element_type=jnp.float32)
         )
         lined = pltpu.roll(part, span - (chunk - 1), 1, stride=1, stride_axis=0)
         for h in range(chunk // share):
@@ -218,10 +226,10 @@
     )
     col_wide = col_ext.astype(jnp.float32)
     col_part = jnp.sum(col_wide * col_wide, axis=1)
-    width = 2 * block
-    col_pad = jnp.pad(col_ext, ((0, width - col_ext.shape[0]), (0, 0)))
-    col_part_pad = jnp.pad(col_part, (0, width - col_ext.shape[0]))
-    col_sum = jnp.dot(col_weights, col_part, precision=lax.Precision.HIGHEST, preferred_element_type=jnp.float32)
+    extent_rows = block + lags
+    col_pad = jnp.pad(col_ext, ((0, extent_rows - col_ext.shape[0]), (0, 0)))
+    col_part_pad = jnp.pad(col_part, (0, extent_rows - col_ext.shape[0]))
+    col_sum = jnp.sum(col_weights * col_part[None, :], axis=1)
     n_chan = lax.axis_size("chan")
     share = block // n_chan
     payload = lag_total(pieces, col_pad, col_part_pad[None, :], col_sum[None, :], row_weights, n_chan, lags)

time: 85.3 us -> 85.1 us (level)
  matrix products: 2.98 us -> 0 us
  other arithmetic: 7.68 us -> 9.43 us
  waiting for transfers between devices: 35.9 us -> 37.1 us
    dot_general x1 -> x0, matrix products: 2.98 us -> none  [shards(): jnp.dot(col_weights, col_part, precision=lax.Precision.HIGHEST, preferred...]
    reduce_sum x0 -> x1, other arithmetic: none -> 1.86 us  [shards(): col_sum = jnp.sum(col_weights * col_part[None, :], axis=1)]
    all_to_all x1, waiting for transfers between devices: 3.85 us -> 5.05 us  [broadcast_block(): return lax.all_to_all(spread_out, 'col', 0, 0, tiled=False)]
  transfers between devices with their start and end apart: 4 -> 4, of which waited for: 2 -> 2; matrix products, arithmetic and copies ran while one was open for 17% -> 15% of each run, Pallas kernels for 0% -> 0%
where the time goes in v9:
time: 85.1 us; the launch traced here: 84.6 us
  waiting for transfers between devices  37.1 us (44%)
  starting transfers between devices  23 us (27%)
  other arithmetic  9.43 us (11%)
  Pallas kernels  6.43 us (8%)
  local copies, waits for them, and re-layouts  5.35 us (6%)
  between operations  3.36 us (4%)
    all_to_all x1, waiting for transfers between devices, shards(): mine = jnp.sum(lax.all_to_all(payload, 'chan', 0, 0, tiled=False), axis=0)  32 us
    all_to_all x1, starting transfers between devices, broadcast_block(): got = lax.all_to_all(parts, 'col', 0, 0, tiled=False)  10.2 us
    pallas_call x1, Pallas kernels, lag_total(): pl.pallas_call(functools.partial(lag_kernel, lags), out_shape=jax.ShapeDt...  6.43 us
    all_to_all x1, starting transfers between devices, broadcast_block(): return lax.all_to_all(spread_out, 'col', 0, 0, tiled=False)  5.06 us
    all_to_all x1, waiting for transfers between devices, broadcast_block(): return lax.all_to_all(spread_out, 'col', 0, 0, tiled=False)  5.05 us
    all_to_all x1, starting transfers between devices, shards(): mine = jnp.sum(lax.all_to_all(payload, 'chan', 0, 0, tiled=False), axis=0)  4.16 us
    ppermute x1, starting transfers between devices, shifted(): return lax.ppermute(block, axis, route)  3.55 us
    div x1, other arithmetic, reversed_cone(): return cone / jnp.sum(cone, axis=1, keepdims=True)  2.09 us
  transfers between devices with their start and end apart: 4, of which 2 were waited for; matrix products, arithmetic and copies ran while one was open for 15% of the time, Pallas kernels for 0%

profile of v9, /device:TPU:1, one launch (start us, length us, event | category | flops | bytes accessed | tf_op | source)
XLA Modules:
  0.0 84.6 jit_solution(13870950975255054216)
XLA Ops:
  0.0 10.2 %all-to-all-start = ((bf16[16,32,256]{2,1,0:T(8,128)(2,1)}), bf16[16,32,256]{2,1,0:T(8,128)(2,1)S(1)}, u32[]{:S(2)}, u32[]{:S(2)}) async-start(bf16[16,32,256]{2,1,0:T(8,128)(2,1)} %bitcast.6), calls=%async_computation | async-start | bytes 524288 | tf_op jit(solution)/shard_map/all_to_all | solution.py:91
  10.2 1.0 %slice.12 = bf16[255,256]{1,0:T(8,128)(2,1)S(1)} slice(bf16[512,256]{1,0:T(8,128)(2,1)} %param.4), slice={[257:512], [0:256]} | slice | bytes 261120 | tf_op jit(solution)/shard_map/slice | solution.py:211
  11.2 3.5 %collective-permute-start = (bf16[255,256]{1,0:T(8,128)(2,1)S(1)}, bf16[255,256]{1,0:T(8,128)(2,1)S(1)}, u32[]{:S(2)}, u32[]{:S(2)}) collective-permute-start(bf16[255,256]{1,0:T(8,128)(2,1)S(1)} %slice.12), channel_id=1, source_target_pairs={{120,0},{0,8},{8,16},{16,24},{24,32},{32,40},{40,48},{48,56},{56,6... | collective-permute-start | bytes 391688 | tf_op jit(solution)/shard_map/ppermute | solution.py:20
  14.7 1.2 %dynamic_slice.26 = s32[1]{0:T(128)} dynamic-slice(s32[4]{0:T(128)} %param.5, s32[]{:T(128)S(6)} %select_n.57), dynamic_slice_sizes={1} | dynamic-slice | bytes 12 | tf_op jit(solution)/shard_map/jit(dynamic_index_in_dim)/dynamic_slice | solution.py:214
  18.6 0.8 dynamic-slice_compare_fusion.2
  19.4 0.8 fusion.20
  20.8 1.4 %fusion.12 = f32[512]{0:T(512)S(1)} fusion(pred[512]{0:T(512)(128)(4,1)S(1)} %get-tuple-element.17, f32[512]{0:T(512)S(1)} %get-tuple-element.5, pred[512]{0:T(512)(128)(4,1)S(1)} %get-tuple-element.16, pred[512]{0:T(512)(128)(4,1)S(1)} %get-tuple-element.13, s32[512]{0:T(512)S(1)} %get-tuple-element.6), kind=kLoop, calls=%fused_computation.19 | loop fusion | flops 5897728 | bytes 7680 | tf_op jit(solution)/shard_map/reduce_sum | solution.py:129
  22.3 0.0 copy-start
  22.3 2.1 %broadcast_divide_fusion.w_ref = f32[512,768]{1,0:T(8,128)} fusion(f32[512]{0:T(512)S(1)} %fusion.12, pred[512]{0:T(512)(128)(4,1)S(1)} %get-tuple-element.17, f32[512]{0:T(512)S(1)} %get-tuple-element.5, pred[512]{0:T(512)(128)(4,1)S(1)} %get-tuple-element.16, pred[512]{0:T(512)(128)(4,1)S(1)} %get-tuple-element.13, s32[512]{0:T(512)S(1)} %get-tuple-element.6), kind=kLoop, calls=%fused_computation.17 | loop fusion | flops 5898240 | bytes 1580544 | tf_op jit(solution)/shard_map/div | solution.py:129
  24.4 0.0 all-to-all-done
  24.4 0.1 rev.3
  24.5 0.9 %broadcast_in_dim.69 = bf16[16,2,32,256]{3,2,1,0:T(8,128)(2,1)} broadcast(bf16[2,32,256]{2,1,0:T(8,128)(2,1)S(1)} %rev.3), dimensions={1,2,3} | broadcast | bytes 557056 | tf_op jit(solution)/shard_map/broadcast_in_dim | solution.py:95
  25.3 5.1 %all-to-all-start.1 = ((bf16[16,2,32,256]{3,2,1,0:T(8,128)(2,1)}), bf16[16,2,32,256]{3,2,1,0:T(8,128)(2,1)S(1)}, u32[]{:S(2)}, u32[]{:S(2)}) async-start(bf16[16,2,32,256]{3,2,1,0:T(8,128)(2,1)} %broadcast_in_dim.69), calls=%async_computation.1 | async-start | bytes 1048576 | tf_op jit(solution)/shard_map/all_to_all | solution.py:96
  30.4 1.2 %fusion.13 = f32[512]{0:T(512)S(1)} fusion(pred[512]{0:T(512)(128)(4,1)S(1)} %get-tuple-element.15, f32[512]{0:T(512)S(1)} %get-tuple-element.19, pred[512]{0:T(512)(128)(4,1)S(1)} %get-tuple-element.14, pred[512]{0:T(512)(128)(4,1)S(1)} %get-tuple-element.18, s32[512]{0:T(512)S(1)} %get-tuple-element.20, s32[512]{0:T(512)S(1)} %get-tuple-element.21), kind=kLoop, calls=%fused_computation.20 | loop fusion | flops 5497344 | bytes 9728 | tf_op jit(solution)/shard_map/reduce_sum | solution.py:117
  31.7 0.0 collective-permute-done
  31.7 0.0 copy-done
  31.7 0.2 multiply_reduce_fusion.1
  31.9 0.6 broadcast_in_dim.70.cp_ref
  32.5 0.1 pad_maximum_fusion
  32.5 0.8 pad.8.q_ref
  33.3 1.9 %multiply_reduce_fusion = f32[512]{0:T(512)} fusion(f32[767]{0:T(1024)S(1)} %multiply_reduce_fusion.1, f32[512]{0:T(512)S(1)} %fusion.13, pred[512]{0:T(512)(128)(4,1)S(1)} %get-tuple-element.15, f32[512]{0:T(512)S(1)} %get-tuple-element.19, pred[512]{0:T(512)(128)(4,1)S(1)} %get-tuple-element.14, pred[512]{0:T(512)(128)(4,1)S(1)} %get-tuple-element.18, ...), kind=kLoop, calls=%fused_computation.11 | loop fusion | flops 6282752 | bytes 14844 | tf_op jit(solution)/shard_map/reduce_sum | solution.py:232
  35.2 5.0 %all-to-all-done.1.r_ref = bf16[16,2,32,256]{3,2,1,0:T(8,128)(2,1)S(1)} async-done(((bf16[16,2,32,256]{3,2,1,0:T(8,128)(2,1)}), bf16[16,2,32,256]{3,2,1,0:T(8,128)(2,1)S(1)}, u32[]{:S(2)}, u32[]{:S(2)}) %all-to-all-start.1) | async-done | bytes 524320 | tf_op jit(solution)/shard_map/all_to_all | solution.py:96
  40.2 0.0 copy-start.1
  40.2 0.8 copy-done.1
  41.0 6.4 %shard_map.46 = f32[8,72,512]{2,1,0:T(8,128)} custom-call(bf16[16,2,32,256]{3,2,1,0:T(8,128)(2,1)} %copy-done.1, bf16[768,256]{1,0:T(8,128)(2,1)} %pad.8.q_ref, f32[1,768]{1,0:T(1,128)} %broadcast_in_dim.70.cp_ref, f32[1,512]{1,0:T(1,128)} %bitcast.8, f32[512,768]{1,0:T(8,128)} %broadcast_divide_fusion.w_ref), custom_call_target="tpu_custom_call" | custom-call | flops 1811939328 | bytes 3407872 | tf_op jit(solution)/shard_map/pallas_call | solution.py:196
  47.4 4.2 %all-to-all-start.2 = ((f32[8,72,512]{2,1,0:T(8,128)}), f32[8,72,512]{2,1,0:T(8,128)S(1)}, u32[]{:S(2)}, u32[]{:S(2)}) async-start(f32[8,72,512]{2,1,0:T(8,128)} %shard_map.46), calls=%async_computation.2 | async-start | bytes 2359296 | tf_op jit(solution)/shard_map/all_to_all | solution.py:236
  51.6 32.0 %all-to-all-done.2 = f32[8,72,512]{2,1,0:T(8,128)S(1)} async-done(((f32[8,72,512]{2,1,0:T(8,128)}), f32[8,72,512]{2,1,0:T(8,128)S(1)}, u32[]{:S(2)}, u32[]{:S(2)}) %all-to-all-start.2) | async-done | bytes 1179680 | tf_op jit(solution)/shard_map/all_to_all | solution.py:236
  83.6 0.1 reduce_sum.49
  83.7 0.1 multiply_bitcast_fusion
  83.8 0.8 fusion.15
  (4 shorter events, 0.0 us)
Async XLA Ops:
  0.0 24.4 %all-to-all-start = ((bf16[16,32,256]{2,1,0:T(8,128)(2,1)}), bf16[16,32,256]{2,1,0:T(8,128)(2,1)S(1)}, u32[]{:S(2)}, u32[]{:S(2)}) async-start(bf16[16,32,256]{2,1,0:T(8,128)(2,1)} %bitcast.6), calls=%async_computation | async-start | bytes 524288 | tf_op jit(solution)/shard_map/all_to_all | solution.py:91
  11.2 20.5 %collective-permute-start = (bf16[255,256]{1,0:T(8,128)(2,1)S(1)}, bf16[255,256]{1,0:T(8,128)(2,1)S(1)}, u32[]{:S(2)}, u32[]{:S(2)}) collective-permute-start(bf16[255,256]{1,0:T(8,128)(2,1)S(1)} %slice.12), channel_id=1, source_target_pairs={{120,0},{0,8},{8,16},{16,24},{24,32},{32,40},{40,48},{48,56},{56,6... | collective-permute-start | bytes 391688 | tf_op jit(solution)/shard_map/ppermute | solution.py:20
  22.3 9.4 %copy-start = (bf16[512,256]{1,0:T(8,128)(2,1)S(1)}, bf16[512,256]{1,0:T(8,128)(2,1)}, u32[]{:S(2)}) copy-start(bf16[512,256]{1,0:T(8,128)(2,1)} %param.4) | copy-start | bytes 786436
  25.3 14.9 %all-to-all-start.1 = ((bf16[16,2,32,256]{3,2,1,0:T(8,128)(2,1)}), bf16[16,2,32,256]{3,2,1,0:T(8,128)(2,1)S(1)}, u32[]{:S(2)}, u32[]{:S(2)}) async-start(bf16[16,2,32,256]{3,2,1,0:T(8,128)(2,1)} %broadcast_in_dim.69), calls=%async_computation.1 | async-start | bytes 1048576 | tf_op jit(solution)/shard_map/all_to_all | solution.py:96
  40.2 0.8 copy-start.1
  47.4 36.2 %all-to-all-start.2 = ((f32[8,72,512]{2,1,0:T(8,128)}), f32[8,72,512]{2,1,0:T(8,128)S(1)}, u32[]{:S(2)}, u32[]{:S(2)}) async-start(f32[8,72,512]{2,1,0:T(8,128)} %shard_map.46), calls=%async_computation.2 | async-start | bytes 2359296 | tf_op jit(solution)/shard_map/all_to_all | solution.py:236

commit v10 on v9

--- a/solution.py
+++ b/solution.py
@@ -84,16 +84,17 @@
     return jnp.where(core == 0, jnp.concatenate([mine, other], axis=0), jnp.concatenate([other, mine], axis=0))
 
 
-def broadcast_block(block, source):
+def broadcast_block(block, source, held):
     count = lax.axis_size("col")
     piece = block.shape[0] // count
     parts = block.reshape(count, piece, block.shape[1])
     got = lax.all_to_all(parts, "col", 0, 0, tiled=False)
+    got, held = lax.optimization_barrier((got, held))
     early = lax.dynamic_index_in_dim(got, (source + count - 1) % count, 0, keepdims=False)
     late = lax.dynamic_index_in_dim(got, source, 0, keepdims=False)
     pair = jnp.stack([early, late])[:, ::-1]
     spread_out = jnp.broadcast_to(pair[None], (count,) + pair.shape)
-    return lax.all_to_all(spread_out, "col", 0, 0, tiled=False)
+    return lax.all_to_all(spread_out, "col", 0, 0, tiled=False), held
 
 
 def power_int(frac, exps):
@@ -212,12 +213,14 @@
     history = shifted(tail, "col", 1)
     col_ext = jnp.concatenate([history, snapshots], axis=0)
     chosen = lax.dynamic_index_in_dim(offsets, lax.axis_index("row"), 0, keepdims=False)
-    pieces = broadcast_block(snapshots, chosen)
     row_begin = chosen * block
     col_begin = lax.axis_index("col") * block
     extent = block + lags
-    row_lengths = lax.dynamic_slice_in_dim(window_len, row_begin, block)
-    row_exps = lax.dynamic_slice_in_dim(cone_exp, row_begin, block)
+    pieces, (row_lengths, row_exps) = broadcast_block(
+        snapshots,
+        chosen,
+        (lax.dynamic_slice_in_dim(window_len, row_begin, block), lax.dynamic_slice_in_dim(cone_exp, row_begin, block)),
+    )
     row_weights = reversed_cone(row_lengths, row_exps, lags, extent)
     col_weights = cone_matrix(
         lax.dynamic_slice_in_dim(window_len, col_begin, block),

time: 85.1 us -> 89.1 us (1.047)
  other arithmetic: 9.43 us -> 11.3 us
  waiting for transfers between devices: 37.1 us -> 38.3 us
    all_to_all x1, waiting for transfers between devices: 5.05 us -> 6.25 us  [broadcast_block(): return (lax.all_to_all(spread_out, 'col', 0, 0, tiled=False), held)]
    reduce_sum x1, other arithmetic: 0.18 us -> 1.13 us  [shards(): col_part = jnp.sum(col_wide * col_wide, axis=1)]
    concatenate x1, other arithmetic: 0.06 us -> 1.01 us  [shards(): col_ext = jnp.concatenate([history, snapshots], axis=0)]
  transfers between devices with their start and end apart: 4 -> 4, of which waited for: 2 -> 2; matrix products, arithmetic and copies ran while one was open for 15% -> 17% of each run, Pallas kernels for 0% -> 0%
where the time goes in v10:
time: 89.1 us; the launch traced here: 88.4 us
  waiting for transfers between devices  38.3 us (43%)
  starting transfers between devices  23 us (26%)
  other arithmetic  11.3 us (13%)
  Pallas kernels  6.44 us (7%)
  local copies, waits for them, and re-layouts  6.11 us (7%)
  between operations  3.37 us (4%)
    all_to_all x1, waiting for transfers between devices, shards(): mine = jnp.sum(lax.all_to_all(payload, 'chan', 0, 0, tiled=False), axis=0)  32 us
    all_to_all x1, starting transfers between devices, broadcast_block(): got = lax.all_to_all(parts, 'col', 0, 0, tiled=False)  10.2 us
    pallas_call x1, Pallas kernels, lag_total(): pl.pallas_call(functools.partial(lag_kernel, lags), out_shape=jax.ShapeDt...  6.44 us
    all_to_all x1, waiting for transfers between devices, broadcast_block(): return (lax.all_to_all(spread_out, 'col', 0, 0, tiled=False), held)  6.25 us
    all_to_all x1, starting transfers between devices, broadcast_block(): return (lax.all_to_all(spread_out, 'col', 0, 0, tiled=False), held)  5.06 us
    all_to_all x1, starting transfers between devices, shards(): mine = jnp.sum(lax.all_to_all(payload, 'chan', 0, 0, tiled=False), axis=0)  4.16 us
    ppermute x1, starting transfers between devices, shifted(): return lax.ppermute(block, axis, route)  3.55 us
    div x1, other arithmetic, reversed_cone(): return cone / jnp.sum(cone, axis=1, keepdims=True)  2.09 us
  transfers between devices with their start and end apart: 4, of which 2 were waited for; matrix products, arithmetic and copies ran while one was open for 17% of the time, Pallas kernels for 0%

profile of v10, /device:TPU:1, one launch (start us, length us, event | category | flops | bytes accessed | tf_op | source)
XLA Modules:
  0.0 88.4 jit_solution(8746782208263895952)
XLA Ops:
  0.0 10.2 %all-to-all-start = ((bf16[16,32,256]{2,1,0:T(8,128)(2,1)}), bf16[16,32,256]{2,1,0:T(8,128)(2,1)S(1)}, u32[]{:S(2)}, u32[]{:S(2)}) async-start(bf16[16,32,256]{2,1,0:T(8,128)(2,1)} %bitcast.6), calls=%async_computation | async-start | bytes 524288 | tf_op jit(solution)/shard_map/all_to_all | solution.py:91
  10.2 1.0 %slice.12 = bf16[255,256]{1,0:T(8,128)(2,1)S(1)} slice(bf16[512,256]{1,0:T(8,128)(2,1)} %param.4), slice={[257:512], [0:256]} | slice | bytes 261120 | tf_op jit(solution)/shard_map/slice | solution.py:212
  11.2 3.5 %collective-permute-start = (bf16[255,256]{1,0:T(8,128)(2,1)S(1)}, bf16[255,256]{1,0:T(8,128)(2,1)S(1)}, u32[]{:S(2)}, u32[]{:S(2)}) collective-permute-start(bf16[255,256]{1,0:T(8,128)(2,1)S(1)} %slice.12), channel_id=1, source_target_pairs={{120,0},{0,8},{8,16},{16,24},{24,32},{32,40},{40,48},{48,56},{56,6... | collective-permute-start | bytes 391688 | tf_op jit(solution)/shard_map/ppermute | solution.py:20
  14.7 1.2 %dynamic_slice.26 = s32[1]{0:T(128)} dynamic-slice(s32[4]{0:T(128)} %param.5, s32[]{:T(128)S(6)} %select_n.57), dynamic_slice_sizes={1} | dynamic-slice | bytes 12 | tf_op jit(solution)/shard_map/jit(dynamic_index_in_dim)/dynamic_slice | solution.py:215
  16.6 0.8 dynamic-slice_compare_fusion.2
  17.4 0.8 fusion.20
  18.2 1.2 %fusion.13 = f32[512]{0:T(512)S(1)} fusion(pred[512]{0:T(512)(128)(4,1)S(1)} %get-tuple-element.19, f32[512]{0:T(512)S(1)} %get-tuple-element.11, pred[512]{0:T(512)(128)(4,1)S(1)} %get-tuple-element.18, pred[512]{0:T(512)(128)(4,1)S(1)} %get-tuple-element.17, s32[512]{0:T(512)S(1)} %get-tuple-element.12, s32[512]{0:T(512)S(1)} %iota_add_fusion), kind=kLoop, calls=%fused_computation.20 | loop fusion | flops 5497344 | bytes 9728 | tf_op jit(solution)/shard_map/reduce_sum | solution.py:118
  21.4 0.8 dynamic_slice.28
  22.8 0.0 collective-permute-done
  22.8 1.1 %multiply_reduce_fusion.1 = f32[767]{0:T(1024)S(1)} fusion(bf16[512,256]{1,0:T(8,128)(2,1)} %param.4, bf16[255,256]{1,0:T(8,128)(2,1)S(1)} %collective-permute-done), kind=kLoop, calls=%fused_computation.18 | loop fusion | flops 1177345 | bytes 395772 | tf_op jit(solution)/shard_map/reduce_sum | solution.py:231
  24.0 0.6 broadcast_in_dim.70.cp_ref
  24.6 1.0 %pad_maximum_fusion = bf16[767,256]{1,0:T(8,128)(2,1)S(1)} fusion(bf16[512,256]{1,0:T(8,128)(2,1)} %param.4, bf16[255,256]{1,0:T(8,128)(2,1)S(1)} %collective-permute-done), kind=kLoop, calls=%fused_computation.21 | loop fusion | flops 785408 | bytes 785408 | tf_op jit(solution)/shard_map/concatenate | solution.py:214
  25.6 0.8 pad.8.q_ref
  26.4 1.9 %multiply_reduce_fusion = f32[512]{0:T(512)} fusion(f32[767]{0:T(1024)S(1)} %multiply_reduce_fusion.1, f32[512]{0:T(512)S(1)} %fusion.13, pred[512]{0:T(512)(128)(4,1)S(1)} %get-tuple-element.19, f32[512]{0:T(512)S(1)} %get-tuple-element.11, pred[512]{0:T(512)(128)(4,1)S(1)} %get-tuple-element.18, pred[512]{0:T(512)(128)(4,1)S(1)} %get-tuple-element.17, ...), kind=kLoop, calls=%fused_computation.11 | loop fusion | flops 6282752 | bytes 14844 | tf_op jit(solution)/shard_map/reduce_sum | solution.py:235
  28.2 0.0 all-to-all-done
  28.2 0.1 rev.3
  28.3 0.9 broadcast_in_dim.69
  29.2 5.1 %all-to-all-start.1 = ((bf16[16,2,32,256]{3,2,1,0:T(8,128)(2,1)}), bf16[16,2,32,256]{3,2,1,0:T(8,128)(2,1)S(1)}, u32[]{:S(2)}, u32[]{:S(2)}) async-start(bf16[16,2,32,256]{3,2,1,0:T(8,128)(2,1)} %broadcast_in_dim.69), calls=%async_computation.1 | async-start | bytes 1048576 | tf_op jit(solution)/shard_map/all_to_all | solution.py:97
  34.3 1.4 %fusion.12 = f32[512]{0:T(512)S(1)} fusion(pred[512]{0:T(512)(128)(4,1)S(1)} %get-tuple-element.22, f32[512]{0:T(512)S(1)} %convert_element_type.26, pred[512]{0:T(512)(128)(4,1)S(1)} %get-tuple-element.23, pred[512]{0:T(512)(128)(4,1)S(1)} %get-tuple-element.21, s32[512]{0:T(512)S(1)} %get-tuple-element.9), kind=kLoop, calls=%fused_computation.19 | loop fusion | flops 5897728 | bytes 7680 | tf_op jit(solution)/shard_map/reduce_sum | solution.py:130
  35.7 2.1 %broadcast_divide_fusion.w_ref = f32[512,768]{1,0:T(8,128)} fusion(f32[512]{0:T(512)S(1)} %fusion.12, pred[512]{0:T(512)(128)(4,1)S(1)} %get-tuple-element.22, f32[512]{0:T(512)S(1)} %convert_element_type.26, pred[512]{0:T(512)(128)(4,1)S(1)} %get-tuple-element.23, pred[512]{0:T(512)(128)(4,1)S(1)} %get-tuple-element.21, s32[512]{0:T(512)S(1)} %get-tuple-element.9), kind=kLoop, calls=%fused_computation.17 | loop fusion | flops 5898240 | bytes 1580544 | tf_op jit(solution)/shard_map/div | solution.py:130
  37.8 6.2 %all-to-all-done.1.r_ref = bf16[16,2,32,256]{3,2,1,0:T(8,128)(2,1)S(1)} async-done(((bf16[16,2,32,256]{3,2,1,0:T(8,128)(2,1)}), bf16[16,2,32,256]{3,2,1,0:T(8,128)(2,1)S(1)}, u32[]{:S(2)}, u32[]{:S(2)}) %all-to-all-start.1) | async-done | bytes 524320 | tf_op jit(solution)/shard_map/all_to_all | solution.py:97
  44.1 0.0 copy-start
  44.1 0.8 copy-done
  44.9 6.4 %shard_map.46 = f32[8,72,512]{2,1,0:T(8,128)} custom-call(bf16[16,2,32,256]{3,2,1,0:T(8,128)(2,1)} %copy-done, bf16[768,256]{1,0:T(8,128)(2,1)} %pad.8.q_ref, f32[1,768]{1,0:T(1,128)} %broadcast_in_dim.70.cp_ref, f32[1,512]{1,0:T(1,128)} %bitcast.8, f32[512,768]{1,0:T(8,128)} %broadcast_divide_fusion.w_ref), custom_call_target="tpu_custom_call" | custom-call | flops 1811939328 | bytes 3407872 | tf_op jit(solution)/shard_map/pallas_call | solution.py:197
  51.3 4.2 %all-to-all-start.2 = ((f32[8,72,512]{2,1,0:T(8,128)}), f32[8,72,512]{2,1,0:T(8,128)S(1)}, u32[]{:S(2)}, u32[]{:S(2)}) async-start(f32[8,72,512]{2,1,0:T(8,128)} %shard_map.46), calls=%async_computation.2 | async-start | bytes 2359296 | tf_op jit(solution)/shard_map/all_to_all | solution.py:239
  55.5 32.0 %all-to-all-done.2 = f32[8,72,512]{2,1,0:T(8,128)S(1)} async-done(((f32[8,72,512]{2,1,0:T(8,128)}), f32[8,72,512]{2,1,0:T(8,128)S(1)}, u32[]{:S(2)}, u32[]{:S(2)}) %all-to-all-start.2) | async-done | bytes 1179680 | tf_op jit(solution)/shard_map/all_to_all | solution.py:239
  87.5 0.1 reduce_sum.49
  87.6 0.1 multiply_bitcast_fusion
  87.7 0.8 fusion.15
  (7 shorter events, 0.0 us)
Async XLA Ops:
  0.0 28.2 %all-to-all-start = ((bf16[16,32,256]{2,1,0:T(8,128)(2,1)}), bf16[16,32,256]{2,1,0:T(8,128)(2,1)S(1)}, u32[]{:S(2)}, u32[]{:S(2)}) async-start(bf16[16,32,256]{2,1,0:T(8,128)(2,1)} %bitcast.6), calls=%async_computation | async-start | bytes 524288 | tf_op jit(solution)/shard_map/all_to_all | solution.py:91
  11.2 11.6 %collective-permute-start = (bf16[255,256]{1,0:T(8,128)(2,1)S(1)}, bf16[255,256]{1,0:T(8,128)(2,1)S(1)}, u32[]{:S(2)}, u32[]{:S(2)}) collective-permute-start(bf16[255,256]{1,0:T(8,128)(2,1)S(1)} %slice.12), channel_id=1, source_target_pairs={{120,0},{0,8},{8,16},{16,24},{24,32},{32,40},{40,48},{48,56},{56,6... | collective-permute-start | bytes 391688 | tf_op jit(solution)/shard_map/ppermute | solution.py:20
  29.2 14.9 %all-to-all-start.1 = ((bf16[16,2,32,256]{3,2,1,0:T(8,128)(2,1)}), bf16[16,2,32,256]{3,2,1,0:T(8,128)(2,1)S(1)}, u32[]{:S(2)}, u32[]{:S(2)}) async-start(bf16[16,2,32,256]{3,2,1,0:T(8,128)(2,1)} %broadcast_in_dim.69), calls=%async_computation.1 | async-start | bytes 1048576 | tf_op jit(solution)/shard_map/all_to_all | solution.py:97
  44.1 0.8 copy-start
  51.3 36.2 %all-to-all-start.2 = ((f32[8,72,512]{2,1,0:T(8,128)}), f32[8,72,512]{2,1,0:T(8,128)S(1)}, u32[]{:S(2)}, u32[]{:S(2)}) async-start(f32[8,72,512]{2,1,0:T(8,128)} %shard_map.46), calls=%async_computation.2 | async-start | bytes 2359296 | tf_op jit(solution)/shard_map/all_to_all | solution.py:239

commit v11 on v9

--- a/solution.py
+++ b/solution.py
@@ -89,7 +89,7 @@
     piece = block.shape[0] // count
     parts = block.reshape(count, piece, block.shape[1])
     got = lax.all_to_all(parts, "col", 0, 0, tiled=False)
-    early = lax.dynamic_index_in_dim(got, (source + count - 1) % count, 0, keepdims=False)
+    early = lax.dynamic_index_in_dim(got, lax.rem(source + count - 1, count), 0, keepdims=False)
     late = lax.dynamic_index_in_dim(got, source, 0, keepdims=False)
     pair = jnp.stack([early, late])[:, ::-1]
     spread_out = jnp.broadcast_to(pair[None], (count,) + pair.shape)
@@ -146,7 +146,7 @@
     near = row_norm + cp_ref[...] - 2.0 * inner
     width = 2 * o_ref.shape[2]
     dist = jnp.concatenate([near, jnp.zeros((depth, width - near.shape[1]), jnp.float32)], axis=1)
-    skew = pltpu.roll(dist, width - lags + 1, 1, stride=1, stride_axis=0)
+    skew = pltpu.roll(dist, width - lags, 1, stride=1, stride_axis=0)
     skew_hi = skew.astype(jnp.bfloat16)
     skew_lo = (skew - skew_hi.astype(jnp.float32)).astype(jnp.bfloat16)
     weights = w_ref[...]
@@ -207,8 +207,7 @@
 def shards(snapshots, offsets, window_len, cone_exp):
     block = snapshots.shape[0]
     lags = LAGS
-    count = lax.axis_size("col")
-    tail = snapshots[block - (lags - 1) :]
+    tail = snapshots[block - lags :]
     history = shifted(tail, "col", 1)
     col_ext = jnp.concatenate([history, snapshots], axis=0)
     chosen = lax.dynamic_index_in_dim(offsets, lax.axis_index("row"), 0, keepdims=False)
@@ -222,17 +221,14 @@
     col_weights = cone_matrix(
         lax.dynamic_slice_in_dim(window_len, col_begin, block),
         lax.dynamic_slice_in_dim(cone_exp, col_begin, block),
-        lags,
+        lags + 1,
     )
     col_wide = col_ext.astype(jnp.float32)
     col_part = jnp.sum(col_wide * col_wide, axis=1)
-    extent_rows = block + lags
-    col_pad = jnp.pad(col_ext, ((0, extent_rows - col_ext.shape[0]), (0, 0)))
-    col_part_pad = jnp.pad(col_part, (0, extent_rows - col_ext.shape[0]))
     col_sum = jnp.sum(col_weights * col_part[None, :], axis=1)
     n_chan = lax.axis_size("chan")
     share = block // n_chan
-    payload = lag_total(pieces, col_pad, col_part_pad[None, :], col_sum[None, :], row_weights, n_chan, lags)
+    payload = lag_total(pieces, col_ext, col_part[None, :], col_sum[None, :], row_weights, n_chan, lags)
     mine = jnp.sum(lax.all_to_all(payload, "chan", 0, 0, tiled=False), axis=0)
     row_sum = lax.dynamic_slice_in_dim(mine[share + 1], lax.axis_index("chan") * share, share)
     row_scale = jnp.sqrt(row_sum / C + epsilon)

time: 85.1 us -> 85.1 us (level)
  transfers between devices with their start and end apart: 4 -> 4, of which waited for: 2 -> 2; matrix products, arithmetic and copies ran while one was open for 15% -> 14% of each run, Pallas kernels for 0% -> 0%
where the time goes in v11:
time: 85.1 us; the launch traced here: 84.6 us
  waiting for transfers between devices  37.9 us (45%)
  starting transfers between devices  23 us (27%)
  other arithmetic  9.31 us (11%)
  Pallas kernels  6.44 us (8%)
  local copies, waits for them, and re-layouts  4.57 us (5%)
  between operations  3.37 us (4%)
    all_to_all x1, waiting for transfers between devices, shards(): mine = jnp.sum(lax.all_to_all(payload, 'chan', 0, 0, tiled=False), axis=0)  32 us
    all_to_all x1, starting transfers between devices, broadcast_block(): got = lax.all_to_all(parts, 'col', 0, 0, tiled=False)  10.2 us
    pallas_call x1, Pallas kernels, lag_total(): pl.pallas_call(functools.partial(lag_kernel, lags), out_shape=jax.ShapeDt...  6.44 us
    all_to_all x1, waiting for transfers between devices, broadcast_block(): return lax.all_to_all(spread_out, 'col', 0, 0, tiled=False)  5.9 us
    all_to_all x1, starting transfers between devices, broadcast_block(): return lax.all_to_all(spread_out, 'col', 0, 0, tiled=False)  5.06 us
    all_to_all x1, starting transfers between devices, shards(): mine = jnp.sum(lax.all_to_all(payload, 'chan', 0, 0, tiled=False), axis=0)  4.16 us
    ppermute x1, starting transfers between devices, shifted(): return lax.ppermute(block, axis, route)  3.55 us
    div x1, other arithmetic, reversed_cone(): return cone / jnp.sum(cone, axis=1, keepdims=True)  2.09 us
  transfers between devices with their start and end apart: 4, of which 2 were waited for; matrix products, arithmetic and copies ran while one was open for 14% of the time, Pallas kernels for 0%

profile of v11, /device:TPU:1, one launch (start us, length us, event | category | flops | bytes accessed | tf_op | source)
XLA Modules:
  0.0 84.6 jit_solution(1315720190676612811)
XLA Ops:
  0.0 10.2 %all-to-all-start = ((bf16[16,32,256]{2,1,0:T(8,128)(2,1)}), bf16[16,32,256]{2,1,0:T(8,128)(2,1)S(1)}, u32[]{:S(2)}, u32[]{:S(2)}) async-start(bf16[16,32,256]{2,1,0:T(8,128)(2,1)} %bitcast.6), calls=%async_computation | async-start | bytes 524288 | tf_op jit(solution)/shard_map/all_to_all | solution.py:91
  10.2 0.9 %slice.12 = bf16[256,256]{1,0:T(8,128)(2,1)S(1)} slice(bf16[512,256]{1,0:T(8,128)(2,1)} %param.4), slice={[256:512], [0:256]} | slice | bytes 262144 | tf_op jit(solution)/shard_map/slice | solution.py:210
  11.1 3.5 %collective-permute-start = (bf16[256,256]{1,0:T(8,128)(2,1)S(1)}, bf16[256,256]{1,0:T(8,128)(2,1)S(1)}, u32[]{:S(2)}, u32[]{:S(2)}) collective-permute-start(bf16[256,256]{1,0:T(8,128)(2,1)S(1)} %slice.12), channel_id=1, source_target_pairs={{120,0},{0,8},{8,16},{16,24},{24,32},{32,40},{40,48},{48,56},{56,6... | collective-permute-start | bytes 393224 | tf_op jit(solution)/shard_map/ppermute | solution.py:20
  14.7 1.2 %dynamic_slice.26 = s32[1]{0:T(128)} dynamic-slice(s32[4]{0:T(128)} %param.5, s32[]{:T(128)S(6)} %select_n.48), dynamic_slice_sizes={1} | dynamic-slice | bytes 12 | tf_op jit(solution)/shard_map/jit(dynamic_index_in_dim)/dynamic_slice | solution.py:213
  18.6 0.8 dynamic-slice_compare_fusion.2
  19.3 0.8 fusion.20
  20.8 1.4 %fusion.12 = f32[512]{0:T(512)S(1)} fusion(pred[512]{0:T(512)(128)(4,1)S(1)} %get-tuple-element.17, f32[512]{0:T(512)S(1)} %get-tuple-element.5, pred[512]{0:T(512)(128)(4,1)S(1)} %get-tuple-element.16, pred[512]{0:T(512)(128)(4,1)S(1)} %get-tuple-element.13, s32[512]{0:T(512)S(1)} %get-tuple-element.6), kind=kLoop, calls=%fused_computation.19 | loop fusion | flops 5897728 | bytes 7680 | tf_op jit(solution)/shard_map/reduce_sum | solution.py:129
  22.2 0.0 copy-start
  22.2 2.1 %broadcast_divide_fusion.w_ref = f32[512,768]{1,0:T(8,128)} fusion(f32[512]{0:T(512)S(1)} %fusion.12, pred[512]{0:T(512)(128)(4,1)S(1)} %get-tuple-element.17, f32[512]{0:T(512)S(1)} %get-tuple-element.5, pred[512]{0:T(512)(128)(4,1)S(1)} %get-tuple-element.16, pred[512]{0:T(512)(128)(4,1)S(1)} %get-tuple-element.13, s32[512]{0:T(512)S(1)} %get-tuple-element.6), kind=kLoop, calls=%fused_computation.17 | loop fusion | flops 5898240 | bytes 1580544 | tf_op jit(solution)/shard_map/div | solution.py:129
  24.3 0.0 all-to-all-done
  24.3 0.1 rev.3
  24.4 0.9 %broadcast_in_dim.54 = bf16[16,2,32,256]{3,2,1,0:T(8,128)(2,1)} broadcast(bf16[2,32,256]{2,1,0:T(8,128)(2,1)S(1)} %rev.3), dimensions={1,2,3} | broadcast | bytes 557056 | tf_op jit(solution)/shard_map/broadcast_in_dim | solution.py:95
  25.3 5.1 %all-to-all-start.1 = ((bf16[16,2,32,256]{3,2,1,0:T(8,128)(2,1)}), bf16[16,2,32,256]{3,2,1,0:T(8,128)(2,1)S(1)}, u32[]{:S(2)}, u32[]{:S(2)}) async-start(bf16[16,2,32,256]{3,2,1,0:T(8,128)(2,1)} %broadcast_in_dim.54), calls=%async_computation.1 | async-start | bytes 1048576 | tf_op jit(solution)/shard_map/all_to_all | solution.py:96
  30.4 1.2 %fusion.13 = f32[512]{0:T(512)S(1)} fusion(pred[512]{0:T(512)(128)(4,1)S(1)} %get-tuple-element.15, f32[512]{0:T(512)S(1)} %get-tuple-element.19, pred[512]{0:T(512)(128)(4,1)S(1)} %get-tuple-element.14, pred[512]{0:T(512)(128)(4,1)S(1)} %get-tuple-element.18, s32[512]{0:T(512)S(1)} %get-tuple-element.20, s32[512]{0:T(512)S(1)} %get-tuple-element.21), kind=kLoop, calls=%fused_computation.20 | loop fusion | flops 5504512 | bytes 9728 | tf_op jit(solution)/shard_map/reduce_sum | solution.py:117
  31.6 0.0 collective-permute-done
  31.6 0.0 copy-done
  31.7 0.0 copy-start.1
  31.7 0.2 multiply_reduce_fusion.1
  31.8 0.6 broadcast_in_dim.55.cp_ref
  32.4 1.8 %multiply_reduce_fusion = f32[512]{0:T(512)} fusion(f32[768]{0:T(1024)S(1)} %multiply_reduce_fusion.1, f32[512]{0:T(512)S(1)} %fusion.13, pred[512]{0:T(512)(128)(4,1)S(1)} %get-tuple-element.15, f32[512]{0:T(512)S(1)} %get-tuple-element.19, pred[512]{0:T(512)(128)(4,1)S(1)} %get-tuple-element.14, pred[512]{0:T(512)(128)(4,1)S(1)} %get-tuple-element.18, ...), kind=kLoop, calls=%fused_computation.11 | loop fusion | flops 6290944 | bytes 14848 | tf_op jit(solution)/shard_map/reduce_sum | solution.py:228
  34.3 5.9 %all-to-all-done.1.r_ref = bf16[16,2,32,256]{3,2,1,0:T(8,128)(2,1)S(1)} async-done(((bf16[16,2,32,256]{3,2,1,0:T(8,128)(2,1)}), bf16[16,2,32,256]{3,2,1,0:T(8,128)(2,1)S(1)}, u32[]{:S(2)}, u32[]{:S(2)}) %all-to-all-start.1) | async-done | bytes 524320 | tf_op jit(solution)/shard_map/all_to_all | solution.py:96
  40.2 0.0 copy-start.2
  40.2 0.0 copy-done.1
  40.2 0.8 copy-done.2
  41.0 6.4 %shard_map.46 = f32[8,72,512]{2,1,0:T(8,128)} custom-call(bf16[16,2,32,256]{3,2,1,0:T(8,128)(2,1)} %copy-done.2, bf16[768,256]{1,0:T(8,128)(2,1)} %copy-done.1, f32[1,768]{1,0:T(1,128)} %broadcast_in_dim.55.cp_ref, f32[1,512]{1,0:T(1,128)} %bitcast.8, f32[512,768]{1,0:T(8,128)} %broadcast_divide_fusion.w_ref), custom_call_target="tpu_custom_call" | custom-call | flops 1811939328 | bytes 3407872 | tf_op jit(solution)/shard_map/pallas_call | solution.py:196
  47.4 4.2 %all-to-all-start.2 = ((f32[8,72,512]{2,1,0:T(8,128)}), f32[8,72,512]{2,1,0:T(8,128)S(1)}, u32[]{:S(2)}, u32[]{:S(2)}) async-start(f32[8,72,512]{2,1,0:T(8,128)} %shard_map.46), calls=%async_computation.2 | async-start | bytes 2359296 | tf_op jit(solution)/shard_map/all_to_all | solution.py:232
  51.6 32.0 %all-to-all-done.2 = f32[8,72,512]{2,1,0:T(8,128)S(1)} async-done(((f32[8,72,512]{2,1,0:T(8,128)}), f32[8,72,512]{2,1,0:T(8,128)S(1)}, u32[]{:S(2)}, u32[]{:S(2)}) %all-to-all-start.2) | async-done | bytes 1179680 | tf_op jit(solution)/shard_map/all_to_all | solution.py:232
  83.6 0.1 reduce_sum.49
  83.7 0.1 multiply_bitcast_fusion
  83.8 0.8 fusion.15
  (5 shorter events, 0.1 us)
Async XLA Ops:
  0.0 24.3 %all-to-all-start = ((bf16[16,32,256]{2,1,0:T(8,128)(2,1)}), bf16[16,32,256]{2,1,0:T(8,128)(2,1)S(1)}, u32[]{:S(2)}, u32[]{:S(2)}) async-start(bf16[16,32,256]{2,1,0:T(8,128)(2,1)} %bitcast.6), calls=%async_computation | async-start | bytes 524288 | tf_op jit(solution)/shard_map/all_to_all | solution.py:91
  11.1 20.4 %collective-permute-start = (bf16[256,256]{1,0:T(8,128)(2,1)S(1)}, bf16[256,256]{1,0:T(8,128)(2,1)S(1)}, u32[]{:S(2)}, u32[]{:S(2)}) collective-permute-start(bf16[256,256]{1,0:T(8,128)(2,1)S(1)} %slice.12), channel_id=1, source_target_pairs={{120,0},{0,8},{8,16},{16,24},{24,32},{32,40},{40,48},{48,56},{56,6... | collective-permute-start | bytes 393224 | tf_op jit(solution)/shard_map/ppermute | solution.py:20
  22.2 9.4 %copy-start = (bf16[512,256]{1,0:T(8,128)(2,1)S(1)}, bf16[512,256]{1,0:T(8,128)(2,1)}, u32[]{:S(2)}) copy-start(bf16[512,256]{1,0:T(8,128)(2,1)} %param.4) | copy-start | bytes 786436
  25.3 14.9 %all-to-all-start.1 = ((bf16[16,2,32,256]{3,2,1,0:T(8,128)(2,1)}), bf16[16,2,32,256]{3,2,1,0:T(8,128)(2,1)S(1)}, u32[]{:S(2)}, u32[]{:S(2)}) async-start(bf16[16,2,32,256]{3,2,1,0:T(8,128)(2,1)} %broadcast_in_dim.54), calls=%async_computation.1 | async-start | bytes 1048576 | tf_op jit(solution)/shard_map/all_to_all | solution.py:96
  31.7 8.5 %copy-start.1 = (bf16[768,256]{1,0:T(8,128)(2,1)}, bf16[768,256]{1,0:T(8,128)(2,1)S(1)}, u32[]{:S(2)}) copy-start(bf16[768,256]{1,0:T(8,128)(2,1)S(1)} %constant_dynamic-update-slice_fusion.q_ref) | copy-start | bytes 1179652
  40.2 0.8 copy-start.2
  47.4 36.2 %all-to-all-start.2 = ((f32[8,72,512]{2,1,0:T(8,128)}), f32[8,72,512]{2,1,0:T(8,128)S(1)}, u32[]{:S(2)}, u32[]{:S(2)}) async-start(f32[8,72,512]{2,1,0:T(8,128)} %shard_map.46), calls=%async_computation.2 | async-start | bytes 2359296 | tf_op jit(solution)/shard_map/all_to_all | solution.py:232

commit v12 on v11

--- a/solution.py
+++ b/solution.py
@@ -84,13 +84,18 @@
     return jnp.where(core == 0, jnp.concatenate([mine, other], axis=0), jnp.concatenate([other, mine], axis=0))
 
 
+def pick(stack, index):
+    mask = lax.broadcasted_iota(jnp.int32, (stack.shape[0],) + (1,) * (stack.ndim - 1), 0) == index
+    return jnp.sum(jnp.where(mask, stack, jnp.zeros_like(stack)), axis=0)
+
+
 def broadcast_block(block, source):
     count = lax.axis_size("col")
     piece = block.shape[0] // count
     parts = block.reshape(count, piece, block.shape[1])
     got = lax.all_to_all(parts, "col", 0, 0, tiled=False)
-    early = lax.dynamic_index_in_dim(got, lax.rem(source + count - 1, count), 0, keepdims=False)
-    late = lax.dynamic_index_in_dim(got, source, 0, keepdims=False)
+    early = pick(got, lax.rem(source + count - 1, count))
+    late = pick(got, source)
     pair = jnp.stack([early, late])[:, ::-1]
     spread_out = jnp.broadcast_to(pair[None], (count,) + pair.shape)
     return lax.all_to_all(spread_out, "col", 0, 0, tiled=False)
@@ -210,19 +215,14 @@
     tail = snapshots[block - lags :]
     history = shifted(tail, "col", 1)
     col_ext = jnp.concatenate([history, snapshots], axis=0)
-    chosen = lax.dynamic_index_in_dim(offsets, lax.axis_index("row"), 0, keepdims=False)
+    chosen = pick(offsets, lax.axis_index("row"))
     pieces = broadcast_block(snapshots, chosen)
-    row_begin = chosen * block
-    col_begin = lax.axis_index("col") * block
+    me = lax.axis_index("col")
     extent = block + lags
-    row_lengths = lax.dynamic_slice_in_dim(window_len, row_begin, block)
-    row_exps = lax.dynamic_slice_in_dim(cone_exp, row_begin, block)
-    row_weights = reversed_cone(row_lengths, row_exps, lags, extent)
-    col_weights = cone_matrix(
-        lax.dynamic_slice_in_dim(window_len, col_begin, block),
-        lax.dynamic_slice_in_dim(cone_exp, col_begin, block),
-        lags + 1,
-    )
+    lengths = window_len.reshape(-1, block)
+    exps = cone_exp.reshape(-1, block)
+    row_weights = reversed_cone(pick(lengths, chosen), pick(exps, chosen), lags, extent)
+    col_weights = cone_matrix(pick(lengths, me), pick(exps, me), lags + 1)
     col_wide = col_ext.astype(jnp.float32)
     col_part = jnp.sum(col_wide * col_wide, axis=1)
     col_sum = jnp.sum(col_weights * col_part[None, :], axis=1)

time: 85.1 us -> 83.5 us (0.981)
  between operations: 3.37 us -> 0.83 us
    reshape x0 -> x2, local copies, waits for them, and re-layouts: none -> 1.53 us  [the longest x1 0.77 us: shards(): lengths = window_len.reshape(-1, block)]
    reduce_sum x0 -> x3, other arithmetic: none -> 1.52 us  [pick(): return jnp.sum(jnp.where(mask, stack, jnp.zeros_like(stack)), axis=0)]
    dynamic_slice x2 -> x0, local copies, waits for them, and re-layouts: 1.25 us -> none  [the longest x1 1.24 us: shards(): lax.dynamic_index_in_dim(offsets, lax.axis_index('row'), 0, keepdims=False)]
  transfers between devices with their start and end apart: 4 -> 4, of which waited for: 2 -> 2; matrix products, arithmetic and copies ran while one was open for 14% -> 16% of each run, Pallas kernels for 0% -> 0%
where the time goes in v12:
time: 83.5 us; the launch traced here: 82.9 us
  waiting for transfers between devices  37.9 us (45%)
  starting transfers between devices  23 us (28%)
  other arithmetic  9.94 us (12%)
  Pallas kernels  6.44 us (8%)
  local copies, waits for them, and re-layouts  4.86 us (6%)
    all_to_all x1, waiting for transfers between devices, shards(): mine = jnp.sum(lax.all_to_all(payload, 'chan', 0, 0, tiled=False), axis=0)  32 us
    all_to_all x1, starting transfers between devices, broadcast_block(): got = lax.all_to_all(parts, 'col', 0, 0, tiled=False)  10.2 us
    pallas_call x1, Pallas kernels, lag_total(): pl.pallas_call(functools.partial(lag_kernel, lags), out_shape=jax.ShapeDt...  6.44 us
    all_to_all x1, waiting for transfers between devices, broadcast_block(): return lax.all_to_all(spread_out, 'col', 0, 0, tiled=False)  5.9 us
    all_to_all x1, starting transfers between devices, broadcast_block(): return lax.all_to_all(spread_out, 'col', 0, 0, tiled=False)  5.06 us
    all_to_all x1, starting transfers between devices, shards(): mine = jnp.sum(lax.all_to_all(payload, 'chan', 0, 0, tiled=False), axis=0)  4.16 us
    ppermute x1, starting transfers between devices, shifted(): return lax.ppermute(block, axis, route)  3.55 us
    div x1, other arithmetic, reversed_cone(): return cone / jnp.sum(cone, axis=1, keepdims=True)  2.09 us
  transfers between devices with their start and end apart: 4, of which 2 were waited for; matrix products, arithmetic and copies ran while one was open for 16% of the time, Pallas kernels for 0%

profile of v12, /device:TPU:1, one launch (start us, length us, event | category | flops | bytes accessed | tf_op | source)
XLA Modules:
  0.0 82.9 jit_solution(18108194420542013177)
XLA Ops:
  0.0 10.2 %all-to-all-start = ((bf16[16,32,256]{2,1,0:T(8,128)(2,1)}), bf16[16,32,256]{2,1,0:T(8,128)(2,1)S(1)}, u32[]{:S(2)}, u32[]{:S(2)}) async-start(bf16[16,32,256]{2,1,0:T(8,128)(2,1)} %bitcast.7), calls=%async_computation | async-start | bytes 524288 | tf_op jit(solution)/shard_map/all_to_all | solution.py:96
  10.2 0.9 %slice.12 = bf16[256,256]{1,0:T(8,128)(2,1)S(1)} slice(bf16[512,256]{1,0:T(8,128)(2,1)} %param.4), slice={[256:512], [0:256]} | slice | bytes 262144 | tf_op jit(solution)/shard_map/slice | solution.py:215
  11.1 3.5 %collective-permute-start = (bf16[256,256]{1,0:T(8,128)(2,1)S(1)}, bf16[256,256]{1,0:T(8,128)(2,1)S(1)}, u32[]{:S(2)}, u32[]{:S(2)}) collective-permute-start(bf16[256,256]{1,0:T(8,128)(2,1)S(1)} %slice.12), channel_id=1, source_target_pairs={{120,0},{0,8},{8,16},{16,24},{24,32},{32,40},{40,48},{48,56},{56,6... | collective-permute-start | bytes 393224 | tf_op jit(solution)/shard_map/ppermute | solution.py:20
  14.7 1.3 %fusion.18 = s32[]{:T(128)} fusion(s32[4]{0:T(128)} %param.5, s32[]{:T(128)S(6)} %axis_index.33), kind=kLoop, calls=%fused_computation.44 | loop fusion | flops 11 | bytes 24 | tf_op jit(solution)/shard_map/reduce_sum | solution.py:89
  16.7 0.7 iota_compare_fusion.1
  17.3 0.8 reshape.85
  18.1 0.8 reshape.86
  18.9 0.1 select_reduce_fusion.2
  19.0 1.4 %fusion.12 = f32[512]{0:T(512)S(1)} fusion(pred[512]{0:T(512)(128)(4,1)S(1)} %get-tuple-element.16, f32[512]{0:T(512)S(1)} %convert_element_type.34, pred[512]{0:T(512)(128)(4,1)S(1)} %get-tuple-element.17, pred[512]{0:T(512)(128)(4,1)S(1)} %get-tuple-element.15, s32[512]{0:T(512)S(1)} %get-tuple-element.12), kind=kLoop, calls=%fused_computation.19 | loop fusion | flops 5897728 | bytes 7680 | tf_op jit(solution)/shard_map/reduce_sum | solution.py:134
  20.5 0.0 copy-start
  20.5 2.1 %broadcast_divide_fusion.w_ref = f32[512,768]{1,0:T(8,128)} fusion(f32[512]{0:T(512)S(1)} %fusion.12, pred[512]{0:T(512)(128)(4,1)S(1)} %get-tuple-element.16, f32[512]{0:T(512)S(1)} %convert_element_type.34, pred[512]{0:T(512)(128)(4,1)S(1)} %get-tuple-element.17, pred[512]{0:T(512)(128)(4,1)S(1)} %get-tuple-element.15, s32[512]{0:T(512)S(1)} %get-tuple-element.12), kind=kLoop, calls=%fused_computation.17 | loop fusion | flops 5898240 | bytes 1580544 | tf_op jit(solution)/shard_map/div | solution.py:134
  22.6 0.0 all-to-all-done
  22.6 0.1 select_reduce_fusion.1
  22.7 0.1 rev.3
  22.8 0.9 %broadcast_in_dim.88 = bf16[16,2,32,256]{3,2,1,0:T(8,128)(2,1)} broadcast(bf16[2,32,256]{2,1,0:T(8,128)(2,1)S(1)} %rev.3), dimensions={1,2,3} | broadcast | bytes 557056 | tf_op jit(solution)/shard_map/broadcast_in_dim | solution.py:100
  23.7 5.1 %all-to-all-start.1 = ((bf16[16,2,32,256]{3,2,1,0:T(8,128)(2,1)}), bf16[16,2,32,256]{3,2,1,0:T(8,128)(2,1)S(1)}, u32[]{:S(2)}, u32[]{:S(2)}) async-start(bf16[16,2,32,256]{3,2,1,0:T(8,128)(2,1)} %broadcast_in_dim.88), calls=%async_computation.1 | async-start | bytes 1048576 | tf_op jit(solution)/shard_map/all_to_all | solution.py:101
  28.7 1.2 %fusion.13 = f32[512]{0:T(512)S(1)} fusion(pred[512]{0:T(512)(128)(4,1)S(1)} %get-tuple-element.19, f32[512]{0:T(512)S(1)} %convert_element_type.32, pred[512]{0:T(512)(128)(4,1)S(1)} %get-tuple-element.20, pred[512]{0:T(512)(128)(4,1)S(1)} %get-tuple-element.18, s32[512]{0:T(512)S(1)} %get-tuple-element.11, s32[512]{0:T(512)S(1)} %iota_add_fusion), kind=kLoop, calls=%fused_computation.20 | loop fusion | flops 5504512 | bytes 9728 | tf_op jit(solution)/shard_map/reduce_sum | solution.py:122
  30.0 0.0 collective-permute-done
  30.0 0.0 copy-done
  30.0 0.0 copy-start.1
  30.0 0.2 multiply_reduce_fusion.1
  30.2 0.6 broadcast_in_dim.89.cp_ref
  30.8 1.8 %multiply_reduce_fusion = f32[512]{0:T(512)} fusion(f32[768]{0:T(1024)S(1)} %multiply_reduce_fusion.1, f32[512]{0:T(512)S(1)} %fusion.13, pred[512]{0:T(512)(128)(4,1)S(1)} %get-tuple-element.19, f32[512]{0:T(512)S(1)} %convert_element_type.32, pred[512]{0:T(512)(128)(4,1)S(1)} %get-tuple-element.20, pred[512]{0:T(512)(128)(4,1)S(1)} %get-tuple-element.18, ...), kind=kLoop, calls=%fused_computation.11 | loop fusion | flops 6290944 | bytes 14848 | tf_op jit(solution)/shard_map/reduce_sum | solution.py:228
  32.7 5.9 %all-to-all-done.1.r_ref = bf16[16,2,32,256]{3,2,1,0:T(8,128)(2,1)S(1)} async-done(((bf16[16,2,32,256]{3,2,1,0:T(8,128)(2,1)}), bf16[16,2,32,256]{3,2,1,0:T(8,128)(2,1)S(1)}, u32[]{:S(2)}, u32[]{:S(2)}) %all-to-all-start.1) | async-done | bytes 524320 | tf_op jit(solution)/shard_map/all_to_all | solution.py:101
  38.5 0.0 copy-start.2
  38.5 0.0 copy-done.1
  38.6 0.8 copy-done.2
  39.4 6.4 %shard_map.46 = f32[8,72,512]{2,1,0:T(8,128)} custom-call(bf16[16,2,32,256]{3,2,1,0:T(8,128)(2,1)} %copy-done.2, bf16[768,256]{1,0:T(8,128)(2,1)} %copy-done.1, f32[1,768]{1,0:T(1,128)} %broadcast_in_dim.89.cp_ref, f32[1,512]{1,0:T(1,128)} %bitcast.11, f32[512,768]{1,0:T(8,128)} %broadcast_divide_fusion.w_ref), custom_call_target="tpu_custom_call" | custom-call | flops 1811939328 | bytes 3407872 | tf_op jit(solution)/shard_map/pallas_call | solution.py:201
  45.8 4.2 %all-to-all-start.2 = ((f32[8,72,512]{2,1,0:T(8,128)}), f32[8,72,512]{2,1,0:T(8,128)S(1)}, u32[]{:S(2)}, u32[]{:S(2)}) async-start(f32[8,72,512]{2,1,0:T(8,128)} %shard_map.46), calls=%async_computation.2 | async-start | bytes 2359296 | tf_op jit(solution)/shard_map/all_to_all | solution.py:232
  50.0 32.0 %all-to-all-done.2 = f32[8,72,512]{2,1,0:T(8,128)S(1)} async-done(((f32[8,72,512]{2,1,0:T(8,128)}), f32[8,72,512]{2,1,0:T(8,128)S(1)}, u32[]{:S(2)}, u32[]{:S(2)}) %all-to-all-start.2) | async-done | bytes 1179680 | tf_op jit(solution)/shard_map/all_to_all | solution.py:232
  82.0 0.1 reduce_sum.125
  82.1 0.1 multiply_bitcast_fusion
  82.2 0.8 fusion.15
  (10 shorter events, 0.1 us)
Async XLA Ops:
  0.0 22.6 %all-to-all-start = ((bf16[16,32,256]{2,1,0:T(8,128)(2,1)}), bf16[16,32,256]{2,1,0:T(8,128)(2,1)S(1)}, u32[]{:S(2)}, u32[]{:S(2)}) async-start(bf16[16,32,256]{2,1,0:T(8,128)(2,1)} %bitcast.7), calls=%async_computation | async-start | bytes 524288 | tf_op jit(solution)/shard_map/all_to_all | solution.py:96
  11.1 18.8 %collective-permute-start = (bf16[256,256]{1,0:T(8,128)(2,1)S(1)}, bf16[256,256]{1,0:T(8,128)(2,1)S(1)}, u32[]{:S(2)}, u32[]{:S(2)}) collective-permute-start(bf16[256,256]{1,0:T(8,128)(2,1)S(1)} %slice.12), channel_id=1, source_target_pairs={{120,0},{0,8},{8,16},{16,24},{24,32},{32,40},{40,48},{48,56},{56,6... | collective-permute-start | bytes 393224 | tf_op jit(solution)/shard_map/ppermute | solution.py:20
  20.5 9.5 %copy-start = (bf16[512,256]{1,0:T(8,128)(2,1)S(1)}, bf16[512,256]{1,0:T(8,128)(2,1)}, u32[]{:S(2)}) copy-start(bf16[512,256]{1,0:T(8,128)(2,1)} %param.4) | copy-start | bytes 786436
  23.7 14.9 %all-to-all-start.1 = ((bf16[16,2,32,256]{3,2,1,0:T(8,128)(2,1)}), bf16[16,2,32,256]{3,2,1,0:T(8,128)(2,1)S(1)}, u32[]{:S(2)}, u32[]{:S(2)}) async-start(bf16[16,2,32,256]{3,2,1,0:T(8,128)(2,1)} %broadcast_in_dim.88), calls=%async_computation.1 | async-start | bytes 1048576 | tf_op jit(solution)/shard_map/all_to_all | solution.py:101
  30.0 8.5 %copy-start.1 = (bf16[768,256]{1,0:T(8,128)(2,1)}, bf16[768,256]{1,0:T(8,128)(2,1)S(1)}, u32[]{:S(2)}) copy-start(bf16[768,256]{1,0:T(8,128)(2,1)S(1)} %constant_dynamic-update-slice_fusion.q_ref) | copy-start | bytes 1179652
  38.5 0.8 copy-start.2
  45.8 36.2 %all-to-all-start.2 = ((f32[8,72,512]{2,1,0:T(8,128)}), f32[8,72,512]{2,1,0:T(8,128)S(1)}, u32[]{:S(2)}, u32[]{:S(2)}) async-start(f32[8,72,512]{2,1,0:T(8,128)} %shard_map.46), calls=%async_computation.2 | async-start | bytes 2359296 | tf_op jit(solution)/shard_map/all_to_all | solution.py:232

commit v13 on v12

--- a/solution.py
+++ b/solution.py
@@ -117,9 +117,10 @@
     lag = row_pos + (lags - 1) - col_pos
     span = lengths[:, None]
     valid = (lag >= 0) & (lag < span)
-    frac = (span.astype(jnp.float32) - lag.astype(jnp.float32)) / span.astype(jnp.float32)
+    inverse = 1.0 / span.astype(jnp.float32)
+    frac = (span.astype(jnp.float32) - lag.astype(jnp.float32)) * inverse
     cone = jnp.where(valid, power_int(frac, exps[:, None]), jnp.zeros_like(frac))
-    return cone / jnp.sum(cone, axis=1, keepdims=True)
+    return cone * (1.0 / jnp.sum(cone, axis=1, keepdims=True))
 
 
 def reversed_cone(lengths, exps, lags, depth):
@@ -129,9 +130,10 @@
     lag = row_pos + col_pos - (depth - lags) + 1
     span = lengths[:, None]
     valid = (lag >= 0) & (lag < span)
-    frac = (span.astype(jnp.float32) - lag.astype(jnp.float32)) / span.astype(jnp.float32)
+    inverse = 1.0 / span.astype(jnp.float32)
+    frac = (span.astype(jnp.float32) - lag.astype(jnp.float32)) * inverse
     cone = jnp.where(valid, power_int(frac, exps[:, None]), jnp.zeros_like(frac))
-    return cone / jnp.sum(cone, axis=1, keepdims=True)
+    return cone * (1.0 / jnp.sum(cone, axis=1, keepdims=True))
 
 
 def lag_kernel(lags, r_ref, q_ref, cp_ref, csum_ref, w_ref, o_ref):
@@ -219,10 +221,11 @@
     pieces = broadcast_block(snapshots, chosen)
     me = lax.axis_index("col")
     extent = block + lags
-    lengths = window_len.reshape(-1, block)
-    exps = cone_exp.reshape(-1, block)
-    row_weights = reversed_cone(pick(lengths, chosen), pick(exps, chosen), lags, extent)
-    col_weights = cone_matrix(pick(lengths, me), pick(exps, me), lags + 1)
+    tables = jnp.stack([window_len, cone_exp]).reshape(2, -1, block).transpose(1, 0, 2)
+    row_lengths, row_exps = pick(tables, chosen)
+    col_lengths, col_exps = pick(tables, me)
+    row_weights = reversed_cone(row_lengths, row_exps, lags, extent)
+    col_weights = cone_matrix(col_lengths, col_exps, lags + 1)
     col_wide = col_ext.astype(jnp.float32)
     col_part = jnp.sum(col_wide * col_wide, axis=1)
     col_sum = jnp.sum(col_weights * col_part[None, :], axis=1)

time: 83.5 us -> 83.5 us (level)
    div x1 -> x4, other arithmetic: 2.09 us -> 0.02 us  [the longest x1 0.01 us: reversed_cone(): return cone * (1.0 / jnp.sum(cone, axis=1, keepdims=True))]
    mul x0 -> x1, other arithmetic: none -> 2 us  [reversed_cone(): return cone * (1.0 / jnp.sum(cone, axis=1, keepdims=True))]
    another operation x0 -> x5, local copies, waits for them, and re-layouts: none -> 1.54 us  [the longest x3 1.54 us: shards(): jnp.stack([window_len, cone_exp]).reshape(2, -1, block).transpose(1, 0, 2)]
    reshape x2 -> x0, local copies, waits for them, and re-layouts: 1.53 us -> none  [the longest x1 0.77 us: shards(): lengths = window_len.reshape(-1, block)]
where the time goes in v13:
time: 83.5 us; the launch traced here: 82.9 us
  waiting for transfers between devices  37.9 us (45%)
  starting transfers between devices  23 us (28%)
  other arithmetic  9.86 us (12%)
  Pallas kernels  6.44 us (8%)
  local copies, waits for them, and re-layouts  4.88 us (6%)
  between operations  0.85 us (1%)
    all_to_all x1, waiting for transfers between devices, shards(): mine = jnp.sum(lax.all_to_all(payload, 'chan', 0, 0, tiled=False), axis=0)  32 us
    all_to_all x1, starting transfers between devices, broadcast_block(): got = lax.all_to_all(parts, 'col', 0, 0, tiled=False)  10.2 us
    pallas_call x1, Pallas kernels, lag_total(): pl.pallas_call(functools.partial(lag_kernel, lags), out_shape=jax.ShapeDt...  6.44 us
    all_to_all x1, waiting for transfers between devices, broadcast_block(): return lax.all_to_all(spread_out, 'col', 0, 0, tiled=False)  5.9 us
    all_to_all x1, starting transfers between devices, broadcast_block(): return lax.all_to_all(spread_out, 'col', 0, 0, tiled=False)  5.06 us
    all_to_all x1, starting transfers between devices, shards(): mine = jnp.sum(lax.all_to_all(payload, 'chan', 0, 0, tiled=False), axis=0)  4.16 us
    ppermute x1, starting transfers between devices, shifted(): return lax.ppermute(block, axis, route)  3.55 us
    mul x1, other arithmetic, reversed_cone(): return cone * (1.0 / jnp.sum(cone, axis=1, keepdims=True))  2 us
  transfers between devices with their start and end apart: 4, of which 2 were waited for; matrix products, arithmetic and copies ran while one was open for 16% of the time, Pallas kernels for 0%

profile of v13, /device:TPU:1, one launch (start us, length us, event | category | flops | bytes accessed | tf_op | source)
XLA Modules:
  0.0 82.9 jit_solution(11987933704660967818)
XLA Ops:
  0.0 10.2 %all-to-all-start = ((bf16[16,32,256]{2,1,0:T(8,128)(2,1)}), bf16[16,32,256]{2,1,0:T(8,128)(2,1)S(1)}, u32[]{:S(2)}, u32[]{:S(2)}) async-start(bf16[16,32,256]{2,1,0:T(8,128)(2,1)} %bitcast.9), calls=%async_computation | async-start | bytes 524288 | tf_op jit(solution)/shard_map/all_to_all | solution.py:96
  10.2 0.9 %slice.12 = bf16[256,256]{1,0:T(8,128)(2,1)S(1)} slice(bf16[512,256]{1,0:T(8,128)(2,1)} %param.4), slice={[256:512], [0:256]} | slice | bytes 262144 | tf_op jit(solution)/shard_map/slice | solution.py:217
  11.1 3.5 %collective-permute-start = (bf16[256,256]{1,0:T(8,128)(2,1)S(1)}, bf16[256,256]{1,0:T(8,128)(2,1)S(1)}, u32[]{:S(2)}, u32[]{:S(2)}) collective-permute-start(bf16[256,256]{1,0:T(8,128)(2,1)S(1)} %slice.12), channel_id=1, source_target_pairs={{120,0},{0,8},{8,16},{16,24},{24,32},{32,40},{40,48},{48,56},{56,6... | collective-permute-start | bytes 393224 | tf_op jit(solution)/shard_map/ppermute | solution.py:20
  14.7 1.3 %fusion.18 = s32[]{:T(128)} fusion(s32[4]{0:T(128)} %param.5, s32[]{:T(128)S(6)} %axis_index.33), kind=kLoop, calls=%fused_computation.48 | loop fusion | flops 11 | bytes 24 | tf_op jit(solution)/shard_map/reduce_sum | solution.py:89
  16.7 0.7 iota_compare_fusion.1
  17.3 0.8 stack.21
  18.1 0.8 stack.22
  18.9 0.1 select_reduce_fusion.2
  19.1 1.4 %fusion.13 = f32[512]{0:T(512)S(1)} fusion(pred[512]{0:T(512)(128)(4,1)S(1)} %get-tuple-element.11, f32[512]{0:T(512)S(1)} %broadcast_divide_fusion.1, f32[512]{0:T(512)S(1)} %convert_element_type.40, pred[512]{0:T(512)(128)(4,1)S(1)} %get-tuple-element.10, pred[512]{0:T(512)(128)(4,1)S(1)} %get-tuple-element.9, s32[512]{0:T(512)S(1)} %bitcast.14), kind=kLoop, calls=%fused_computation.20 | loop fusion | flops 5897728 | bytes 9728 | tf_op jit(solution)/shard_map/reduce_sum | solution.py:136
  20.5 0.0 copy-start
  20.5 2.0 %broadcast_multiply_fusion.w_ref = f32[512,768]{1,0:T(8,128)} fusion(f32[512]{0:T(512)S(1)} %broadcast_divide_fusion, pred[512]{0:T(512)(128)(4,1)S(1)} %get-tuple-element.11, f32[512]{0:T(512)S(1)} %broadcast_divide_fusion.1, f32[512]{0:T(512)S(1)} %convert_element_type.40, pred[512]{0:T(512)(128)(4,1)S(1)} %get-tuple-element.10, ...), kind=kLoop, calls=%fused_computation.18 | loop fusion | flops 5898240 | bytes 1582592 | tf_op jit(solution)/shard_map/mul | solution.py:136
  22.5 0.0 all-to-all-done
  22.5 0.1 select_reduce_fusion.1
  22.7 0.1 rev.3
  22.8 0.9 %broadcast_in_dim.78 = bf16[16,2,32,256]{3,2,1,0:T(8,128)(2,1)} broadcast(bf16[2,32,256]{2,1,0:T(8,128)(2,1)S(1)} %rev.3), dimensions={1,2,3} | broadcast | bytes 557056 | tf_op jit(solution)/shard_map/broadcast_in_dim | solution.py:100
  23.6 5.1 %all-to-all-start.1 = ((bf16[16,2,32,256]{3,2,1,0:T(8,128)(2,1)}), bf16[16,2,32,256]{3,2,1,0:T(8,128)(2,1)S(1)}, u32[]{:S(2)}, u32[]{:S(2)}) async-start(bf16[16,2,32,256]{3,2,1,0:T(8,128)(2,1)} %broadcast_in_dim.78), calls=%async_computation.1 | async-start | bytes 1048576 | tf_op jit(solution)/shard_map/all_to_all | solution.py:101
  28.7 1.2 %fusion.12 = f32[512]{0:T(512)S(1)} fusion(f32[512]{0:T(512)S(1)} %broadcast_divide_fusion.3, f32[512]{0:T(512)S(1)} %convert_element_type.38, s32[512]{0:T(512)S(1)} %bitcast.18, s32[512]{0:T(512)S(1)} %iota_add_fusion, pred[512]{0:T(512)(128)(4,1)S(1)} %get-tuple-element.14, pred[512]{0:T(512)(128)(4,1)S(1)} %get-tuple-element.13, ...), kind=kLoop, calls=%fused_computation.17 | loop fusion | flops 5504512 | bytes 11776 | tf_op jit(solution)/shard_map/reduce_sum | solution.py:123
  29.9 0.0 collective-permute-done
  30.0 0.0 copy-done
  30.0 0.0 copy-start.1
  30.0 0.2 multiply_reduce_fusion.1
  30.2 0.6 broadcast_in_dim.79.cp_ref
  30.8 1.8 %multiply_reduce_fusion = f32[512]{0:T(512)} fusion(f32[768]{0:T(1024)S(1)} %multiply_reduce_fusion.1, f32[512]{0:T(512)S(1)} %broadcast_divide_fusion.2, f32[512]{0:T(512)S(1)} %broadcast_divide_fusion.3, f32[512]{0:T(512)S(1)} %convert_element_type.38, s32[512]{0:T(512)S(1)} %bitcast.19, s32[512]{0:T(512)S(1)} %iota_add_fusion, ...), kind=kLoop, calls=%fused_computation.11 | loop fusion | flops 6290944 | bytes 16896 | tf_op jit(solution)/shard_map/reduce_sum | solution.py:231
  32.6 5.9 %all-to-all-done.1.r_ref = bf16[16,2,32,256]{3,2,1,0:T(8,128)(2,1)S(1)} async-done(((bf16[16,2,32,256]{3,2,1,0:T(8,128)(2,1)}), bf16[16,2,32,256]{3,2,1,0:T(8,128)(2,1)S(1)}, u32[]{:S(2)}, u32[]{:S(2)}) %all-to-all-start.1) | async-done | bytes 524320 | tf_op jit(solution)/shard_map/all_to_all | solution.py:101
  38.5 0.0 copy-start.2
  38.5 0.0 copy-done.1
  38.5 0.8 copy-done.2
  39.3 6.4 %shard_map.46 = f32[8,72,512]{2,1,0:T(8,128)} custom-call(bf16[16,2,32,256]{3,2,1,0:T(8,128)(2,1)} %copy-done.2, bf16[768,256]{1,0:T(8,128)(2,1)} %copy-done.1, f32[1,768]{1,0:T(1,128)} %broadcast_in_dim.79.cp_ref, f32[1,512]{1,0:T(1,128)} %bitcast.21, f32[512,768]{1,0:T(8,128)} %broadcast_multiply_fusion.w_ref), custom_call_target="tpu_custom_call" | custom-call | flops 1811939328 | bytes 3407872 | tf_op jit(solution)/shard_map/pallas_call | solution.py:203
  45.8 4.2 %all-to-all-start.2 = ((f32[8,72,512]{2,1,0:T(8,128)}), f32[8,72,512]{2,1,0:T(8,128)S(1)}, u32[]{:S(2)}, u32[]{:S(2)}) async-start(f32[8,72,512]{2,1,0:T(8,128)} %shard_map.46), calls=%async_computation.2 | async-start | bytes 2359296 | tf_op jit(solution)/shard_map/all_to_all | solution.py:235
  49.9 32.0 %all-to-all-done.2 = f32[8,72,512]{2,1,0:T(8,128)S(1)} async-done(((f32[8,72,512]{2,1,0:T(8,128)}), f32[8,72,512]{2,1,0:T(8,128)S(1)}, u32[]{:S(2)}, u32[]{:S(2)}) %all-to-all-start.2) | async-done | bytes 1179680 | tf_op jit(solution)/shard_map/all_to_all | solution.py:235
  81.9 0.1 reduce_sum.105
  82.0 0.1 multiply_bitcast_fusion
  82.1 0.8 fusion.15
  (18 shorter events, 0.2 us)
Async XLA Ops:
  0.0 22.5 %all-to-all-start = ((bf16[16,32,256]{2,1,0:T(8,128)(2,1)}), bf16[16,32,256]{2,1,0:T(8,128)(2,1)S(1)}, u32[]{:S(2)}, u32[]{:S(2)}) async-start(bf16[16,32,256]{2,1,0:T(8,128)(2,1)} %bitcast.9), calls=%async_computation | async-start | bytes 524288 | tf_op jit(solution)/shard_map/all_to_all | solution.py:96
  11.1 18.8 %collective-permute-start = (bf16[256,256]{1,0:T(8,128)(2,1)S(1)}, bf16[256,256]{1,0:T(8,128)(2,1)S(1)}, u32[]{:S(2)}, u32[]{:S(2)}) collective-permute-start(bf16[256,256]{1,0:T(8,128)(2,1)S(1)} %slice.12), channel_id=1, source_target_pairs={{120,0},{0,8},{8,16},{16,24},{24,32},{32,40},{40,48},{48,56},{56,6... | collective-permute-start | bytes 393224 | tf_op jit(solution)/shard_map/ppermute | solution.py:20
  20.5 9.4 %copy-start = (bf16[512,256]{1,0:T(8,128)(2,1)S(1)}, bf16[512,256]{1,0:T(8,128)(2,1)}, u32[]{:S(2)}) copy-start(bf16[512,256]{1,0:T(8,128)(2,1)} %param.4) | copy-start | bytes 786436
  23.6 14.9 %all-to-all-start.1 = ((bf16[16,2,32,256]{3,2,1,0:T(8,128)(2,1)}), bf16[16,2,32,256]{3,2,1,0:T(8,128)(2,1)S(1)}, u32[]{:S(2)}, u32[]{:S(2)}) async-start(bf16[16,2,32,256]{3,2,1,0:T(8,128)(2,1)} %broadcast_in_dim.78), calls=%async_computation.1 | async-start | bytes 1048576 | tf_op jit(solution)/shard_map/all_to_all | solution.py:101
  30.0 8.5 %copy-start.1 = (bf16[768,256]{1,0:T(8,128)(2,1)}, bf16[768,256]{1,0:T(8,128)(2,1)S(1)}, u32[]{:S(2)}) copy-start(bf16[768,256]{1,0:T(8,128)(2,1)S(1)} %constant_dynamic-update-slice_fusion.q_ref) | copy-start | bytes 1179652
  38.5 0.8 copy-start.2
  45.8 36.2 %all-to-all-start.2 = ((f32[8,72,512]{2,1,0:T(8,128)}), f32[8,72,512]{2,1,0:T(8,128)S(1)}, u32[]{:S(2)}, u32[]{:S(2)}) async-start(f32[8,72,512]{2,1,0:T(8,128)} %shard_map.46), calls=%async_computation.2 | async-start | bytes 2359296 | tf_op jit(solution)/shard_map/all_to_all | solution.py:235

commit v14 on v12

--- a/solution.py
+++ b/solution.py
@@ -89,16 +89,17 @@
     return jnp.sum(jnp.where(mask, stack, jnp.zeros_like(stack)), axis=0)
 
 
-def broadcast_block(block, source):
+def broadcast_block(block, source, held):
     count = lax.axis_size("col")
     piece = block.shape[0] // count
     parts = block.reshape(count, piece, block.shape[1])
     got = lax.all_to_all(parts, "col", 0, 0, tiled=False)
+    got, held = lax.optimization_barrier((got, held))
     early = pick(got, lax.rem(source + count - 1, count))
     late = pick(got, source)
     pair = jnp.stack([early, late])[:, ::-1]
     spread_out = jnp.broadcast_to(pair[None], (count,) + pair.shape)
-    return lax.all_to_all(spread_out, "col", 0, 0, tiled=False)
+    return lax.all_to_all(spread_out, "col", 0, 0, tiled=False), held
 
 
 def power_int(frac, exps):
@@ -216,13 +217,13 @@
     history = shifted(tail, "col", 1)
     col_ext = jnp.concatenate([history, snapshots], axis=0)
     chosen = pick(offsets, lax.axis_index("row"))
-    pieces = broadcast_block(snapshots, chosen)
     me = lax.axis_index("col")
     extent = block + lags
     lengths = window_len.reshape(-1, block)
     exps = cone_exp.reshape(-1, block)
+    pieces, (col_lengths, col_exps) = broadcast_block(snapshots, chosen, (pick(lengths, me), pick(exps, me)))
     row_weights = reversed_cone(pick(lengths, chosen), pick(exps, chosen), lags, extent)
-    col_weights = cone_matrix(pick(lengths, me), pick(exps, me), lags + 1)
+    col_weights = cone_matrix(col_lengths, col_exps, lags + 1)
     col_wide = col_ext.astype(jnp.float32)
     col_part = jnp.sum(col_wide * col_wide, axis=1)
     col_sum = jnp.sum(col_weights * col_part[None, :], axis=1)

time: 83.5 us -> 84.4 us (1.011)
  transfers between devices with their start and end apart: 4 -> 4, of which waited for: 2 -> 2; matrix products, arithmetic and copies ran while one was open for 16% -> 14% of each run, Pallas kernels for 0% -> 0%
where the time goes in v14:
time: 84.4 us; the launch traced here: 83.8 us
  waiting for transfers between devices  38.7 us (46%)
  starting transfers between devices  23.1 us (27%)
  other arithmetic  9.97 us (12%)
  Pallas kernels  6.44 us (8%)
  local copies, waits for them, and re-layouts  4.86 us (6%)
    all_to_all x1, waiting for transfers between devices, shards(): mine = jnp.sum(lax.all_to_all(payload, 'chan', 0, 0, tiled=False), axis=0)  32 us
    all_to_all x1, starting transfers between devices, broadcast_block(): got = lax.all_to_all(parts, 'col', 0, 0, tiled=False)  10.3 us
    all_to_all x1, waiting for transfers between devices, broadcast_block(): return (lax.all_to_all(spread_out, 'col', 0, 0, tiled=False), held)  6.68 us
    pallas_call x1, Pallas kernels, lag_total(): pl.pallas_call(functools.partial(lag_kernel, lags), out_shape=jax.ShapeDt...  6.44 us
    all_to_all x1, starting transfers between devices, broadcast_block(): return (lax.all_to_all(spread_out, 'col', 0, 0, tiled=False), held)  5.06 us
    all_to_all x1, starting transfers between devices, shards(): mine = jnp.sum(lax.all_to_all(payload, 'chan', 0, 0, tiled=False), axis=0)  4.16 us
    ppermute x1, starting transfers between devices, shifted(): return lax.ppermute(block, axis, route)  3.55 us
    div x1, other arithmetic, reversed_cone(): return cone / jnp.sum(cone, axis=1, keepdims=True)  2.09 us
  transfers between devices with their start and end apart: 4, of which 2 were waited for; matrix products, arithmetic and copies ran while one was open for 14% of the time, Pallas kernels for 0%

profile of v14, /device:TPU:1, one launch (start us, length us, event | category | flops | bytes accessed | tf_op | source)
XLA Modules:
  0.0 83.8 jit_solution(4582119252234055916)
XLA Ops:
  0.0 0.0 copy-start
  0.0 10.3 %all-to-all-start = ((bf16[16,32,256]{2,1,0:T(8,128)(2,1)}), bf16[16,32,256]{2,1,0:T(8,128)(2,1)S(1)}, u32[]{:S(2)}, u32[]{:S(2)}) async-start(bf16[16,32,256]{2,1,0:T(8,128)(2,1)} %bitcast.7), calls=%async_computation | async-start | bytes 524288 | tf_op jit(solution)/shard_map/all_to_all | solution.py:96
  10.3 0.9 %slice.12 = bf16[256,256]{1,0:T(8,128)(2,1)S(1)} slice(bf16[512,256]{1,0:T(8,128)(2,1)} %param.4), slice={[256:512], [0:256]} | slice | bytes 262144 | tf_op jit(solution)/shard_map/slice | solution.py:216
  11.3 3.5 %collective-permute-start = (bf16[256,256]{1,0:T(8,128)(2,1)S(1)}, bf16[256,256]{1,0:T(8,128)(2,1)S(1)}, u32[]{:S(2)}, u32[]{:S(2)}) collective-permute-start(bf16[256,256]{1,0:T(8,128)(2,1)S(1)} %slice.12), channel_id=1, source_target_pairs={{120,0},{0,8},{8,16},{16,24},{24,32},{32,40},{40,48},{48,56},{56,6... | collective-permute-start | bytes 393224 | tf_op jit(solution)/shard_map/ppermute | solution.py:20
  14.8 1.3 %fusion.18 = s32[]{:T(128)} fusion(s32[4]{0:T(128)} %param.5, s32[]{:T(128)S(6)} %axis_index.33), kind=kLoop, calls=%fused_computation.44 | loop fusion | flops 11 | bytes 24 | tf_op jit(solution)/shard_map/reduce_sum | solution.py:89
  16.8 0.7 iota_compare_fusion
  17.5 0.8 reshape.77
  18.2 0.8 reshape.78
  19.0 0.1 select_reduce_fusion.2
  19.1 1.4 %fusion.12 = f32[512]{0:T(512)S(1)} fusion(pred[512]{0:T(512)(128)(4,1)S(1)} %get-tuple-element.22, f32[512]{0:T(512)S(1)} %convert_element_type.30, pred[512]{0:T(512)(128)(4,1)S(1)} %get-tuple-element.23, pred[512]{0:T(512)(128)(4,1)S(1)} %get-tuple-element.21, s32[512]{0:T(512)S(1)} %get-tuple-element.18), kind=kLoop, calls=%fused_computation.19 | loop fusion | flops 5897728 | bytes 7680 | tf_op jit(solution)/shard_map/reduce_sum | solution.py:135
  20.6 2.1 %broadcast_divide_fusion.w_ref = f32[512,768]{1,0:T(8,128)} fusion(f32[512]{0:T(512)S(1)} %fusion.12, pred[512]{0:T(512)(128)(4,1)S(1)} %get-tuple-element.22, f32[512]{0:T(512)S(1)} %convert_element_type.30, pred[512]{0:T(512)(128)(4,1)S(1)} %get-tuple-element.23, pred[512]{0:T(512)(128)(4,1)S(1)} %get-tuple-element.21, s32[512]{0:T(512)S(1)} %get-tuple-element.18), kind=kLoop, calls=%fused_computation.17 | loop fusion | flops 5898240 | bytes 1580544 | tf_op jit(solution)/shard_map/div | solution.py:135
  22.7 0.0 collective-permute-done
  22.7 0.0 copy-done
  22.7 0.0 copy-start.1
  22.7 0.2 multiply_reduce_fusion.1
  22.9 0.6 broadcast_in_dim.90.cp_ref
  23.5 0.0 all-to-all-done
  23.5 0.1 select_reduce_fusion.1
  23.6 0.1 rev.3
  23.7 0.9 %broadcast_in_dim.89 = bf16[16,2,32,256]{3,2,1,0:T(8,128)(2,1)} broadcast(bf16[2,32,256]{2,1,0:T(8,128)(2,1)S(1)} %rev.3), dimensions={1,2,3} | broadcast | bytes 557056 | tf_op jit(solution)/shard_map/broadcast_in_dim | solution.py:101
  24.6 5.1 %all-to-all-start.1 = ((bf16[16,2,32,256]{3,2,1,0:T(8,128)(2,1)}), bf16[16,2,32,256]{3,2,1,0:T(8,128)(2,1)S(1)}, u32[]{:S(2)}, u32[]{:S(2)}) async-start(bf16[16,2,32,256]{3,2,1,0:T(8,128)(2,1)} %broadcast_in_dim.89), calls=%async_computation.1 | async-start | bytes 1048576 | tf_op jit(solution)/shard_map/all_to_all | solution.py:102
  29.7 1.2 %fusion.13 = f32[512]{0:T(512)S(1)} fusion(pred[512]{0:T(512)(128)(4,1)S(1)} %get-tuple-element.25, f32[512]{0:T(512)S(1)} %convert_element_type.28, pred[512]{0:T(512)(128)(4,1)S(1)} %get-tuple-element.26, pred[512]{0:T(512)(128)(4,1)S(1)} %get-tuple-element.24, s32[512]{0:T(512)S(1)} %get-tuple-element.9, s32[512]{0:T(512)S(1)} %iota_add_fusion), kind=kLoop, calls=%fused_computation.20 | loop fusion | flops 5504512 | bytes 9728 | tf_op jit(solution)/shard_map/reduce_sum | solution.py:123
  30.9 1.9 %multiply_reduce_fusion = f32[512]{0:T(512)} fusion(f32[768]{0:T(1024)S(1)} %multiply_reduce_fusion.1, f32[512]{0:T(512)S(1)} %fusion.13, pred[512]{0:T(512)(128)(4,1)S(1)} %get-tuple-element.25, f32[512]{0:T(512)S(1)} %convert_element_type.28, pred[512]{0:T(512)(128)(4,1)S(1)} %get-tuple-element.26, pred[512]{0:T(512)(128)(4,1)S(1)} %get-tuple-element.24, ...), kind=kLoop, calls=%fused_computation.11 | loop fusion | flops 6290944 | bytes 14848 | tf_op jit(solution)/shard_map/reduce_sum | solution.py:229
  32.8 6.7 %all-to-all-done.1.r_ref = bf16[16,2,32,256]{3,2,1,0:T(8,128)(2,1)S(1)} async-done(((bf16[16,2,32,256]{3,2,1,0:T(8,128)(2,1)}), bf16[16,2,32,256]{3,2,1,0:T(8,128)(2,1)S(1)}, u32[]{:S(2)}, u32[]{:S(2)}) %all-to-all-start.1) | async-done | bytes 524320 | tf_op jit(solution)/shard_map/all_to_all | solution.py:102
  39.5 0.0 copy-start.2
  39.5 0.0 copy-done.1
  39.5 0.8 copy-done.2
  40.3 6.4 %shard_map.46 = f32[8,72,512]{2,1,0:T(8,128)} custom-call(bf16[16,2,32,256]{3,2,1,0:T(8,128)(2,1)} %copy-done.2, bf16[768,256]{1,0:T(8,128)(2,1)} %copy-done.1, f32[1,768]{1,0:T(1,128)} %broadcast_in_dim.90.cp_ref, f32[1,512]{1,0:T(1,128)} %bitcast.11, f32[512,768]{1,0:T(8,128)} %broadcast_divide_fusion.w_ref), custom_call_target="tpu_custom_call" | custom-call | flops 1811939328 | bytes 3407872 | tf_op jit(solution)/shard_map/pallas_call | solution.py:202
  46.7 4.2 %all-to-all-start.2 = ((f32[8,72,512]{2,1,0:T(8,128)}), f32[8,72,512]{2,1,0:T(8,128)S(1)}, u32[]{:S(2)}, u32[]{:S(2)}) async-start(f32[8,72,512]{2,1,0:T(8,128)} %shard_map.46), calls=%async_computation.2 | async-start | bytes 2359296 | tf_op jit(solution)/shard_map/all_to_all | solution.py:233
  50.9 32.0 %all-to-all-done.2 = f32[8,72,512]{2,1,0:T(8,128)S(1)} async-done(((f32[8,72,512]{2,1,0:T(8,128)}), f32[8,72,512]{2,1,0:T(8,128)S(1)}, u32[]{:S(2)}, u32[]{:S(2)}) %all-to-all-start.2) | async-done | bytes 1179680 | tf_op jit(solution)/shard_map/all_to_all | solution.py:233
  82.9 0.1 reduce_sum.125
  83.0 0.1 multiply_bitcast_fusion
  83.1 0.8 fusion.15
  (10 shorter events, 0.1 us)
Async XLA Ops:
  0.0 22.7 %copy-start = (bf16[512,256]{1,0:T(8,128)(2,1)S(1)}, bf16[512,256]{1,0:T(8,128)(2,1)}, u32[]{:S(2)}) copy-start(bf16[512,256]{1,0:T(8,128)(2,1)} %param.4) | copy-start | bytes 786436
  0.0 23.5 %all-to-all-start = ((bf16[16,32,256]{2,1,0:T(8,128)(2,1)}), bf16[16,32,256]{2,1,0:T(8,128)(2,1)S(1)}, u32[]{:S(2)}, u32[]{:S(2)}) async-start(bf16[16,32,256]{2,1,0:T(8,128)(2,1)} %bitcast.7), calls=%async_computation | async-start | bytes 524288 | tf_op jit(solution)/shard_map/all_to_all | solution.py:96
  11.3 11.4 %collective-permute-start = (bf16[256,256]{1,0:T(8,128)(2,1)S(1)}, bf16[256,256]{1,0:T(8,128)(2,1)S(1)}, u32[]{:S(2)}, u32[]{:S(2)}) collective-permute-start(bf16[256,256]{1,0:T(8,128)(2,1)S(1)} %slice.12), channel_id=1, source_target_pairs={{120,0},{0,8},{8,16},{16,24},{24,32},{32,40},{40,48},{48,56},{56,6... | collective-permute-start | bytes 393224 | tf_op jit(solution)/shard_map/ppermute | solution.py:20
  22.7 16.8 %copy-start.1 = (bf16[768,256]{1,0:T(8,128)(2,1)}, bf16[768,256]{1,0:T(8,128)(2,1)S(1)}, u32[]{:S(2)}) copy-start(bf16[768,256]{1,0:T(8,128)(2,1)S(1)} %constant_dynamic-update-slice_fusion.q_ref) | copy-start | bytes 1179652
  24.6 14.9 %all-to-all-start.1 = ((bf16[16,2,32,256]{3,2,1,0:T(8,128)(2,1)}), bf16[16,2,32,256]{3,2,1,0:T(8,128)(2,1)S(1)}, u32[]{:S(2)}, u32[]{:S(2)}) async-start(bf16[16,2,32,256]{3,2,1,0:T(8,128)(2,1)} %broadcast_in_dim.89), calls=%async_computation.1 | async-start | bytes 1048576 | tf_op jit(solution)/shard_map/all_to_all | solution.py:102
  39.5 0.8 copy-start.2
  46.7 36.2 %all-to-all-start.2 = ((f32[8,72,512]{2,1,0:T(8,128)}), f32[8,72,512]{2,1,0:T(8,128)S(1)}, u32[]{:S(2)}, u32[]{:S(2)}) async-start(f32[8,72,512]{2,1,0:T(8,128)} %shard_map.46), calls=%async_computation.2 | async-start | bytes 2359296 | tf_op jit(solution)/shard_map/all_to_all | solution.py:233

commit v15 on v12

--- a/solution.py
+++ b/solution.py
@@ -212,8 +212,7 @@
 def shards(snapshots, offsets, window_len, cone_exp):
     block = snapshots.shape[0]
     lags = LAGS
-    tail = snapshots[block - lags :]
-    history = shifted(tail, "col", 1)
+    history = shifted(snapshots, "col", 1)[block - lags :]
     col_ext = jnp.concatenate([history, snapshots], axis=0)
     chosen = pick(offsets, lax.axis_index("row"))
     pieces = broadcast_block(snapshots, chosen)

time: 83.5 us -> 81.7 us (0.978)
  the two profiles are of different devices: /device:TPU:1 before, /device:TPU:129 now
where the time goes in v15:
time: 81.7 us; the launch traced here: 81.2 us
  waiting for transfers between devices  37.2 us (46%)
  starting transfers between devices  22.2 us (27%)
  other arithmetic  10.7 us (13%)
  Pallas kernels  6.43 us (8%)
  local copies, waits for them, and re-layouts  3.89 us (5%)
    all_to_all x1, waiting for transfers between devices, shards(): mine = jnp.sum(lax.all_to_all(payload, 'chan', 0, 0, tiled=False), axis=0)  32 us
    all_to_all x1, starting transfers between devices, shards(): mine = jnp.sum(lax.all_to_all(payload, 'chan', 0, 0, tiled=False), axis=0)  6.83 us
    pallas_call x1, Pallas kernels, lag_total(): pl.pallas_call(functools.partial(lag_kernel, lags), out_shape=jax.ShapeDt...  6.43 us
    all_to_all x1, starting transfers between devices, broadcast_block(): got = lax.all_to_all(parts, 'col', 0, 0, tiled=False)  5.95 us
    all_to_all x1, starting transfers between devices, broadcast_block(): return lax.all_to_all(spread_out, 'col', 0, 0, tiled=False)  5.72 us
    all_to_all x1, waiting for transfers between devices, broadcast_block(): return lax.all_to_all(spread_out, 'col', 0, 0, tiled=False)  5.16 us
    ppermute x1, starting transfers between devices, shifted(): return lax.ppermute(block, axis, route)  3.67 us
    div x1, other arithmetic, reversed_cone(): return cone / jnp.sum(cone, axis=1, keepdims=True)  2.09 us
  transfers between devices with their start and end apart: 4, of which 2 were waited for; matrix products, arithmetic and copies ran while one was open for 16% of the time, Pallas kernels for 0%

profile of v15, /device:TPU:129, one launch (start us, length us, event | category | flops | bytes accessed | tf_op | source)
XLA Modules:
  0.0 81.2 jit_solution(6971884615962781891)
XLA Ops:
  0.0 3.7 %collective-permute-start = (bf16[512,256]{1,0:T(8,128)(2,1)}, bf16[512,256]{1,0:T(8,128)(2,1)S(1)}, u32[]{:S(2)}, u32[]{:S(2)}) collective-permute-start(bf16[512,256]{1,0:T(8,128)(2,1)} %param.4), channel_id=1, source_target_pairs={{120,0},{0,8},{8,16},{16,24},{24,32},{32,40},{40,48},{48,56},{56,6... | collective-permute-start | bytes 786440 | tf_op jit(solution)/shard_map/ppermute | solution.py:20
  3.7 6.0 %all-to-all-start = ((bf16[16,32,256]{2,1,0:T(8,128)(2,1)}), bf16[16,32,256]{2,1,0:T(8,128)(2,1)S(1)}, u32[]{:S(2)}, u32[]{:S(2)}) async-start(bf16[16,32,256]{2,1,0:T(8,128)(2,1)} %bitcast.7), calls=%async_computation | async-start | bytes 524288 | tf_op jit(solution)/shard_map/all_to_all | solution.py:96
  9.7 1.3 %fusion.18 = s32[]{:T(128)} fusion(s32[4]{0:T(128)} %param.5, s32[]{:T(128)S(6)} %axis_index.33), kind=kLoop, calls=%fused_computation.43 | loop fusion | flops 11 | bytes 24 | tf_op jit(solution)/shard_map/reduce_sum | solution.py:89
  11.6 0.7 iota_compare_fusion.1
  12.3 0.8 reshape.85
  13.0 0.8 reshape.86
  13.8 0.1 select_reduce_fusion.2
  13.9 1.4 %fusion.12 = f32[512]{0:T(512)S(1)} fusion(pred[512]{0:T(512)(128)(4,1)S(1)} %get-tuple-element.16, f32[512]{0:T(512)S(1)} %convert_element_type.34, pred[512]{0:T(512)(128)(4,1)S(1)} %get-tuple-element.17, pred[512]{0:T(512)(128)(4,1)S(1)} %get-tuple-element.15, s32[512]{0:T(512)S(1)} %get-tuple-element.12), kind=kLoop, calls=%fused_computation.19 | loop fusion | flops 5897728 | bytes 7680 | tf_op jit(solution)/shard_map/reduce_sum | solution.py:134
  15.4 0.0 copy-start
  15.4 2.1 %broadcast_divide_fusion.w_ref = f32[512,768]{1,0:T(8,128)} fusion(f32[512]{0:T(512)S(1)} %fusion.12, pred[512]{0:T(512)(128)(4,1)S(1)} %get-tuple-element.16, f32[512]{0:T(512)S(1)} %convert_element_type.34, pred[512]{0:T(512)(128)(4,1)S(1)} %get-tuple-element.17, pred[512]{0:T(512)(128)(4,1)S(1)} %get-tuple-element.15, s32[512]{0:T(512)S(1)} %get-tuple-element.12), kind=kLoop, calls=%fused_computation.17 | loop fusion | flops 5898240 | bytes 1580544 | tf_op jit(solution)/shard_map/div | solution.py:134
  17.5 0.0 all-to-all-done
  17.5 0.1 select_reduce_fusion.1
  17.6 0.1 rev.3
  17.7 0.9 %broadcast_in_dim.88 = bf16[16,2,32,256]{3,2,1,0:T(8,128)(2,1)} broadcast(bf16[2,32,256]{2,1,0:T(8,128)(2,1)S(1)} %rev.3), dimensions={1,2,3} | broadcast | bytes 557056 | tf_op jit(solution)/shard_map/broadcast_in_dim | solution.py:100
  18.6 5.7 %all-to-all-start.1 = ((bf16[16,2,32,256]{3,2,1,0:T(8,128)(2,1)}), bf16[16,2,32,256]{3,2,1,0:T(8,128)(2,1)S(1)}, u32[]{:S(2)}, u32[]{:S(2)}) async-start(bf16[16,2,32,256]{3,2,1,0:T(8,128)(2,1)} %broadcast_in_dim.88), calls=%async_computation.1 | async-start | bytes 1048576 | tf_op jit(solution)/shard_map/all_to_all | solution.py:101
  24.3 1.2 %fusion.13 = f32[512]{0:T(512)S(1)} fusion(pred[512]{0:T(512)(128)(4,1)S(1)} %get-tuple-element.19, f32[512]{0:T(512)S(1)} %convert_element_type.32, pred[512]{0:T(512)(128)(4,1)S(1)} %get-tuple-element.20, pred[512]{0:T(512)(128)(4,1)S(1)} %get-tuple-element.18, s32[512]{0:T(512)S(1)} %get-tuple-element.11, s32[512]{0:T(512)S(1)} %iota_add_fusion), kind=kLoop, calls=%fused_computation.20 | loop fusion | flops 5504512 | bytes 9728 | tf_op jit(solution)/shard_map/reduce_sum | solution.py:122
  25.5 0.0 collective-permute-done
  25.6 0.0 copy-done
  25.6 0.2 multiply_reduce_fusion.1
  25.8 0.6 broadcast_in_dim.89.cp_ref
  26.4 0.8 pad_maximum_fusion.q_ref
  27.1 1.8 %multiply_reduce_fusion = f32[512]{0:T(512)} fusion(f32[768]{0:T(1024)S(1)} %multiply_reduce_fusion.1, f32[512]{0:T(512)S(1)} %fusion.13, pred[512]{0:T(512)(128)(4,1)S(1)} %get-tuple-element.19, f32[512]{0:T(512)S(1)} %convert_element_type.32, pred[512]{0:T(512)(128)(4,1)S(1)} %get-tuple-element.20, pred[512]{0:T(512)(128)(4,1)S(1)} %get-tuple-element.18, ...), kind=kLoop, calls=%fused_computation.11 | loop fusion | flops 6290944 | bytes 14848 | tf_op jit(solution)/shard_map/reduce_sum | solution.py:227
  29.0 5.2 %all-to-all-done.1.r_ref = bf16[16,2,32,256]{3,2,1,0:T(8,128)(2,1)S(1)} async-done(((bf16[16,2,32,256]{3,2,1,0:T(8,128)(2,1)}), bf16[16,2,32,256]{3,2,1,0:T(8,128)(2,1)S(1)}, u32[]{:S(2)}, u32[]{:S(2)}) %all-to-all-start.1) | async-done | bytes 524320 | tf_op jit(solution)/shard_map/all_to_all | solution.py:101
  34.1 0.0 copy-start.1
  34.1 0.8 copy-done.1
  34.9 6.4 %shard_map.46 = f32[8,72,512]{2,1,0:T(8,128)} custom-call(bf16[16,2,32,256]{3,2,1,0:T(8,128)(2,1)} %copy-done.1, bf16[768,256]{1,0:T(8,128)(2,1)} %pad_maximum_fusion.q_ref, f32[1,768]{1,0:T(1,128)} %broadcast_in_dim.89.cp_ref, f32[1,512]{1,0:T(1,128)} %bitcast.11, f32[512,768]{1,0:T(8,128)} %broadcast_divide_fusion.w_ref), custom_call_target="tpu_custom_call" | custom-call | flops 1811939328 | bytes 3407872 | tf_op jit(solution)/shard_map/pallas_call | solution.py:201
  41.4 6.8 %all-to-all-start.2 = ((f32[8,72,512]{2,1,0:T(8,128)}), f32[8,72,512]{2,1,0:T(8,128)S(1)}, u32[]{:S(2)}, u32[]{:S(2)}) async-start(f32[8,72,512]{2,1,0:T(8,128)} %shard_map.46), calls=%async_computation.2 | async-start | bytes 2359296 | tf_op jit(solution)/shard_map/all_to_all | solution.py:231
  48.2 32.0 %all-to-all-done.2 = f32[8,72,512]{2,1,0:T(8,128)S(1)} async-done(((f32[8,72,512]{2,1,0:T(8,128)}), f32[8,72,512]{2,1,0:T(8,128)S(1)}, u32[]{:S(2)}, u32[]{:S(2)}) %all-to-all-start.2) | async-done | bytes 1179680 | tf_op jit(solution)/shard_map/all_to_all | solution.py:231
  80.2 0.1 reduce_sum.125
  80.3 0.1 multiply_bitcast_fusion
  80.4 0.8 fusion.15
  (9 shorter events, 0.1 us)
Async XLA Ops:
  0.0 25.5 %collective-permute-start = (bf16[512,256]{1,0:T(8,128)(2,1)}, bf16[512,256]{1,0:T(8,128)(2,1)S(1)}, u32[]{:S(2)}, u32[]{:S(2)}) collective-permute-start(bf16[512,256]{1,0:T(8,128)(2,1)} %param.4), channel_id=1, source_target_pairs={{120,0},{0,8},{8,16},{16,24},{24,32},{32,40},{40,48},{48,56},{56,6... | collective-permute-start | bytes 786440 | tf_op jit(solution)/shard_map/ppermute | solution.py:20
  3.7 13.8 %all-to-all-start = ((bf16[16,32,256]{2,1,0:T(8,128)(2,1)}), bf16[16,32,256]{2,1,0:T(8,128)(2,1)S(1)}, u32[]{:S(2)}, u32[]{:S(2)}) async-start(bf16[16,32,256]{2,1,0:T(8,128)(2,1)} %bitcast.7), calls=%async_computation | async-start | bytes 524288 | tf_op jit(solution)/shard_map/all_to_all | solution.py:96
  15.4 10.2 %copy-start = (bf16[512,256]{1,0:T(8,128)(2,1)S(1)}, bf16[512,256]{1,0:T(8,128)(2,1)}, u32[]{:S(2)}) copy-start(bf16[512,256]{1,0:T(8,128)(2,1)} %param.4) | copy-start | bytes 786436
  18.6 15.5 %all-to-all-start.1 = ((bf16[16,2,32,256]{3,2,1,0:T(8,128)(2,1)}), bf16[16,2,32,256]{3,2,1,0:T(8,128)(2,1)S(1)}, u32[]{:S(2)}, u32[]{:S(2)}) async-start(bf16[16,2,32,256]{3,2,1,0:T(8,128)(2,1)} %broadcast_in_dim.88), calls=%async_computation.1 | async-start | bytes 1048576 | tf_op jit(solution)/shard_map/all_to_all | solution.py:101
  34.1 0.8 copy-start.1
  41.4 38.8 %all-to-all-start.2 = ((f32[8,72,512]{2,1,0:T(8,128)}), f32[8,72,512]{2,1,0:T(8,128)S(1)}, u32[]{:S(2)}, u32[]{:S(2)}) async-start(f32[8,72,512]{2,1,0:T(8,128)} %shard_map.46), calls=%async_computation.2 | async-start | bytes 2359296 | tf_op jit(solution)/shard_map/all_to_all | solution.py:231

commit v16 on v15

--- a/solution.py
+++ b/solution.py
@@ -157,14 +157,19 @@
     weights = w_ref[...]
     w_hi = weights.astype(jnp.bfloat16)
     w_lo = (weights - w_hi.astype(jnp.float32)).astype(jnp.bfloat16)
-    ones = jnp.ones((8, square.shape[1]), jnp.float32)
-    norm_rows = lax.dot_general(
-        ones, square, (((1,), (1,)), ((), ())), precision=lax.Precision.HIGHEST,
-        preferred_element_type=jnp.float32,
-    )
-    row_sum = lax.dot_general(
-        norm_rows, w_ref[...], (((1,), (1,)), ((), ())), precision=lax.Precision.HIGHEST,
-        preferred_element_type=jnp.float32,
+    ones = jnp.ones((8, square.shape[1]), jnp.bfloat16)
+    square_hi = square.astype(jnp.bfloat16)
+    square_lo = (square - square_hi.astype(jnp.float32)).astype(jnp.bfloat16)
+    contract = (((1,), (1,)), ((), ()))
+    norm_rows = lax.dot_general(ones, square_hi, contract, preferred_element_type=jnp.float32) + lax.dot_general(
+        ones, square_lo, contract, preferred_element_type=jnp.float32
+    )
+    norm_hi = norm_rows.astype(jnp.bfloat16)
+    norm_lo = (norm_rows - norm_hi.astype(jnp.float32)).astype(jnp.bfloat16)
+    row_sum = (
+        lax.dot_general(norm_hi, w_hi, contract, preferred_element_type=jnp.float32)
+        + lax.dot_general(norm_hi, w_lo, contract, preferred_element_type=jnp.float32)
+        + lax.dot_general(norm_lo, w_hi, contract, preferred_element_type=jnp.float32)
     )
     count, share, block = o_ref.shape[0], 64, o_ref.shape[2]
     share = block // count

time: 81.7 us -> 80.7 us (0.988)
  Pallas kernels: 6.43 us -> 5.36 us
    pallas_call x1, Pallas kernels: 6.43 us -> 5.36 us  [lag_total(): pl.pallas_call(functools.partial(lag_kernel, lags), out_shape=jax.ShapeDt...]
where the time goes in v16:
time: 80.7 us; the launch traced here: 80.1 us
  waiting for transfers between devices  37.2 us (46%)
  starting transfers between devices  22.2 us (28%)
  other arithmetic  10.7 us (13%)
  Pallas kernels  5.36 us (7%)
  local copies, waits for them, and re-layouts  3.89 us (5%)
    all_to_all x1, waiting for transfers between devices, shards(): mine = jnp.sum(lax.all_to_all(payload, 'chan', 0, 0, tiled=False), axis=0)  32 us
    all_to_all x1, starting transfers between devices, shards(): mine = jnp.sum(lax.all_to_all(payload, 'chan', 0, 0, tiled=False), axis=0)  6.82 us
    all_to_all x1, starting transfers between devices, broadcast_block(): got = lax.all_to_all(parts, 'col', 0, 0, tiled=False)  5.95 us
    all_to_all x1, starting transfers between devices, broadcast_block(): return lax.all_to_all(spread_out, 'col', 0, 0, tiled=False)  5.72 us
    pallas_call x1, Pallas kernels, lag_total(): pl.pallas_call(functools.partial(lag_kernel, lags), out_shape=jax.ShapeDt...  5.36 us
    all_to_all x1, waiting for transfers between devices, broadcast_block(): return lax.all_to_all(spread_out, 'col', 0, 0, tiled=False)  5.16 us
    ppermute x1, starting transfers between devices, shifted(): return lax.ppermute(block, axis, route)  3.67 us
    div x1, other arithmetic, reversed_cone(): return cone / jnp.sum(cone, axis=1, keepdims=True)  2.09 us
  transfers between devices with their start and end apart: 4, of which 2 were waited for; matrix products, arithmetic and copies ran while one was open for 16% of the time, Pallas kernels for 0%

profile of v16, /device:TPU:129, one launch (start us, length us, event | category | flops | bytes accessed | tf_op | source)
XLA Modules:
  0.0 80.1 jit_solution(2718976040359079622)
XLA Ops:
  0.0 3.7 %collective-permute-start = (bf16[512,256]{1,0:T(8,128)(2,1)}, bf16[512,256]{1,0:T(8,128)(2,1)S(1)}, u32[]{:S(2)}, u32[]{:S(2)}) collective-permute-start(bf16[512,256]{1,0:T(8,128)(2,1)} %param.4), channel_id=1, source_target_pairs={{120,0},{0,8},{8,16},{16,24},{24,32},{32,40},{40,48},{48,56},{56,6... | collective-permute-start | bytes 786440 | tf_op jit(solution)/shard_map/ppermute | solution.py:20
  3.7 6.0 %all-to-all-start = ((bf16[16,32,256]{2,1,0:T(8,128)(2,1)}), bf16[16,32,256]{2,1,0:T(8,128)(2,1)S(1)}, u32[]{:S(2)}, u32[]{:S(2)}) async-start(bf16[16,32,256]{2,1,0:T(8,128)(2,1)} %bitcast.7), calls=%async_computation | async-start | bytes 524288 | tf_op jit(solution)/shard_map/all_to_all | solution.py:96
  9.7 1.3 %fusion.18 = s32[]{:T(128)} fusion(s32[4]{0:T(128)} %param.5, s32[]{:T(128)S(6)} %axis_index.33), kind=kLoop, calls=%fused_computation.43 | loop fusion | flops 11 | bytes 24 | tf_op jit(solution)/shard_map/reduce_sum | solution.py:89
  11.6 0.7 iota_compare_fusion.1
  12.3 0.8 reshape.85
  13.0 0.8 reshape.86
  13.8 0.1 select_reduce_fusion.2
  13.9 1.4 %fusion.12 = f32[512]{0:T(512)S(1)} fusion(pred[512]{0:T(512)(128)(4,1)S(1)} %get-tuple-element.16, f32[512]{0:T(512)S(1)} %convert_element_type.34, pred[512]{0:T(512)(128)(4,1)S(1)} %get-tuple-element.17, pred[512]{0:T(512)(128)(4,1)S(1)} %get-tuple-element.15, s32[512]{0:T(512)S(1)} %get-tuple-element.12), kind=kLoop, calls=%fused_computation.19 | loop fusion | flops 5897728 | bytes 7680 | tf_op jit(solution)/shard_map/reduce_sum | solution.py:134
  15.4 0.0 copy-start
  15.4 2.1 %broadcast_divide_fusion.w_ref = f32[512,768]{1,0:T(8,128)} fusion(f32[512]{0:T(512)S(1)} %fusion.12, pred[512]{0:T(512)(128)(4,1)S(1)} %get-tuple-element.16, f32[512]{0:T(512)S(1)} %convert_element_type.34, pred[512]{0:T(512)(128)(4,1)S(1)} %get-tuple-element.17, pred[512]{0:T(512)(128)(4,1)S(1)} %get-tuple-element.15, s32[512]{0:T(512)S(1)} %get-tuple-element.12), kind=kLoop, calls=%fused_computation.17 | loop fusion | flops 5898240 | bytes 1580544 | tf_op jit(solution)/shard_map/div | solution.py:134
  17.5 0.0 all-to-all-done
  17.5 0.1 select_reduce_fusion.1
  17.6 0.1 rev.3
  17.7 0.9 %broadcast_in_dim.88 = bf16[16,2,32,256]{3,2,1,0:T(8,128)(2,1)} broadcast(bf16[2,32,256]{2,1,0:T(8,128)(2,1)S(1)} %rev.3), dimensions={1,2,3} | broadcast | bytes 557056 | tf_op jit(solution)/shard_map/broadcast_in_dim | solution.py:100
  18.6 5.7 %all-to-all-start.1 = ((bf16[16,2,32,256]{3,2,1,0:T(8,128)(2,1)}), bf16[16,2,32,256]{3,2,1,0:T(8,128)(2,1)S(1)}, u32[]{:S(2)}, u32[]{:S(2)}) async-start(bf16[16,2,32,256]{3,2,1,0:T(8,128)(2,1)} %broadcast_in_dim.88), calls=%async_computation.1 | async-start | bytes 1048576 | tf_op jit(solution)/shard_map/all_to_all | solution.py:101
  24.3 1.2 %fusion.13 = f32[512]{0:T(512)S(1)} fusion(pred[512]{0:T(512)(128)(4,1)S(1)} %get-tuple-element.19, f32[512]{0:T(512)S(1)} %convert_element_type.32, pred[512]{0:T(512)(128)(4,1)S(1)} %get-tuple-element.20, pred[512]{0:T(512)(128)(4,1)S(1)} %get-tuple-element.18, s32[512]{0:T(512)S(1)} %get-tuple-element.11, s32[512]{0:T(512)S(1)} %iota_add_fusion), kind=kLoop, calls=%fused_computation.20 | loop fusion | flops 5504512 | bytes 9728 | tf_op jit(solution)/shard_map/reduce_sum | solution.py:122
  25.5 0.0 collective-permute-done
  25.6 0.0 copy-done
  25.6 0.2 multiply_reduce_fusion.1
  25.8 0.6 broadcast_in_dim.89.cp_ref
  26.4 0.8 pad_maximum_fusion.q_ref
  27.1 1.8 %multiply_reduce_fusion = f32[512]{0:T(512)} fusion(f32[768]{0:T(1024)S(1)} %multiply_reduce_fusion.1, f32[512]{0:T(512)S(1)} %fusion.13, pred[512]{0:T(512)(128)(4,1)S(1)} %get-tuple-element.19, f32[512]{0:T(512)S(1)} %convert_element_type.32, pred[512]{0:T(512)(128)(4,1)S(1)} %get-tuple-element.20, pred[512]{0:T(512)(128)(4,1)S(1)} %get-tuple-element.18, ...), kind=kLoop, calls=%fused_computation.11 | loop fusion | flops 6290944 | bytes 14848 | tf_op jit(solution)/shard_map/reduce_sum | solution.py:232
  29.0 5.2 %all-to-all-done.1.r_ref = bf16[16,2,32,256]{3,2,1,0:T(8,128)(2,1)S(1)} async-done(((bf16[16,2,32,256]{3,2,1,0:T(8,128)(2,1)}), bf16[16,2,32,256]{3,2,1,0:T(8,128)(2,1)S(1)}, u32[]{:S(2)}, u32[]{:S(2)}) %all-to-all-start.1) | async-done | bytes 524320 | tf_op jit(solution)/shard_map/all_to_all | solution.py:101
  34.1 0.0 copy-start.1
  34.1 0.8 %copy-done.1 = bf16[16,2,32,256]{3,2,1,0:T(8,128)(2,1)} copy-done((bf16[16,2,32,256]{3,2,1,0:T(8,128)(2,1)}, bf16[16,2,32,256]{3,2,1,0:T(8,128)(2,1)S(1)}, u32[]{:S(2)}) %copy-start.1) | copy-done | bytes 524312
  34.9 5.4 %shard_map.46 = f32[8,72,512]{2,1,0:T(8,128)} custom-call(bf16[16,2,32,256]{3,2,1,0:T(8,128)(2,1)} %copy-done.1, bf16[768,256]{1,0:T(8,128)(2,1)} %pad_maximum_fusion.q_ref, f32[1,768]{1,0:T(1,128)} %broadcast_in_dim.89.cp_ref, f32[1,512]{1,0:T(1,128)} %bitcast.11, f32[512,768]{1,0:T(8,128)} %broadcast_divide_fusion.w_ref), custom_call_target="tpu_custom_call" | custom-call | flops 1811939328 | bytes 3407872 | tf_op jit(solution)/shard_map/pallas_call | solution.py:206
  40.3 6.8 %all-to-all-start.2 = ((f32[8,72,512]{2,1,0:T(8,128)}), f32[8,72,512]{2,1,0:T(8,128)S(1)}, u32[]{:S(2)}, u32[]{:S(2)}) async-start(f32[8,72,512]{2,1,0:T(8,128)} %shard_map.46), calls=%async_computation.2 | async-start | bytes 2359296 | tf_op jit(solution)/shard_map/all_to_all | solution.py:236
  47.1 32.0 %all-to-all-done.2 = f32[8,72,512]{2,1,0:T(8,128)S(1)} async-done(((f32[8,72,512]{2,1,0:T(8,128)}), f32[8,72,512]{2,1,0:T(8,128)S(1)}, u32[]{:S(2)}, u32[]{:S(2)}) %all-to-all-start.2) | async-done | bytes 1179680 | tf_op jit(solution)/shard_map/all_to_all | solution.py:236
  79.1 0.1 reduce_sum.125
  79.2 0.1 multiply_bitcast_fusion
  79.3 0.8 fusion.15
  (9 shorter events, 0.1 us)
Async XLA Ops:
  0.0 25.5 %collective-permute-start = (bf16[512,256]{1,0:T(8,128)(2,1)}, bf16[512,256]{1,0:T(8,128)(2,1)S(1)}, u32[]{:S(2)}, u32[]{:S(2)}) collective-permute-start(bf16[512,256]{1,0:T(8,128)(2,1)} %param.4), channel_id=1, source_target_pairs={{120,0},{0,8},{8,16},{16,24},{24,32},{32,40},{40,48},{48,56},{56,6... | collective-permute-start | bytes 786440 | tf_op jit(solution)/shard_map/ppermute | solution.py:20
  3.7 13.8 %all-to-all-start = ((bf16[16,32,256]{2,1,0:T(8,128)(2,1)}), bf16[16,32,256]{2,1,0:T(8,128)(2,1)S(1)}, u32[]{:S(2)}, u32[]{:S(2)}) async-start(bf16[16,32,256]{2,1,0:T(8,128)(2,1)} %bitcast.7), calls=%async_computation | async-start | bytes 524288 | tf_op jit(solution)/shard_map/all_to_all | solution.py:96
  15.4 10.2 %copy-start = (bf16[512,256]{1,0:T(8,128)(2,1)S(1)}, bf16[512,256]{1,0:T(8,128)(2,1)}, u32[]{:S(2)}) copy-start(bf16[512,256]{1,0:T(8,128)(2,1)} %param.4) | copy-start | bytes 786436
  18.6 15.5 %all-to-all-start.1 = ((bf16[16,2,32,256]{3,2,1,0:T(8,128)(2,1)}), bf16[16,2,32,256]{3,2,1,0:T(8,128)(2,1)S(1)}, u32[]{:S(2)}, u32[]{:S(2)}) async-start(bf16[16,2,32,256]{3,2,1,0:T(8,128)(2,1)} %broadcast_in_dim.88), calls=%async_computation.1 | async-start | bytes 1048576 | tf_op jit(solution)/shard_map/all_to_all | solution.py:101
  34.1 0.8 %copy-start.1 = (bf16[16,2,32,256]{3,2,1,0:T(8,128)(2,1)}, bf16[16,2,32,256]{3,2,1,0:T(8,128)(2,1)S(1)}, u32[]{:S(2)}) copy-start(bf16[16,2,32,256]{3,2,1,0:T(8,128)(2,1)S(1)} %all-to-all-done.1.r_ref) | copy-start | bytes 1572868
  40.3 38.8 %all-to-all-start.2 = ((f32[8,72,512]{2,1,0:T(8,128)}), f32[8,72,512]{2,1,0:T(8,128)S(1)}, u32[]{:S(2)}, u32[]{:S(2)}) async-start(f32[8,72,512]{2,1,0:T(8,128)} %shard_map.46), calls=%async_computation.2 | async-start | bytes 2359296 | tf_op jit(solution)/shard_map/all_to_all | solution.py:236

commit v17 on v16

--- a/solution.py
+++ b/solution.py
@@ -181,11 +181,9 @@
         rows_at = slice(chunk * m, chunk * (m + 1))
         cols_at = slice(low, low + band)
         out_at = slice(low, low + span)
-        part = (
-            jnp.dot(w_hi[rows_at, cols_at], skew_hi[cols_at, out_at], preferred_element_type=jnp.float32)
-            + jnp.dot(w_hi[rows_at, cols_at], skew_lo[cols_at, out_at], preferred_element_type=jnp.float32)
-            + jnp.dot(w_lo[rows_at, cols_at], skew_hi[cols_at, out_at], preferred_element_type=jnp.float32)
-        )
+        left = jnp.concatenate([w_hi[rows_at, cols_at], w_hi[rows_at, cols_at], w_lo[rows_at, cols_at]], axis=1)
+        right = jnp.concatenate([skew_hi[cols_at, out_at], skew_lo[cols_at, out_at], skew_hi[cols_at, out_at]], axis=0)
+        part = jnp.dot(left, right, preferred_element_type=jnp.float32)
         lined = pltpu.roll(part, span - (chunk - 1), 1, stride=1, stride_axis=0)
         for h in range(chunk // share):
             o_ref[(chunk * m) // share + h, 0:share, :] = lined[share * h : share * (h + 1), :block]

time: 80.7 us -> 80.6 us (level)
  no operation moved by 1% of the time
where the time goes in v17:
time: 80.6 us; the launch traced here: 80 us
  waiting for transfers between devices  37.2 us (46%)
  starting transfers between devices  22.2 us (28%)
  other arithmetic  10.7 us (13%)
  Pallas kernels  5.3 us (7%)
  local copies, waits for them, and re-layouts  3.89 us (5%)
    all_to_all x1, waiting for transfers between devices, shards(): mine = jnp.sum(lax.all_to_all(payload, 'chan', 0, 0, tiled=False), axis=0)  32 us
    all_to_all x1, starting transfers between devices, shards(): mine = jnp.sum(lax.all_to_all(payload, 'chan', 0, 0, tiled=False), axis=0)  6.81 us
    all_to_all x1, starting transfers between devices, broadcast_block(): got = lax.all_to_all(parts, 'col', 0, 0, tiled=False)  5.95 us
    all_to_all x1, starting transfers between devices, broadcast_block(): return lax.all_to_all(spread_out, 'col', 0, 0, tiled=False)  5.72 us
    pallas_call x1, Pallas kernels, lag_total(): pl.pallas_call(functools.partial(lag_kernel, lags), out_shape=jax.ShapeDt...  5.3 us
    all_to_all x1, waiting for transfers between devices, broadcast_block(): return lax.all_to_all(spread_out, 'col', 0, 0, tiled=False)  5.16 us
    ppermute x1, starting transfers between devices, shifted(): return lax.ppermute(block, axis, route)  3.67 us
    div x1, other arithmetic, reversed_cone(): return cone / jnp.sum(cone, axis=1, keepdims=True)  2.09 us
  transfers between devices with their start and end apart: 4, of which 2 were waited for; matrix products, arithmetic and copies ran while one was open for 16% of the time, Pallas kernels for 0%

profile of v17, /device:TPU:129, one launch (start us, length us, event | category | flops | bytes accessed | tf_op | source)
XLA Modules:
  0.0 80.0 jit_solution(11151033573627376336)
XLA Ops:
  0.0 3.7 %collective-permute-start = (bf16[512,256]{1,0:T(8,128)(2,1)}, bf16[512,256]{1,0:T(8,128)(2,1)S(1)}, u32[]{:S(2)}, u32[]{:S(2)}) collective-permute-start(bf16[512,256]{1,0:T(8,128)(2,1)} %param.4), channel_id=1, source_target_pairs={{120,0},{0,8},{8,16},{16,24},{24,32},{32,40},{40,48},{48,56},{56,6... | collective-permute-start | bytes 786440 | tf_op jit(solution)/shard_map/ppermute | solution.py:20
  3.7 6.0 %all-to-all-start = ((bf16[16,32,256]{2,1,0:T(8,128)(2,1)}), bf16[16,32,256]{2,1,0:T(8,128)(2,1)S(1)}, u32[]{:S(2)}, u32[]{:S(2)}) async-start(bf16[16,32,256]{2,1,0:T(8,128)(2,1)} %bitcast.7), calls=%async_computation | async-start | bytes 524288 | tf_op jit(solution)/shard_map/all_to_all | solution.py:96
  9.7 1.3 %fusion.18 = s32[]{:T(128)} fusion(s32[4]{0:T(128)} %param.5, s32[]{:T(128)S(6)} %axis_index.33), kind=kLoop, calls=%fused_computation.43 | loop fusion | flops 11 | bytes 24 | tf_op jit(solution)/shard_map/reduce_sum | solution.py:89
  11.6 0.7 iota_compare_fusion.1
  12.3 0.8 reshape.85
  13.0 0.8 reshape.86
  13.8 0.1 select_reduce_fusion.2
  13.9 1.4 %fusion.12 = f32[512]{0:T(512)S(1)} fusion(pred[512]{0:T(512)(128)(4,1)S(1)} %get-tuple-element.16, f32[512]{0:T(512)S(1)} %convert_element_type.34, pred[512]{0:T(512)(128)(4,1)S(1)} %get-tuple-element.17, pred[512]{0:T(512)(128)(4,1)S(1)} %get-tuple-element.15, s32[512]{0:T(512)S(1)} %get-tuple-element.12), kind=kLoop, calls=%fused_computation.19 | loop fusion | flops 5897728 | bytes 7680 | tf_op jit(solution)/shard_map/reduce_sum | solution.py:134
  15.4 0.0 copy-start
  15.4 2.1 %broadcast_divide_fusion.w_ref = f32[512,768]{1,0:T(8,128)} fusion(f32[512]{0:T(512)S(1)} %fusion.12, pred[512]{0:T(512)(128)(4,1)S(1)} %get-tuple-element.16, f32[512]{0:T(512)S(1)} %convert_element_type.34, pred[512]{0:T(512)(128)(4,1)S(1)} %get-tuple-element.17, pred[512]{0:T(512)(128)(4,1)S(1)} %get-tuple-element.15, s32[512]{0:T(512)S(1)} %get-tuple-element.12), kind=kLoop, calls=%fused_computation.17 | loop fusion | flops 5898240 | bytes 1580544 | tf_op jit(solution)/shard_map/div | solution.py:134
  17.5 0.0 all-to-all-done
  17.5 0.1 select_reduce_fusion.1
  17.6 0.1 rev.3
  17.7 0.9 %broadcast_in_dim.88 = bf16[16,2,32,256]{3,2,1,0:T(8,128)(2,1)} broadcast(bf16[2,32,256]{2,1,0:T(8,128)(2,1)S(1)} %rev.3), dimensions={1,2,3} | broadcast | bytes 557056 | tf_op jit(solution)/shard_map/broadcast_in_dim | solution.py:100
  18.6 5.7 %all-to-all-start.1 = ((bf16[16,2,32,256]{3,2,1,0:T(8,128)(2,1)}), bf16[16,2,32,256]{3,2,1,0:T(8,128)(2,1)S(1)}, u32[]{:S(2)}, u32[]{:S(2)}) async-start(bf16[16,2,32,256]{3,2,1,0:T(8,128)(2,1)} %broadcast_in_dim.88), calls=%async_computation.1 | async-start | bytes 1048576 | tf_op jit(solution)/shard_map/all_to_all | solution.py:101
  24.3 1.2 %fusion.13 = f32[512]{0:T(512)S(1)} fusion(pred[512]{0:T(512)(128)(4,1)S(1)} %get-tuple-element.19, f32[512]{0:T(512)S(1)} %convert_element_type.32, pred[512]{0:T(512)(128)(4,1)S(1)} %get-tuple-element.20, pred[512]{0:T(512)(128)(4,1)S(1)} %get-tuple-element.18, s32[512]{0:T(512)S(1)} %get-tuple-element.11, s32[512]{0:T(512)S(1)} %iota_add_fusion), kind=kLoop, calls=%fused_computation.20 | loop fusion | flops 5504512 | bytes 9728 | tf_op jit(solution)/shard_map/reduce_sum | solution.py:122
  25.5 0.0 collective-permute-done
  25.6 0.0 copy-done
  25.6 0.2 multiply_reduce_fusion.1
  25.8 0.6 broadcast_in_dim.89.cp_ref
  26.4 0.8 pad_maximum_fusion.q_ref
  27.1 1.8 %multiply_reduce_fusion = f32[512]{0:T(512)} fusion(f32[768]{0:T(1024)S(1)} %multiply_reduce_fusion.1, f32[512]{0:T(512)S(1)} %fusion.13, pred[512]{0:T(512)(128)(4,1)S(1)} %get-tuple-element.19, f32[512]{0:T(512)S(1)} %convert_element_type.32, pred[512]{0:T(512)(128)(4,1)S(1)} %get-tuple-element.20, pred[512]{0:T(512)(128)(4,1)S(1)} %get-tuple-element.18, ...), kind=kLoop, calls=%fused_computation.11 | loop fusion | flops 6290944 | bytes 14848 | tf_op jit(solution)/shard_map/reduce_sum | solution.py:230
  29.0 5.2 %all-to-all-done.1.r_ref = bf16[16,2,32,256]{3,2,1,0:T(8,128)(2,1)S(1)} async-done(((bf16[16,2,32,256]{3,2,1,0:T(8,128)(2,1)}), bf16[16,2,32,256]{3,2,1,0:T(8,128)(2,1)S(1)}, u32[]{:S(2)}, u32[]{:S(2)}) %all-to-all-start.1) | async-done | bytes 524320 | tf_op jit(solution)/shard_map/all_to_all | solution.py:101
  34.1 0.0 copy-start.1
  34.1 0.8 %copy-done.1 = bf16[16,2,32,256]{3,2,1,0:T(8,128)(2,1)} copy-done((bf16[16,2,32,256]{3,2,1,0:T(8,128)(2,1)}, bf16[16,2,32,256]{3,2,1,0:T(8,128)(2,1)S(1)}, u32[]{:S(2)}) %copy-start.1) | copy-done | bytes 524312
  34.9 5.3 %shard_map.46 = f32[8,72,512]{2,1,0:T(8,128)} custom-call(bf16[16,2,32,256]{3,2,1,0:T(8,128)(2,1)} %copy-done.1, bf16[768,256]{1,0:T(8,128)(2,1)} %pad_maximum_fusion.q_ref, f32[1,768]{1,0:T(1,128)} %broadcast_in_dim.89.cp_ref, f32[1,512]{1,0:T(1,128)} %bitcast.11, f32[512,768]{1,0:T(8,128)} %broadcast_divide_fusion.w_ref), custom_call_target="tpu_custom_call" | custom-call | flops 1811939328 | bytes 3407872 | tf_op jit(solution)/shard_map/pallas_call | solution.py:204
  40.2 6.8 %all-to-all-start.2 = ((f32[8,72,512]{2,1,0:T(8,128)}), f32[8,72,512]{2,1,0:T(8,128)S(1)}, u32[]{:S(2)}, u32[]{:S(2)}) async-start(f32[8,72,512]{2,1,0:T(8,128)} %shard_map.46), calls=%async_computation.2 | async-start | bytes 2359296 | tf_op jit(solution)/shard_map/all_to_all | solution.py:234
  47.0 32.0 %all-to-all-done.2 = f32[8,72,512]{2,1,0:T(8,128)S(1)} async-done(((f32[8,72,512]{2,1,0:T(8,128)}), f32[8,72,512]{2,1,0:T(8,128)S(1)}, u32[]{:S(2)}, u32[]{:S(2)}) %all-to-all-start.2) | async-done | bytes 1179680 | tf_op jit(solution)/shard_map/all_to_all | solution.py:234
  79.0 0.1 reduce_sum.125
  79.2 0.1 multiply_bitcast_fusion
  79.2 0.8 fusion.15
  (9 shorter events, 0.1 us)
Async XLA Ops:
  0.0 25.5 %collective-permute-start = (bf16[512,256]{1,0:T(8,128)(2,1)}, bf16[512,256]{1,0:T(8,128)(2,1)S(1)}, u32[]{:S(2)}, u32[]{:S(2)}) collective-permute-start(bf16[512,256]{1,0:T(8,128)(2,1)} %param.4), channel_id=1, source_target_pairs={{120,0},{0,8},{8,16},{16,24},{24,32},{32,40},{40,48},{48,56},{56,6... | collective-permute-start | bytes 786440 | tf_op jit(solution)/shard_map/ppermute | solution.py:20
  3.7 13.8 %all-to-all-start = ((bf16[16,32,256]{2,1,0:T(8,128)(2,1)}), bf16[16,32,256]{2,1,0:T(8,128)(2,1)S(1)}, u32[]{:S(2)}, u32[]{:S(2)}) async-start(bf16[16,32,256]{2,1,0:T(8,128)(2,1)} %bitcast.7), calls=%async_computation | async-start | bytes 524288 | tf_op jit(solution)/shard_map/all_to_all | solution.py:96
  15.4 10.2 %copy-start = (bf16[512,256]{1,0:T(8,128)(2,1)S(1)}, bf16[512,256]{1,0:T(8,128)(2,1)}, u32[]{:S(2)}) copy-start(bf16[512,256]{1,0:T(8,128)(2,1)} %param.4) | copy-start | bytes 786436
  18.6 15.5 %all-to-all-start.1 = ((bf16[16,2,32,256]{3,2,1,0:T(8,128)(2,1)}), bf16[16,2,32,256]{3,2,1,0:T(8,128)(2,1)S(1)}, u32[]{:S(2)}, u32[]{:S(2)}) async-start(bf16[16,2,32,256]{3,2,1,0:T(8,128)(2,1)} %broadcast_in_dim.88), calls=%async_computation.1 | async-start | bytes 1048576 | tf_op jit(solution)/shard_map/all_to_all | solution.py:101
  34.1 0.8 %copy-start.1 = (bf16[16,2,32,256]{3,2,1,0:T(8,128)(2,1)}, bf16[16,2,32,256]{3,2,1,0:T(8,128)(2,1)S(1)}, u32[]{:S(2)}) copy-start(bf16[16,2,32,256]{3,2,1,0:T(8,128)(2,1)S(1)} %all-to-all-done.1.r_ref) | copy-start | bytes 1572868
  40.2 38.8 %all-to-all-start.2 = ((f32[8,72,512]{2,1,0:T(8,128)}), f32[8,72,512]{2,1,0:T(8,128)S(1)}, u32[]{:S(2)}, u32[]{:S(2)}) async-start(f32[8,72,512]{2,1,0:T(8,128)} %shard_map.46), calls=%async_computation.2 | async-start | bytes 2359296 | tf_op jit(solution)/shard_map/all_to_all | solution.py:234
